TPU v7x, 32 devices: a whole 2x2x4 slice. The times are simulated.
32 devices in a mesh: member: 1, lat: 32 (over z, y, x, core).
Axes of the slice: x: 2, y: 2, z: 4, core: 2. Of those that a mesh axis runs over, the one named last changes fastest.
Arguments:
- spectral: bfloat16 [512, 512, 256], P(('member', 'lat')), may hold values from -6 to 6
- lat_basis: bfloat16 [512, 512, 192], P('lat'), may hold values from -0.0078125 to 0.0078125
- block_order: int32 [128], replicated, may hold values from 0 to 127, each once
- in_weight: bfloat16 [128, 1024], replicated, may hold values from -0.5 to 0.5
- in_bias: float32 [1024], replicated, may hold values from -3 to 3
- out_weight: bfloat16 [1024, 128], replicated, may hold values from -0.1875 to 0.1875
- col_gain: float32 [128], replicated, may hold values from 0.5 to 2
- damping: float32 [128], replicated, may hold values from 0.2 to 2
Outputs:
- tendency: float32 [512, 512, 256], P(('member', 'lat'))
Inputs may be any that keep to these rules, and one draw needn't show every extreme that they name: `block_order`: each wavenumber block appears exactly once.
All inputs are finite; a program needn't handle non-finite values.
Results may differ from a plain program's by a relative error of at most 0.004.
The roundings to bfloat16 on the way count: a program that leaves them out, or rounds other values in their place, can miss the bound.
Values may be sent and summed in bfloat16 or wider, within the bound.
No kernel may reach another device: no remote copies, remote signals or barrier semaphores. Data moves between devices by JAX's collectives and lax.ppermute only.
A program may use at most 128 MiB of HBM per device.

v0:
```python
import math

import jax
import jax.numpy as jnp
from jax import lax
from jax.sharding import PartitionSpec as P

NN = 512
NLON = 1536
MB = 4


def wavenumbers(block_order, slot_count):
    slot_ids = jnp.arange(slot_count, dtype=jnp.int32)
    blocks = block_order.shape[0]
    matches = (slot_ids // MB)[:, None] == jnp.arange(blocks, dtype=jnp.int32)[None, :]
    chosen = jnp.sum(jnp.where(matches, block_order[None, :], 0), axis=1)
    return chosen * MB + slot_ids % MB


def lon_table(wave_all):
    longitude = jnp.arange(NLON, dtype=jnp.int32)
    phase_index = wave_all[:, None] * longitude[None, :] % NLON
    angles = phase_index.astype(jnp.float32) * (2.0 * math.pi / NLON)
    return jnp.concatenate([jnp.cos(angles), jnp.sin(angles)], axis=0).astype(jnp.bfloat16)


def lat_weights(first_lat, lat_count, lat_total):
    latitude = (first_lat + jnp.arange(lat_count, dtype=jnp.int32)).astype(jnp.float32)
    return jnp.cos(math.pi * ((latitude + 0.5) / lat_total - 0.5))


def on_device(spectral, lat_basis, block_order, in_weight, in_bias, out_weight, col_gain, damping):
    devices = lax.axis_size("lat")
    my_index = lax.axis_index("lat")
    row_count = spectral.shape[0]
    degrees = spectral.shape[1]
    chan_width = spectral.shape[2]
    chan_count = chan_width // 2
    half_lat = lat_basis.shape[2]
    lat_total = 2 * half_lat
    lat_local = lat_total // devices
    wave_total = row_count * devices
    wave_all = wavenumbers(block_order, wave_total)
    wave_own = lax.dynamic_slice_in_dim(wave_all, my_index * row_count, row_count)
    degree = jnp.arange(degrees, dtype=jnp.int32)
    inside = degree[None, :] >= wave_own[:, None]
    parity = jnp.where((degree[None, :] + wave_own[:, None]) % 2 == 0, 1.0, -1.0).astype(
        jnp.float32
    )
    masked = jnp.where(inside[:, :, None], spectral, jnp.zeros_like(spectral))
    flipped = jnp.where(parity[:, :, None] > 0, masked, -masked)
    north_half = jnp.einsum("rnj,rnc->jrc", lat_basis, masked, preferred_element_type=jnp.float32)
    south_half = jnp.einsum("rnj,rnc->jrc", lat_basis, flipped, preferred_element_type=jnp.float32)
    fourier = jnp.concatenate([north_half, south_half[::-1]], axis=0).astype(jnp.bfloat16)
    outbound = fourier.reshape(devices, lat_local, row_count, chan_width)
    wave_table = lon_table(wave_all)
    rows_in = lax.all_to_all(outbound, "lat", split_axis=0, concat_axis=2, tiled=True)[0]
    signed = jnp.concatenate([rows_in[:, :, :chan_count], -rows_in[:, :, chan_count:]], axis=1)
    grid_field = jnp.einsum(
        "jrk,rl->jkl", signed, wave_table, preferred_element_type=jnp.float32
    ).astype(jnp.bfloat16)
    weight_own = lat_weights(my_index * lat_local, lat_local, lat_total)
    grid_wide = grid_field.astype(jnp.float32)
    partial_value = jnp.sum(weight_own[:, None, None] * grid_wide * grid_wide, axis=(0, 2))
    global_sum = lax.psum(partial_value, "lat")
    weight_all = lat_weights(0, lat_total, lat_total)
    variance = global_sum / (NLON * jnp.sum(weight_all))
    col_scale = col_gain * lax.rsqrt(variance + 1e-05)
    inv_root = 1.0 / math.sqrt(NLON)
    contract_first = (((0,), (0,)), ((), ()))

    def column(row_grid):
        normed = (row_grid.astype(jnp.float32) * col_scale[:, None]).astype(jnp.bfloat16)
        hidden = jax.nn.gelu(
            lax.dot_general(in_weight, normed, contract_first, preferred_element_type=jnp.float32)
            + in_bias[:, None]
        ).astype(jnp.bfloat16)
        column_out = lax.dot_general(
            out_weight, hidden, contract_first, preferred_element_type=jnp.float32
        ).astype(jnp.bfloat16)
        back_proj = lax.dot_general(
            wave_table, column_out, (((1,), (1,)), ((), ())), preferred_element_type=jnp.float32
        )
        return (
            jnp.concatenate([back_proj[:wave_total], -back_proj[wave_total:]], axis=1) * inv_root
        ).astype(jnp.bfloat16)

    coeffs = lax.map(column, grid_field)
    returning = coeffs.reshape(lat_local, devices, row_count, chan_width)
    factor = 2.0 * math.sqrt(degrees * wave_total / lat_total)
    weighted = (
        weight_all[:, None, None]
        * lax.all_to_all(returning, "lat", split_axis=1, concat_axis=0, tiled=True)[:, 0].astype(
            jnp.float32
        )
    ).astype(jnp.bfloat16)
    north_part = weighted[:half_lat]
    south_part = weighted[half_lat:][::-1]
    east_sum = jnp.einsum("rnj,jrc->rnc", lat_basis, north_part, preferred_element_type=jnp.float32)
    west_sum = jnp.einsum("rnj,jrc->rnc", lat_basis, south_part, preferred_element_type=jnp.float32)
    legendre = factor * (east_sum + parity[:, :, None] * west_sum)
    damp_all = jnp.concatenate([damping, damping])
    wave_factor = (degree * (degree + 1)).astype(jnp.float32) / (NN * NN)
    damped = legendre - damp_all[None, None, :] * wave_factor[None, :, None] * spectral.astype(
        jnp.float32
    )
    return jnp.where(inside[:, :, None], damped, jnp.zeros_like(damped))


def solution(mesh):
    in_specs = (
        P(("member", "lat"), None, None),
        P("lat", None, None),
        P(),
        P(),
        P(),
        P(),
        P(),
        P(),
    )
    out_specs = P(("member", "lat"), None, None)
    return jax.shard_map(
        on_device, mesh=mesh, in_specs=in_specs, out_specs=out_specs, check_vma=False
    )
```

profile of v0, /device:TPU:0, one launch (start us, length us, event | category | flops | bytes accessed | tf_op | source)
XLA Modules:
  0.0 446.9 jit_solution(13777267566337233392)
XLA Ops:
  1.2 6.4 %copy.40 = bf16[16,512,256]{1,2,0:T(8,128)(2,1)} copy(bf16[16,512,256]{2,1,0:T(8,128)(2,1)} %param.10) | data formatting | bytes 8388608 | tf_op args[0]
  7.7 5.0 %fusion.46 = bf16[192,16,256]{2,0,1:T(8,128)(2,1)} fusion(bf16[16,512,192]{1,2,0:T(8,128)(2,1)S(1)} %copy-done, bf16[16,512,256]{1,2,0:T(8,128)(2,1)} %copy.40, pred[16,512]{1,0:T(8,128)(4,1)S(1)} %get-tuple-element.70), kind=kOutput, calls=%fused_computation.61 | convolution fusion | flops 808189952 | bytes 8921088 | tf_op jit(solution)/shard_map/rnj,rnc->jrc/dot_general | solution.py:53
  15.4 29.9 %rev.6 = bf16[192,16,256]{2,0,1:T(8,128)(2,1)} reverse(bf16[192,16,256]{2,0,1:T(8,128)(2,1)} %fusion.42), dimensions={0} | reverse | bytes 3145728 | tf_op jit(solution)/shard_map/rev | solution.py:55
  50.9 7.6 %all-to-all-start = ((bf16[32,12,16,256]{3,2,1,0:T(8,128)(2,1)}), bf16[32,12,16,256]{3,2,1,0:T(8,128)(2,1)}, u32[]{:S(2)}, u32[]{:S(2)}) async-start(bf16[32,12,16,256]{3,2,1,0:T(8,128)(2,1)} %bitcast.68), calls=%async_computation | async-start | bytes 6291456 | tf_op jit(solution)/shard_map/all_to_all | solution.py:58
  59.9 13.5 %cosine_convert_fusion = (bf16[512,1536]{1,0:T(8,128)(2,1)S(1)}, bf16[512,1536]{1,0:T(8,128)(2,1)S(1)}) fusion(s32[512]{0:T(512)S(1)} %fusion.59), kind=kLoop, calls=%fused_computation.50 | loop fusion | flops 8650752 | bytes 3147776 | tf_op jit(solution)/shard_map/convert.4
  77.0 52.9 %all-to-all-done = bf16[32,12,16,256]{3,2,1,0:T(8,128)(2,1)} async-done(((bf16[32,12,16,256]{3,2,1,0:T(8,128)(2,1)}), bf16[32,12,16,256]{3,2,1,0:T(8,128)(2,1)}, u32[]{:S(2)}, u32[]{:S(2)}) %all-to-all-start) | async-done | bytes 3145760 | tf_op jit(solution)/shard_map/all_to_all | solution.py:58
  142.7 10.3 %fusion.25 = (f32[128]{0:T(128)S(1)}, bf16[12,128,1536]{2,1,0:T(8,128)(2,1)}) fusion(f32[12]{0:T(128)S(1)} %multiply_cosine_fusion.1, bf16[512,1536]{1,0:T(8,128)(2,1)} %copy-done.3, bf16[512,1536]{1,0:T(8,128)(2,1)} %copy-done.2, bf16[12,512,128]{1,2,0:T(8,128)(2,1)} %neg.10, bf16[12,512,128]{1,2,0:T(8,128)(2,1)} %copy.56), kind=kOutput, calls=%fused_computation.28 | convolution fusion | flops 4856217600 | bytes 11010608 | tf_op jit(solution)/shard_map/jrk,rl->jkl/dot_general | solution.py:60
  153.0 38.1 %psum.7 = f32[128]{0:T(128)S(1)} all-reduce(f32[128]{0:T(128)S(1)} %get-tuple-element.72), channel_id=1, replica_groups=mesh['member'=1,'lat'=32] {'lat'}, use_global_device_ids=true, to_apply=%region_2.3 | all-reduce | flops 128 | bytes 1024 | tf_op jit(solution)/shard_map/psum | solution.py:66
  191.1 114.6 %while.10 = (s32[]{:T(128)}, bf16[12,512,256]{2,1,0:T(8,128)(2,1)}, bf16[12,128,1536]{2,1,0:T(8,128)(2,1)}, f32[128]{0:T(128)S(1)}, bf16[128,1024]{1,0:T(8,128)(...) while((s32[]{:T(128)}, bf16[12,512,256]{2,1,0:T(8,128)(2,1)}, ...), condition=%wide.region_5.6_spmd, body=%wide.region_4.5_spmd.sunk | while | flops 1224933376 | bytes 8263261 | solution.py:89
  191.1 3.9 convolution_convert_fusion.3
  200.7 3.9 convolution_convert_fusion.3
  210.2 3.9 convolution_convert_fusion.3
  219.8 3.9 convolution_convert_fusion.3
  267.5 3.9 convolution_convert_fusion.3
  277.1 3.9 convolution_convert_fusion.3
  296.2 3.9 convolution_convert_fusion.3
  305.8 4.0 copy.48
  309.7 5.1 %all-to-all-start.1 = ((bf16[12,32,16,256]{3,2,0,1:T(8,128)(2,1)}), bf16[12,32,16,256]{3,2,0,1:T(8,128)(2,1)}, u32[]{:S(2)}, u32[]{:S(2)}) async-start(bf16[12,32,16,256]{3,2,0,1:T(8,128)(2,1)} %copy.48), calls=%async_computation.1 | async-start | bytes 6291456 | tf_op jit(solution)/shard_map/all_to_all | solution.py:94
  316.0 70.4 %all-to-all-done.1 = bf16[12,32,16,256]{3,2,0,1:T(8,128)(2,1)} async-done(((bf16[12,32,16,256]{3,2,0,1:T(8,128)(2,1)}), bf16[12,32,16,256]{3,2,0,1:T(8,128)(2,1)}, u32[]{:S(2)}, u32[]{:S(2)}) %all-to-all-start.1) | async-done | bytes 3145760 | tf_op jit(solution)/shard_map/all_to_all | solution.py:94
  389.1 4.0 fusion.27
  393.0 4.8 %fusion.44 = f32[16,256,512]{2,1,0:T(8,128)} fusion(bf16[16,512,192]{1,2,0:T(8,128)(2,1)S(1)} %copy-done, bf16[384,16,256]{2,0,1:T(8,128)(2,1)S(1)} %fusion.27), kind=kOutput, calls=%fused_computation.59 | convolution fusion | flops 805306368 | bytes 13107200 | tf_op jit(solution)/shard_map/rnj,jrc->rnc/dot_general | solution.py:100
  399.1 29.9 %rev.7 = bf16[192,16,256]{2,0,1:T(8,128)(2,1)} reverse(bf16[192,16,256]{2,0,1:T(8,128)(2,1)} %slice.27), dimensions={0} | reverse | bytes 3145728 | tf_op jit(solution)/shard_map/rev | solution.py:99
  429.0 8.7 %fusion.26 = f32[16,512,256]{1,2,0:T(8,128)} fusion(bf16[16,512,256]{1,2,0:T(8,128)(2,1)} %copy.40, f32[16,256,512]{2,1,0:T(8,128)} %fusion.44, f32[512,256]{0,1:T(8,128)} %broadcast_multiply_fusion, f32[16,512]{1,0:T(8,128)S(1)} %fusion.51, pred[16,512]{1,0:T(8,128)(4,1)S(1)} %get-tuple-element.70, bf16[192,16,256]{2,0,1:T(8,128)(2,1)} %rev.7, ...), kind=kOutput, calls=%fused_computation.30 | convolution fusion | flops 819986432 | bytes 26255360 | tf_op jit(solution)/shard_map/rnj,jrc->rnc/dot_general | solution.py:101
  437.7 9.2 %copy.51 = f32[16,512,256]{2,1,0:T(8,128)} copy(f32[16,512,256]{1,2,0:T(8,128)} %fusion.26) | data formatting | bytes 16777216 | tf_op jit(solution)/shard_map/jit(_where)/select_n | solution.py:108
  (102 shorter events, 118.8 us)
Async XLA Ops:
  0.0 7.7 %copy-start = (bf16[16,512,192]{1,2,0:T(8,128)(2,1)S(1)}, bf16[16,512,192]{1,2,0:T(8,128)(2,1)}, u32[]{:S(2)}) copy-start(bf16[16,512,192]{1,2,0:T(8,128)(2,1)} %param.11) | copy-start | bytes 9437188
  7.7 5.0 %copy-start.1 = (bf16[16,512,256]{1,2,0:T(8,128)(2,1)S(1)}, bf16[16,512,256]{1,2,0:T(8,128)(2,1)}, u32[]{:S(2)}) copy-start(bf16[16,512,256]{1,2,0:T(8,128)(2,1)} %copy.40) | copy-start | bytes 12582916
  50.9 78.9 %all-to-all-start = ((bf16[32,12,16,256]{3,2,1,0:T(8,128)(2,1)}), bf16[32,12,16,256]{3,2,1,0:T(8,128)(2,1)}, u32[]{:S(2)}, u32[]{:S(2)}) async-start(bf16[32,12,16,256]{3,2,1,0:T(8,128)(2,1)} %bitcast.68), calls=%async_computation | async-start | bytes 6291456 | tf_op jit(solution)/shard_map/all_to_all | solution.py:58
  73.4 1.2 copy-start.2
  73.4 1.7 copy-start.3
  142.7 48.4 %copy-start.4 = (f32[128]{0:T(128)S(1)}, f32[128]{0:T(128)}, u32[]{:S(2)}) copy-start(f32[128]{0:T(128)} %param.16) | copy-start | bytes 1540
  309.7 5.2 %copy-start.5 = (f32[128]{0:T(128)S(1)}, f32[128]{0:T(128)}, u32[]{:S(2)}) copy-start(f32[128]{0:T(128)} %param.17) | copy-start | bytes 1540
  309.7 76.6 %all-to-all-start.1 = ((bf16[12,32,16,256]{3,2,0,1:T(8,128)(2,1)}), bf16[12,32,16,256]{3,2,0,1:T(8,128)(2,1)}, u32[]{:S(2)}, u32[]{:S(2)}) async-start(bf16[12,32,16,256]{3,2,0,1:T(8,128)(2,1)} %copy.48), calls=%async_computation.1 | async-start | bytes 6291456 | tf_op jit(solution)/shard_map/all_to_all | solution.py:94
where the time goes:
time: 455 us; the launch traced here: 447 us
  local copies, waits for them, and re-layouts  126 us (28%)
  waiting for transfers between devices  123 us (27%)
  matrix products  115 us (25%)
  blocking collectives  38.1 us (8%)
  other arithmetic  31.1 us (7%)
  starting transfers between devices  12.7 us (3%)
    all_to_all x1, waiting for transfers between devices, on_device(): lax.all_to_all(returning, 'lat', split_axis=1, concat_axis=0, tiled=True)  70.4 us
    all_to_all x1, waiting for transfers between devices, on_device(): lax.all_to_all(outbound, 'lat', split_axis=0, concat_axis=2, tiled=True)[0]  52.9 us
    dot_general x12, matrix products, column(): lax.dot_general(out_weight, hidden, contract_first, preferred_element_typ...  46.7 us
    psum x1, blocking collectives, on_device(): global_sum = lax.psum(partial_value, 'lat')  38.1 us
    dot_general x12, matrix products, column(): lax.dot_general(wave_table, column_out, (((1,), (1,)), ((), ())), preferr...  36.5 us
    dynamic_update_slice x24, local copies, waits for them, and re-layouts, on_device(): coeffs = lax.map(column, grid_field)  30.1 us
    rev x1, local copies, waits for them, and re-layouts, on_device(): south_part = weighted[half_lat:][::-1]  29.9 us
    rev x1, local copies, waits for them, and re-layouts, on_device(): south_half[::-1]  29.9 us
  transfers between devices with their start and end apart: 2, of which 2 were waited for; matrix products, arithmetic and copies ran while one was open for 4% of the time, Pallas kernels for 0%

commit v1 on v0

v1 whole, which is shorter than its diff:
```python
import functools
import math

import jax
import jax.numpy as jnp
from jax import lax
from jax.experimental import pallas as pl
from jax.experimental.pallas import tpu as pltpu
from jax.sharding import PartitionSpec as P

NN = 512
NLON = 1536
MB = 4
LON_TILE = 512


def wavenumbers(block_order, slot_count):
    slot_ids = jnp.arange(slot_count, dtype=jnp.int32)
    blocks = block_order.shape[0]
    matches = (slot_ids // MB)[:, None] == jnp.arange(blocks, dtype=jnp.int32)[None, :]
    chosen = jnp.sum(jnp.where(matches, block_order[None, :], 0), axis=1)
    return chosen * MB + slot_ids % MB


def lon_table(wave_all):
    longitude = jnp.arange(NLON, dtype=jnp.int32)
    phase_index = wave_all[:, None] * longitude[None, :] % NLON
    angles = phase_index.astype(jnp.float32) * (2.0 * math.pi / NLON)
    return jnp.concatenate([jnp.cos(angles), jnp.sin(angles)], axis=0).astype(jnp.bfloat16)


def lat_weights_of(latitude_index, lat_total):
    latitude = latitude_index.astype(jnp.float32)
    return jnp.cos(math.pi * ((latitude + 0.5) / lat_total - 0.5))


def column_kernel(weight_ref, grid_ref, scale_ref, in_t_ref, bias_ref, out_t_ref, table_ref, o_ref):
    j = pl.program_id(0)
    chan = grid_ref.shape[1]
    waves = table_ref.shape[0] // 2
    scale = scale_ref[...]
    acc = jnp.zeros((2 * waves, chan), jnp.float32)
    for c in range(NLON // LON_TILE):
        lo = c * LON_TILE
        g = grid_ref[0, :, lo:lo + LON_TILE].astype(jnp.float32)
        normed = (g * scale).astype(jnp.bfloat16)
        pre = jnp.dot(in_t_ref[...], normed, preferred_element_type=jnp.float32) + bias_ref[...]
        hidden = jax.nn.gelu(pre).astype(jnp.bfloat16)
        col = jnp.dot(out_t_ref[...], hidden, preferred_element_type=jnp.float32).astype(
            jnp.bfloat16
        )
        acc = acc + lax.dot_general(
            table_ref[:, lo:lo + LON_TILE],
            col,
            (((1,), (1,)), ((), ())),
            preferred_element_type=jnp.float32,
        )
    inv_root = 1.0 / math.sqrt(NLON)
    w = weight_ref[j]
    cos_part = (acc[:waves] * inv_root).astype(jnp.bfloat16).astype(jnp.float32)
    sin_part = ((-acc[waves:]) * inv_root).astype(jnp.bfloat16).astype(jnp.float32)
    o_ref[0, :, :chan] = (w * cos_part).astype(jnp.bfloat16)
    o_ref[0, :, chan:] = (w * sin_part).astype(jnp.bfloat16)


def column_network(lat_w, grid_field, col_scale, in_weight, in_bias, out_weight, wave_table):
    lat_local, chan, nlon = grid_field.shape
    hid = in_weight.shape[1]
    two_waves = wave_table.shape[0]
    full = lambda shape: pl.BlockSpec(shape, lambda j: (0,) * len(shape))
    return pl.pallas_call(
        column_kernel,
        grid=(lat_local,),
        in_specs=[
            pl.BlockSpec(memory_space=pltpu.SMEM),
            pl.BlockSpec((1, chan, nlon), lambda j: (j, 0, 0)),
            full((chan, 1)),
            full((hid, chan)),
            full((hid, 1)),
            full((chan, hid)),
            full((two_waves, nlon)),
        ],
        out_specs=pl.BlockSpec((1, two_waves // 2, 2 * chan), lambda j: (j, 0, 0)),
        out_shape=jax.ShapeDtypeStruct((lat_local, two_waves // 2, 2 * chan), jnp.bfloat16),
        compiler_params=pltpu.CompilerParams(vmem_limit_bytes=48 * 1024 * 1024),
    )(
        lat_w,
        grid_field,
        col_scale[:, None],
        in_weight.T,
        in_bias[:, None],
        out_weight.T,
        wave_table,
    )


def on_device(spectral, lat_basis, block_order, in_weight, in_bias, out_weight, col_gain, damping):
    devices = lax.axis_size("lat")
    my_index = lax.axis_index("lat")
    row_count = spectral.shape[0]
    degrees = spectral.shape[1]
    chan_width = spectral.shape[2]
    chan_count = chan_width // 2
    half_lat = lat_basis.shape[2]
    lat_total = 2 * half_lat
    lat_local = lat_total // devices
    wave_total = row_count * devices
    wave_all = wavenumbers(block_order, wave_total)
    wave_own = lax.dynamic_slice_in_dim(wave_all, my_index * row_count, row_count)
    degree = jnp.arange(degrees, dtype=jnp.int32)
    inside = degree[None, :] >= wave_own[:, None]
    parity = jnp.where((degree[None, :] + wave_own[:, None]) % 2 == 0, 1.0, -1.0).astype(
        jnp.float32
    )
    masked = jnp.where(inside[:, :, None], spectral, jnp.zeros_like(spectral))
    flipped = jnp.where(parity[:, :, None] > 0, masked, -masked)
    both = jnp.stack([masked, flipped], axis=0)
    fourier = jnp.einsum(
        "rnj,srnc->sjrc", lat_basis, both, preferred_element_type=jnp.float32
    ).astype(jnp.bfloat16)
    outbound = fourier.reshape(devices, lat_local, row_count, chan_width)
    wave_table = lon_table(wave_all)
    rows_in = lax.all_to_all(outbound, "lat", split_axis=0, concat_axis=2, tiled=True)[0]
    signed = jnp.concatenate([rows_in[:, :, :chan_count], -rows_in[:, :, chan_count:]], axis=1)
    grid_field = jnp.einsum(
        "jrk,rl->jkl", signed, wave_table, preferred_element_type=jnp.float32
    ).astype(jnp.bfloat16)
    row_ids = my_index * lat_local + jnp.arange(lat_local, dtype=jnp.int32)
    lat_ids = jnp.where(row_ids < half_lat, row_ids, lat_total + half_lat - 1 - row_ids)
    weight_own = lat_weights_of(lat_ids, lat_total)
    grid_wide = grid_field.astype(jnp.float32)
    partial_value = jnp.sum(weight_own[:, None, None] * grid_wide * grid_wide, axis=(0, 2))
    global_sum = lax.psum(partial_value, "lat")
    weight_all = lat_weights_of(jnp.arange(lat_total, dtype=jnp.int32), lat_total)
    variance = global_sum / (NLON * jnp.sum(weight_all))
    col_scale = col_gain * lax.rsqrt(variance + 1e-05)
    weighted_local = column_network(
        weight_own, grid_field, col_scale, in_weight, in_bias, out_weight, wave_table
    )
    returning = weighted_local.reshape(lat_local, devices, row_count, chan_width)
    weighted = lax.all_to_all(returning, "lat", split_axis=1, concat_axis=0, tiled=True)[:, 0]
    weighted = weighted.reshape(2, half_lat, row_count, chan_width)
    factor = 2.0 * math.sqrt(degrees * wave_total / lat_total)
    sums = jnp.einsum("rnj,sjrc->srnc", lat_basis, weighted, preferred_element_type=jnp.float32)
    legendre = factor * (sums[0] + parity[:, :, None] * sums[1])
    damp_all = jnp.concatenate([damping, damping])
    wave_factor = (degree * (degree + 1)).astype(jnp.float32) / (NN * NN)
    damped = legendre - damp_all[None, None, :] * wave_factor[None, :, None] * spectral.astype(
        jnp.float32
    )
    return jnp.where(inside[:, :, None], damped, jnp.zeros_like(damped))


def solution(mesh):
    in_specs = (
        P(("member", "lat"), None, None),
        P("lat", None, None),
        P(),
        P(),
        P(),
        P(),
        P(),
        P(),
    )
    out_specs = P(("member", "lat"), None, None)
    return jax.shard_map(
        on_device, mesh=mesh, in_specs=in_specs, out_specs=out_specs, check_vma=False
    )
```

time: 455 us -> 299 us (0.66); the launches traced: 447 us -> 298 us
  local copies, waits for them, and re-layouts: 126 us -> 23.7 us
  matrix products: 115 us -> 20.9 us
  Pallas kernels: 0 us -> 46.8 us
  other arithmetic: 31.1 us -> 36 us
    dot_general x28 -> x2, matrix products: 104 us -> 12.6 us  [the longest x1 10.5 us: on_device(): jnp.einsum('rnj,sjrc->srnc', lat_basis, weighted, preferred_element_type=...]
    rev x2 -> x0, local copies, waits for them, and re-layouts: 59.7 us -> none  [the longest x1 29.9 us: on_device(): south_part = weighted[half_lat:][::-1]]
    pallas_call x0 -> x1, Pallas kernels: none -> 46.8 us  [column_network(): pl.pallas_call(column_kernel, grid=(lat_local,), in_specs=[pl.BlockSpec(m...]
    dynamic_update_slice x24 -> x0, local copies, waits for them, and re-layouts: 30.1 us -> none  [on_device(): coeffs = lax.map(column, grid_field)]
    select_n x0 -> x1, other arithmetic: none -> 9.79 us  [on_device(): return jnp.where(inside[:, :, None], damped, jnp.zeros_like(damped))]
    select_n x1 -> x0, local copies, waits for them, and re-layouts: 9.24 us -> none  [on_device(): return jnp.where(inside[:, :, None], damped, jnp.zeros_like(damped))]
    convert_element_type x14 -> x0, other arithmetic: 7.23 us -> none  [the longest x1 3.96 us: on_device(): weighted = (weight_all[:, None, None] * lax.all_to_all(returning, 'lat',...]
    another operation x1 -> x2, other arithmetic: 13.5 us -> 19.6 us
  transfers between devices with their start and end apart: 2 -> 2, of which waited for: 2 -> 2; matrix products, arithmetic and copies ran while one was open for 4% -> 7% of each run, Pallas kernels for 0% -> 0%
where the time goes in v1:
time: 299 us; the launch traced here: 298 us
  waiting for transfers between devices  119 us (40%)
  Pallas kernels  46.8 us (16%)
  blocking collectives  38.1 us (13%)
  other arithmetic  36 us (12%)
  local copies, waits for them, and re-layouts  23.7 us (8%)
  matrix products  20.9 us (7%)
  starting transfers between devices  12.5 us (4%)
    all_to_all x1, waiting for transfers between devices, on_device(): lax.all_to_all(returning, 'lat', split_axis=1, concat_axis=0, tiled=True)  70.4 us
    all_to_all x1, waiting for transfers between devices, on_device(): lax.all_to_all(outbound, 'lat', split_axis=0, concat_axis=2, tiled=True)[0]  49.1 us
    pallas_call x1, Pallas kernels, column_network(): pl.pallas_call(column_kernel, grid=(lat_local,), in_specs=[pl.BlockSpec(m...  46.8 us
    psum x1, blocking collectives, on_device(): global_sum = lax.psum(partial_value, 'lat')  38.1 us
    another operation x1, other arithmetic  13.5 us
    unnamed x28, local copies, waits for them, and re-layouts  12.2 us
    dot_general x1, matrix products, on_device(): jnp.einsum('rnj,sjrc->srnc', lat_basis, weighted, preferred_element_type=...  10.5 us
    select_n x1, other arithmetic, on_device(): return jnp.where(inside[:, :, None], damped, jnp.zeros_like(damped))  9.79 us
  transfers between devices with their start and end apart: 2, of which 2 were waited for; matrix products, arithmetic and copies ran while one was open for 7% of the time, Pallas kernels for 0%

profile of v1, /device:TPU:0, one launch (start us, length us, event | category | flops | bytes accessed | tf_op | source)
XLA Modules:
  0.0 298.4 jit_solution(3604581288134519286)
XLA Ops:
  1.2 6.1 %fusion.11 = (bf16[1,16,512,256]{3,2,0,1:T(8,128)(2,1)S(1)}, bf16[1,16,512,256]{3,2,0,1:T(8,128)(2,1)S(1)}) fusion(bf16[16,512,256]{2,1,0:T(8,128)(2,1)} %param.8, pred[16,512]{1,0:T(8,128)(4,1)S(1)} %get-tuple-element.11, pred[16,512]{1,0:T(8,128)(4,1)S(1)} %get-tuple-element.12), kind=kLoop, calls=%fused_computation.19 | loop fusion | flops 6291456 | bytes 12599296 | tf_op jit(solution)/shard_map/stack | solution.py:117
  7.3 2.1 convert_bitcast_fusion
  9.4 3.5 %copy.29 = bf16[2,192,16,256]{3,2,1,0:T(8,128)(2,1)} copy(bf16[2,192,16,256]{3,1,0,2:T(8,128)(2,1)S(1)} %convert_bitcast_fusion) | data formatting | bytes 6291456 | tf_op jit(solution)/shard_map/convert_element_type | solution.py:120
  12.9 7.4 %all-to-all-start = ((bf16[32,12,16,256]{3,2,1,0:T(8,128)(2,1)}), bf16[32,12,16,256]{3,2,1,0:T(8,128)(2,1)}, u32[]{:S(2)}, u32[]{:S(2)}) async-start(bf16[32,12,16,256]{3,2,1,0:T(8,128)(2,1)} %bitcast.59), calls=%async_computation | async-start | bytes 6291456 | tf_op jit(solution)/shard_map/all_to_all | solution.py:123
  20.4 1.1 copy.33
  21.5 1.8 copy.34
  25.7 13.5 %cosine_convert_fusion = (bf16[512,1536]{1,0:T(8,128)(2,1)S(1)}, bf16[512,1536]{1,0:T(8,128)(2,1)S(1)}) fusion(s32[512]{0:T(512)S(1)} %fusion.40), kind=kLoop, calls=%fused_computation.31 | loop fusion | flops 8650752 | bytes 3147776 | tf_op jit(solution)/shard_map/convert
  39.2 1.2 copy-done.4
  40.9 1.8 pad_maximum_fusion.table_ref
  42.7 49.1 %all-to-all-done = bf16[32,12,16,256]{3,2,1,0:T(8,128)(2,1)} async-done(((bf16[32,12,16,256]{3,2,1,0:T(8,128)(2,1)}), bf16[32,12,16,256]{3,2,1,0:T(8,128)(2,1)}, u32[]{:S(2)}, u32[]{:S(2)}) %all-to-all-start) | async-done | bytes 3145760 | tf_op jit(solution)/shard_map/all_to_all | solution.py:123
  91.8 2.2 copy.30
  94.0 2.5 fusion.52
  96.5 2.6 copy.44
  99.1 2.6 copy.45
  101.7 1.9 neg.7
  104.1 8.3 %fusion = (f32[128]{0:T(128)S(1)}, bf16[12,128,1536]{2,1,0:T(8,128)(2,1)}) fusion(f32[12]{0:T(128)S(1)} %fusion.49.weight_ref, bf16[512,1536]{1,0:T(8,128)(2,1)S(1)} %copy-done.7, bf16[512,1536]{1,0:T(8,128)(2,1)S(1)} %copy-done.5, bf16[12,512,128]{1,2,0:T(8,128)(2,1)S(1)} %neg.7, bf16[12,512,128]{1,2,0:T(8,128)(2,1)} %copy.44), kind=kOutput, calls=%fused_computation.1 | convolution fusion | flops 4856217600 | bytes 11010608 | tf_op jit(solution)/shard_map/jrk,rl->jkl/dot_general | solution.py:125
  112.4 38.1 %psum.7 = f32[128]{0:T(128)S(1)} all-reduce(f32[128]{0:T(128)S(1)} %get-tuple-element.13), channel_id=1, replica_groups=mesh['member'=1,'lat'=32] {'lat'}, use_global_device_ids=true, to_apply=%region_2.3 | all-reduce | flops 128 | bytes 1024 | tf_op jit(solution)/shard_map/psum | solution.py:133
  150.7 1.0 copy-done.1
  152.6 46.8 %shard_map.82 = bf16[12,512,256]{2,1,0:T(8,128)(2,1)S(1)} custom-call(f32[12]{0:T(128)S(1)} %fusion.49.weight_ref, bf16[12,128,1536]{2,1,0:T(8,128)(2,1)} %get-tuple-element.14.grid_ref, f32[128,1]{1,0:T(8,128)S(1)} %copy.35.scale_ref, bf16[1024,128]{1,0:T(8,128)(2,1)S(1)} %bitcast.57, f32[1024,1]{1,0:T(8,128)S(1)} %copy-done.1, ...), custom_call_target="tpu_custom_call" | custom-call | tf_op jit(solution)/shard_map/pallas_call | solution.py:71
  199.4 2.1 copy.37
  201.5 5.1 %all-to-all-start.1 = ((bf16[12,32,16,256]{3,2,0,1:T(8,128)(2,1)}), bf16[12,32,16,256]{3,2,0,1:T(8,128)(2,1)}, u32[]{:S(2)}, u32[]{:S(2)}) async-start(bf16[12,32,16,256]{3,2,0,1:T(8,128)(2,1)} %copy.37), calls=%async_computation.1 | async-start | bytes 6291456 | tf_op jit(solution)/shard_map/all_to_all | solution.py:141
  207.7 70.4 %all-to-all-done.1 = bf16[12,32,16,256]{3,2,0,1:T(8,128)(2,1)} async-done(((bf16[12,32,16,256]{3,2,0,1:T(8,128)(2,1)}), bf16[12,32,16,256]{3,2,0,1:T(8,128)(2,1)}, u32[]{:S(2)}, u32[]{:S(2)}) %all-to-all-start.1) | async-done | bytes 3145760 | tf_op jit(solution)/shard_map/all_to_all | solution.py:141
  278.1 10.5 %convolution_bitcast_fusion = f32[2,16,512,256]{3,2,1,0:T(8,128)} fusion(bf16[2,192,16,256]{3,2,1,0:T(8,128)(2,1)} %bitcast.18, bf16[16,512,192]{1,2,0:T(8,128)(2,1)S(1)} %copy-done), kind=kOutput, calls=%fused_computation.13 | convolution fusion | flops 1610612736 | bytes 23068672 | tf_op jit(solution)/shard_map/rnj,sjrc->srnc/dot_general | solution.py:144
  288.6 9.8 %fusion.5 = f32[16,512,256]{2,1,0:T(8,128)} fusion(f32[2,16,512,256]{3,2,1,0:T(8,128)} %convolution_bitcast_fusion, bf16[16,512,256]{2,1,0:T(8,128)(2,1)S(1)} %copy-done.3, f32[512,256]{1,0:T(8,128)S(1)} %copy-done.8, f32[16,512]{1,0:T(8,128)S(1)} %fusion.32, pred[16,512]{1,0:T(8,128)(4,1)S(1)} %get-tuple-element.11), kind=kLoop, calls=%fused_computation.7 | loop fusion | flops 14680064 | bytes 29925376 | tf_op jit(solution)/shard_map/jit(_where)/select_n | solution.py:151
  (36 shorter events, 6.0 us)
Async XLA Ops:
  0.0 7.3 %copy-start = (bf16[16,512,192]{1,2,0:T(8,128)(2,1)S(1)}, bf16[16,512,192]{1,2,0:T(8,128)(2,1)}, u32[]{:S(2)}) copy-start(bf16[16,512,192]{1,2,0:T(8,128)(2,1)} %param.9) | copy-start | bytes 9437188
  12.9 10.3 %copy-start.9 = (f32[1024]{0:T(1024)S(1)}, f32[1024]{0:T(1024)}, u32[]{:S(2)}) copy-start(f32[1024]{0:T(1024)} %param.12) | copy-start | bytes 12292
  12.9 78.9 %all-to-all-start = ((bf16[32,12,16,256]{3,2,1,0:T(8,128)(2,1)}), bf16[32,12,16,256]{3,2,1,0:T(8,128)(2,1)}, u32[]{:S(2)}, u32[]{:S(2)}) async-start(bf16[32,12,16,256]{3,2,1,0:T(8,128)(2,1)} %bitcast.59), calls=%async_computation | async-start | bytes 6291456 | tf_op jit(solution)/shard_map/all_to_all | solution.py:123
  39.2 1.2 copy-start.4
  39.2 1.6 copy-start.6
  101.7 1.9 copy-start.5
  101.7 2.4 copy-start.7
  104.1 46.4 %copy-start.10 = (f32[128]{0:T(128)S(1)}, f32[128]{0:T(128)}, u32[]{:S(2)}) copy-start(f32[128]{0:T(128)} %param.14) | copy-start | bytes 1540
  150.6 1.0 copy-start.1
  151.7 0.9 copy-start.2
  201.5 5.2 %copy-start.11 = (f32[128]{0:T(128)S(1)}, f32[128]{0:T(128)}, u32[]{:S(2)}) copy-start(f32[128]{0:T(128)} %param.15) | copy-start | bytes 1540
  201.5 76.6 %all-to-all-start.1 = ((bf16[12,32,16,256]{3,2,0,1:T(8,128)(2,1)}), bf16[12,32,16,256]{3,2,0,1:T(8,128)(2,1)}, u32[]{:S(2)}, u32[]{:S(2)}) async-start(bf16[12,32,16,256]{3,2,0,1:T(8,128)(2,1)} %copy.37), calls=%async_computation.1 | async-start | bytes 6291456 | tf_op jit(solution)/shard_map/all_to_all | solution.py:141
  278.1 10.5 %copy-start.3 = (bf16[16,512,256]{2,1,0:T(8,128)(2,1)S(1)}, bf16[16,512,256]{2,1,0:T(8,128)(2,1)}, u32[]{:S(2)}) copy-start(bf16[16,512,256]{2,1,0:T(8,128)(2,1)} %param.8) | copy-start | bytes 12582916
  278.1 10.5 %copy-start.8 = (f32[512,256]{1,0:T(8,128)S(1)}, f32[512,256]{1,0:T(8,128)}, u32[]{:S(2)}) copy-start(f32[512,256]{1,0:T(8,128)} %broadcast_multiply_fusion) | copy-start | bytes 1572868

commit v2 on v1

--- a/solution.py
+++ b/solution.py
@@ -94,6 +94,39 @@
     )
 
 
+def inverse_kernel(wave_ref, basis_ref, w_ref, spec_ref, damp_ref, o_ref, *, factor):
+    r = pl.program_id(0)
+    m = wave_ref[r]
+    basis = basis_ref[0]
+    east = jnp.dot(basis, w_ref[0, 0], preferred_element_type=jnp.float32)
+    west = jnp.dot(basis, w_ref[0, 1], preferred_element_type=jnp.float32)
+    degrees = basis.shape[0]
+    n = lax.broadcasted_iota(jnp.int32, (degrees, 1), 0)
+    parity = jnp.where((n + m) % 2 == 0, 1.0, -1.0).astype(jnp.float32)
+    legendre = factor * (east + parity * west)
+    wave_factor = (n * (n + 1)).astype(jnp.float32) / (NN * NN)
+    damped = legendre - damp_ref[...] * wave_factor * spec_ref[0].astype(jnp.float32)
+    o_ref[0] = jnp.where(n >= m, damped, 0.0)
+
+
+def inverse_legendre(wave_own, lat_basis, weighted, spectral, damp_all, factor):
+    rows, degrees, half_lat = lat_basis.shape
+    width = spectral.shape[2]
+    return pl.pallas_call(
+        functools.partial(inverse_kernel, factor=factor),
+        grid=(rows,),
+        in_specs=[
+            pl.BlockSpec(memory_space=pltpu.SMEM),
+            pl.BlockSpec((1, degrees, half_lat), lambda r: (r, 0, 0)),
+            pl.BlockSpec((1, 2, half_lat, width), lambda r: (r, 0, 0, 0)),
+            pl.BlockSpec((1, degrees, width), lambda r: (r, 0, 0)),
+            pl.BlockSpec((1, width), lambda r: (0, 0)),
+        ],
+        out_specs=pl.BlockSpec((1, degrees, width), lambda r: (r, 0, 0)),
+        out_shape=jax.ShapeDtypeStruct((rows, degrees, width), jnp.float32),
+    )(wave_own, lat_basis, weighted, spectral, damp_all[None, :])
+
+
 def on_device(spectral, lat_basis, block_order, in_weight, in_bias, out_weight, col_gain, damping):
     devices = lax.axis_size("lat")
     my_index = lax.axis_index("lat")
@@ -130,7 +163,10 @@
     weight_own = lat_weights_of(lat_ids, lat_total)
     grid_wide = grid_field.astype(jnp.float32)
     partial_value = jnp.sum(weight_own[:, None, None] * grid_wide * grid_wide, axis=(0, 2))
-    global_sum = lax.psum(partial_value, "lat")
+    gathered = lax.all_to_all(
+        jnp.broadcast_to(partial_value[None], (devices, chan_count)), "lat", 0, 0, tiled=True
+    )
+    global_sum = jnp.sum(gathered, axis=0)
     weight_all = lat_weights_of(jnp.arange(lat_total, dtype=jnp.int32), lat_total)
     variance = global_sum / (NLON * jnp.sum(weight_all))
     col_scale = col_gain * lax.rsqrt(variance + 1e-05)
@@ -139,16 +175,10 @@
     )
     returning = weighted_local.reshape(lat_local, devices, row_count, chan_width)
     weighted = lax.all_to_all(returning, "lat", split_axis=1, concat_axis=0, tiled=True)[:, 0]
-    weighted = weighted.reshape(2, half_lat, row_count, chan_width)
+    weighted = weighted.reshape(2, half_lat, row_count, chan_width).transpose(2, 0, 1, 3)
     factor = 2.0 * math.sqrt(degrees * wave_total / lat_total)
-    sums = jnp.einsum("rnj,sjrc->srnc", lat_basis, weighted, preferred_element_type=jnp.float32)
-    legendre = factor * (sums[0] + parity[:, :, None] * sums[1])
     damp_all = jnp.concatenate([damping, damping])
-    wave_factor = (degree * (degree + 1)).astype(jnp.float32) / (NN * NN)
-    damped = legendre - damp_all[None, None, :] * wave_factor[None, :, None] * spectral.astype(
-        jnp.float32
-    )
-    return jnp.where(inside[:, :, None], damped, jnp.zeros_like(damped))
+    return inverse_legendre(wave_own, lat_basis, weighted, spectral, damp_all, factor)
 
 
 def solution(mesh):

time: 299 us -> 263 us (0.88)
  blocking collectives: 38.1 us -> 0 us
  Pallas kernels: 46.8 us -> 62.3 us
  other arithmetic: 36 us -> 26.9 us
  matrix products: 20.9 us -> 12.1 us
  waiting for transfers between devices: 119 us -> 124 us
    psum x1 -> x0, blocking collectives: 38.1 us -> none  [on_device(): global_sum = lax.psum(partial_value, 'lat')]
    pallas_call x0 -> x1, Pallas kernels: none -> 15.2 us  [inverse_legendre(): pl.pallas_call(functools.partial(inverse_kernel, factor=factor), grid=(ro...]
    dot_general x1 -> x0, matrix products: 10.5 us -> none  [on_device(): jnp.einsum('rnj,sjrc->srnc', lat_basis, weighted, preferred_element_type=...]
    select_n x2 -> x0, other arithmetic: 9.88 us -> none  [the longest x1 9.79 us: on_device(): return jnp.where(inside[:, :, None], damped, jnp.zeros_like(damped))]
    all_to_all x1, waiting for transfers between devices: 49.1 us -> 56.4 us  [on_device(): lax.all_to_all(outbound, 'lat', split_axis=0, concat_axis=2, tiled=True)[0]]
    all_to_all x1, waiting for transfers between devices: 70.4 us -> 64.9 us  [on_device(): lax.all_to_all(returning, 'lat', split_axis=1, concat_axis=0, tiled=True)]
    all_to_all x0 -> x1, starting transfers between devices: none -> 4.12 us  [on_device(): lax.all_to_all(jnp.broadcast_to(partial_value[None], (devices, chan_count...]
    unnamed x28 -> x21, local copies, waits for them, and re-layouts: 12.2 us -> 10.5 us
  transfers between devices with their start and end apart: 2 -> 3, of which waited for: 2 -> 3; matrix products, arithmetic and copies ran while one was open for 7% -> 10% of each run, Pallas kernels for 0% -> 0%
where the time goes in v2:
time: 263 us; the launch traced here: 262 us
  waiting for transfers between devices  124 us (47%)
  Pallas kernels  62.3 us (24%)
  other arithmetic  26.9 us (10%)
  local copies, waits for them, and re-layouts  21.8 us (8%)
  starting transfers between devices  14.8 us (6%)
  matrix products  12.1 us (5%)
    all_to_all x1, waiting for transfers between devices, on_device(): lax.all_to_all(returning, 'lat', split_axis=1, concat_axis=0, tiled=True)  64.9 us
    all_to_all x1, waiting for transfers between devices, on_device(): lax.all_to_all(outbound, 'lat', split_axis=0, concat_axis=2, tiled=True)[0]  56.4 us
    pallas_call x1, Pallas kernels, column_network(): pl.pallas_call(column_kernel, grid=(lat_local,), in_specs=[pl.BlockSpec(m...  47.1 us
    pallas_call x1, Pallas kernels, inverse_legendre(): pl.pallas_call(functools.partial(inverse_kernel, factor=factor), grid=(ro...  15.2 us
    another operation x1, other arithmetic  15 us
    unnamed x21, local copies, waits for them, and re-layouts  10.5 us
    dot_general x1, matrix products, on_device(): jnp.einsum('jrk,rl->jkl', signed, wave_table, preferred_element_type=jnp....  10 us
    all_to_all x1, starting transfers between devices, on_device(): lax.all_to_all(outbound, 'lat', split_axis=0, concat_axis=2, tiled=True)[0]  7.28 us
  transfers between devices with their start and end apart: 3, of which 3 were waited for; matrix products, arithmetic and copies ran while one was open for 10% of the time, Pallas kernels for 0%

profile of v2, /device:TPU:0, one launch (start us, length us, event | category | flops | bytes accessed | tf_op | source)
XLA Modules:
  0.0 262.4 jit_solution(7355894755487264349)
XLA Ops:
  0.0 0.9 select_reduce_fusion
  1.1 6.2 %fusion.6 = (bf16[1,16,512,256]{3,2,0,1:T(8,128)(2,1)S(1)}, bf16[1,16,512,256]{3,2,0,1:T(8,128)(2,1)S(1)}) fusion(bf16[16,512,256]{2,1,0:T(8,128)(2,1)} %spec_ref.1, pred[16,512]{1,0:T(8,128)(4,1)S(1)} %get-tuple-element.11, pred[16,512]{1,0:T(8,128)(4,1)S(1)} %get-tuple-element.12), kind=kLoop, calls=%fused_computation.11 | loop fusion | flops 6291456 | bytes 12599296 | tf_op jit(solution)/shard_map/stack | solution.py:150
  7.4 2.1 convert_bitcast_fusion
  9.5 3.5 %copy.41 = bf16[2,192,16,256]{3,2,1,0:T(8,128)(2,1)} copy(bf16[2,192,16,256]{3,1,0,2:T(8,128)(2,1)S(1)} %convert_bitcast_fusion) | data formatting | bytes 6291456 | tf_op jit(solution)/shard_map/convert_element_type | solution.py:153
  13.0 7.3 %all-to-all-start = ((bf16[32,12,16,256]{3,2,1,0:T(8,128)(2,1)}), bf16[32,12,16,256]{3,2,1,0:T(8,128)(2,1)S(1)}, u32[]{:S(2)}, u32[]{:S(2)}) async-start(bf16[32,12,16,256]{3,2,1,0:T(8,128)(2,1)} %bitcast.45), calls=%async_computation | async-start | bytes 6291456 | tf_op jit(solution)/shard_map/all_to_all | solution.py:156
  20.3 15.0 %cosine_convert_fusion = (bf16[512,1536]{1,0:T(8,128)(2,1)}, bf16[512,1536]{1,0:T(8,128)(2,1)}) fusion(s32[512]{0:T(512)S(1)} %fusion.30), kind=kLoop, calls=%fused_computation.22 | loop fusion | flops 8650752 | bytes 3147776 | tf_op jit(solution)/shard_map/convert
  35.3 56.4 %all-to-all-done = bf16[32,12,16,256]{3,2,1,0:T(8,128)(2,1)S(1)} async-done(((bf16[32,12,16,256]{3,2,1,0:T(8,128)(2,1)}), bf16[32,12,16,256]{3,2,1,0:T(8,128)(2,1)S(1)}, u32[]{:S(2)}, u32[]{:S(2)}) %all-to-all-start) | async-done | bytes 3145760 | tf_op jit(solution)/shard_map/all_to_all | solution.py:156
  92.0 1.7 fusion.42
  93.7 1.7 copy.55
  95.4 1.5 neg.7
  96.9 1.6 copy.54
  98.5 10.0 %fusion = (f32[128]{0:T(128)S(1)}, bf16[12,128,1536]{2,1,0:T(8,128)(2,1)}) fusion(f32[12]{0:T(128)S(1)} %fusion.39.weight_ref, bf16[512,1536]{1,0:T(8,128)(2,1)} %get-tuple-element.10, bf16[512,1536]{1,0:T(8,128)(2,1)S(1)} %copy-done, bf16[12,512,128]{1,2,0:T(8,128)(2,1)} %neg.7, bf16[12,512,128]{1,2,0:T(8,128)(2,1)} %copy.54), kind=kOutput, calls=%fused_computation.1 | convolution fusion | flops 4856217600 | bytes 11010608 | tf_op jit(solution)/shard_map/jrk,rl->jkl/dot_general | solution.py:158
  109.1 4.1 %all-to-all-start.1 = ((f32[32,1,128]{2,1,0:T(1,128)}), f32[32,1,128]{2,1,0:T(1,128)S(1)}, u32[]{:S(2)}, u32[]{:S(2)}) async-start(f32[32,1,128]{2,1,0:T(1,128)} %broadcast_in_dim.70), calls=%async_computation.1 | async-start | bytes 32768 | tf_op jit(solution)/shard_map/all_to_all | solution.py:166
  113.2 1.8 pad_maximum_fusion.table_ref
  115.5 1.1 copy.47
  116.6 0.7 cosine_reduce_fusion
  117.9 2.2 all-to-all-done.1
  120.3 47.1 %shard_map.82 = bf16[12,512,256]{2,1,0:T(8,128)(2,1)S(1)} custom-call(f32[12]{0:T(128)S(1)} %fusion.39.weight_ref, bf16[12,128,1536]{2,1,0:T(8,128)(2,1)} %get-tuple-element.14.grid_ref, f32[128,1]{1,0:T(8,128)S(1)} %copy.48.scale_ref, bf16[1024,128]{1,0:T(8,128)(2,1)S(1)} %bitcast.42, f32[1024,1]{1,0:T(8,128)S(1)} %copy.49.bias_ref, ...), custom_call_target="tpu_custom_call" | custom-call | tf_op jit(solution)/shard_map/pallas_call | solution.py:71
  167.4 2.1 copy.50
  169.5 3.4 %all-to-all-start.2 = ((bf16[12,32,16,256]{3,2,0,1:T(8,128)(2,1)}), bf16[12,32,16,256]{3,2,0,1:T(8,128)(2,1)S(1)}, u32[]{:S(2)}, u32[]{:S(2)}) async-start(bf16[12,32,16,256]{3,2,0,1:T(8,128)(2,1)} %copy.50), calls=%async_computation.2 | async-start | bytes 6291456 | tf_op jit(solution)/shard_map/all_to_all | solution.py:177
  173.0 5.9 %copy.52.basis_ref = bf16[16,512,192]{2,1,0:T(8,128)(2,1)} copy(bf16[16,512,192]{1,2,0:T(8,128)(2,1)} %param.9) | data formatting | bytes 6291456 | tf_op args[1]
  179.5 64.9 %all-to-all-done.2 = bf16[12,32,16,256]{3,2,0,1:T(8,128)(2,1)S(1)} async-done(((bf16[12,32,16,256]{3,2,0,1:T(8,128)(2,1)}), bf16[12,32,16,256]{3,2,0,1:T(8,128)(2,1)S(1)}, u32[]{:S(2)}, u32[]{:S(2)}) %all-to-all-start.2) | async-done | bytes 3145760 | tf_op jit(solution)/shard_map/all_to_all | solution.py:177
  244.4 2.8 %copy.57 = bf16[2,192,16,256]{3,1,0,2:T(8,128)(2,1)} copy(bf16[2,192,16,256]{3,2,1,0:T(8,128)(2,1)S(1)} %bitcast.46) | data formatting | bytes 6291456 | tf_op jit(solution)/shard_map/reshape;squeeze | solution.py:178
  247.2 15.2 %shard_map.83 = f32[16,512,256]{2,1,0:T(8,128)} custom-call(s32[16]{0:T(128)} %copy-done.5, bf16[16,512,192]{2,1,0:T(8,128)(2,1)} %copy.52.basis_ref, bf16[16,2,192,256]{3,2,1,0:T(8,128)(2,1)} %bitcast.48, bf16[16,512,256]{2,1,0:T(8,128)(2,1)} %spec_ref.1, f32[1,256]{1,0:T(1,128)} %bitcast.51), custom_call_target="tpu_custom_call" | custom-call | tf_op jit(solution)/shard_map/pallas_call | solution.py:115
  (29 shorter events, 2.3 us)
Async XLA Ops:
  1.0 6.4 %copy-start.5 = (s32[16]{0:T(128)}, s32[16]{0:T(128)S(1)}, u32[]{:S(2)}) copy-start(s32[16]{0:T(128)S(1)} %dynamic_slice.3.wave_ref) | copy-start | bytes 196
  1.1 6.3 %copy-start.2 = (bf16[16,512,192]{1,2,0:T(8,128)(2,1)S(1)}, bf16[16,512,192]{1,2,0:T(8,128)(2,1)}, u32[]{:S(2)}) copy-start(bf16[16,512,192]{1,2,0:T(8,128)(2,1)} %param.9) | copy-start | bytes 9437188
  13.0 78.8 %all-to-all-start = ((bf16[32,12,16,256]{3,2,1,0:T(8,128)(2,1)}), bf16[32,12,16,256]{3,2,1,0:T(8,128)(2,1)S(1)}, u32[]{:S(2)}, u32[]{:S(2)}) async-start(bf16[32,12,16,256]{3,2,1,0:T(8,128)(2,1)} %bitcast.45), calls=%async_computation | async-start | bytes 6291456 | tf_op jit(solution)/shard_map/all_to_all | solution.py:156
  96.9 1.6 copy-start
  98.5 14.7 %copy-start.1 = (bf16[512,1536]{1,0:T(8,128)(2,1)S(1)}, bf16[512,1536]{1,0:T(8,128)(2,1)}, u32[]{:S(2)}) copy-start(bf16[512,1536]{1,0:T(8,128)(2,1)} %get-tuple-element.10) | copy-start | bytes 4718596
  109.1 11.1 %all-to-all-start.1 = ((f32[32,1,128]{2,1,0:T(1,128)}), f32[32,1,128]{2,1,0:T(1,128)S(1)}, u32[]{:S(2)}, u32[]{:S(2)}) async-start(f32[32,1,128]{2,1,0:T(1,128)} %broadcast_in_dim.70), calls=%async_computation.1 | async-start | bytes 32768 | tf_op jit(solution)/shard_map/all_to_all | solution.py:166
  113.2 1.9 copy-start.4
  113.2 2.1 copy-start.3
  113.2 7.0 %copy-start.6 = (f32[128]{0:T(128)S(1)}, f32[128]{0:T(128)}, u32[]{:S(2)}) copy-start(f32[128]{0:T(128)} %param.14) | copy-start | bytes 1540
  169.5 74.9 %all-to-all-start.2 = ((bf16[12,32,16,256]{3,2,0,1:T(8,128)(2,1)}), bf16[12,32,16,256]{3,2,0,1:T(8,128)(2,1)S(1)}, u32[]{:S(2)}, u32[]{:S(2)}) async-start(bf16[12,32,16,256]{3,2,0,1:T(8,128)(2,1)} %copy.50), calls=%async_computation.2 | async-start | bytes 6291456 | tf_op jit(solution)/shard_map/all_to_all | solution.py:177
  173.0 5.9 %copy-start.7 = (f32[128]{0:T(128)S(1)}, f32[128]{0:T(128)}, u32[]{:S(2)}) copy-start(f32[128]{0:T(128)} %param.15) | copy-start | bytes 1540

commit v3 on v2

--- a/solution.py
+++ b/solution.py
@@ -83,6 +83,11 @@
         out_specs=pl.BlockSpec((1, two_waves // 2, 2 * chan), lambda j: (j, 0, 0)),
         out_shape=jax.ShapeDtypeStruct((lat_local, two_waves // 2, 2 * chan), jnp.bfloat16),
         compiler_params=pltpu.CompilerParams(vmem_limit_bytes=48 * 1024 * 1024),
+        cost_estimate=pl.CostEstimate(
+            flops=2 * lat_local * nlon * (2 * hid * chan + two_waves * chan),
+            transcendentals=lat_local * nlon * hid,
+            bytes_accessed=two_waves * nlon * 2 + lat_local * (chan * nlon * 2 + two_waves * chan * 2),
+        ),
     )(
         lat_w,
         grid_field,
@@ -94,22 +99,45 @@
     )
 
 
-def inverse_kernel(wave_ref, basis_ref, w_ref, spec_ref, damp_ref, o_ref, *, factor):
+def east_kernel(basis_ref, w_ref, o_ref):
+    o_ref[0] = jnp.dot(basis_ref[0], w_ref[0], preferred_element_type=jnp.float32)
+
+
+def east_sum(lat_basis, north):
+    rows, degrees, half_lat = lat_basis.shape
+    width = north.shape[2]
+    return pl.pallas_call(
+        east_kernel,
+        grid=(rows,),
+        in_specs=[
+            pl.BlockSpec((1, degrees, half_lat), lambda r: (r, 0, 0)),
+            pl.BlockSpec((1, half_lat, width), lambda r: (r, 0, 0)),
+        ],
+        out_specs=pl.BlockSpec((1, degrees, width), lambda r: (r, 0, 0)),
+        out_shape=jax.ShapeDtypeStruct((rows, degrees, width), jnp.float32),
+        cost_estimate=pl.CostEstimate(
+            flops=2 * rows * degrees * half_lat * width,
+            transcendentals=0,
+            bytes_accessed=rows * (degrees * half_lat * 2 + half_lat * width * 2 + degrees * width * 4),
+        ),
+    )(lat_basis, north)
+
+
+def inverse_kernel(wave_ref, basis_ref, w_ref, east_ref, spec_ref, damp_ref, o_ref, *, factor):
     r = pl.program_id(0)
     m = wave_ref[r]
     basis = basis_ref[0]
-    east = jnp.dot(basis, w_ref[0, 0], preferred_element_type=jnp.float32)
-    west = jnp.dot(basis, w_ref[0, 1], preferred_element_type=jnp.float32)
+    west = jnp.dot(basis, w_ref[0], preferred_element_type=jnp.float32)
     degrees = basis.shape[0]
     n = lax.broadcasted_iota(jnp.int32, (degrees, 1), 0)
     parity = jnp.where((n + m) % 2 == 0, 1.0, -1.0).astype(jnp.float32)
-    legendre = factor * (east + parity * west)
+    legendre = factor * (east_ref[0] + parity * west)
     wave_factor = (n * (n + 1)).astype(jnp.float32) / (NN * NN)
     damped = legendre - damp_ref[...] * wave_factor * spec_ref[0].astype(jnp.float32)
     o_ref[0] = jnp.where(n >= m, damped, 0.0)
 
 
-def inverse_legendre(wave_own, lat_basis, weighted, spectral, damp_all, factor):
+def inverse_legendre(wave_own, lat_basis, south, east, spectral, damp_all, factor):
     rows, degrees, half_lat = lat_basis.shape
     width = spectral.shape[2]
     return pl.pallas_call(
@@ -118,13 +146,19 @@
         in_specs=[
             pl.BlockSpec(memory_space=pltpu.SMEM),
             pl.BlockSpec((1, degrees, half_lat), lambda r: (r, 0, 0)),
-            pl.BlockSpec((1, 2, half_lat, width), lambda r: (r, 0, 0, 0)),
+            pl.BlockSpec((1, half_lat, width), lambda r: (r, 0, 0)),
+            pl.BlockSpec((1, degrees, width), lambda r: (r, 0, 0)),
             pl.BlockSpec((1, degrees, width), lambda r: (r, 0, 0)),
             pl.BlockSpec((1, width), lambda r: (0, 0)),
         ],
         out_specs=pl.BlockSpec((1, degrees, width), lambda r: (r, 0, 0)),
         out_shape=jax.ShapeDtypeStruct((rows, degrees, width), jnp.float32),
-    )(wave_own, lat_basis, weighted, spectral, damp_all[None, :])
+        cost_estimate=pl.CostEstimate(
+            flops=2 * rows * degrees * half_lat * width,
+            transcendentals=0,
+            bytes_accessed=rows * (degrees * half_lat * 2 + half_lat * width * 2 + degrees * width * 10),
+        ),
+    )(wave_own, lat_basis, south, east, spectral, damp_all[None, :])
 
 
 def on_device(spectral, lat_basis, block_order, in_weight, in_bias, out_weight, col_gain, damping):
@@ -136,7 +170,7 @@
     chan_count = chan_width // 2
     half_lat = lat_basis.shape[2]
     lat_total = 2 * half_lat
-    lat_local = lat_total // devices
+    half_local = half_lat // devices
     wave_total = row_count * devices
     wave_all = wavenumbers(block_order, wave_total)
     wave_own = lax.dynamic_slice_in_dim(wave_all, my_index * row_count, row_count)
@@ -147,22 +181,32 @@
     )
     masked = jnp.where(inside[:, :, None], spectral, jnp.zeros_like(spectral))
     flipped = jnp.where(parity[:, :, None] > 0, masked, -masked)
-    both = jnp.stack([masked, flipped], axis=0)
-    fourier = jnp.einsum(
-        "rnj,srnc->sjrc", lat_basis, both, preferred_element_type=jnp.float32
-    ).astype(jnp.bfloat16)
-    outbound = fourier.reshape(devices, lat_local, row_count, chan_width)
     wave_table = lon_table(wave_all)
-    rows_in = lax.all_to_all(outbound, "lat", split_axis=0, concat_axis=2, tiled=True)[0]
-    signed = jnp.concatenate([rows_in[:, :, :chan_count], -rows_in[:, :, chan_count:]], axis=1)
-    grid_field = jnp.einsum(
-        "jrk,rl->jkl", signed, wave_table, preferred_element_type=jnp.float32
-    ).astype(jnp.bfloat16)
-    row_ids = my_index * lat_local + jnp.arange(lat_local, dtype=jnp.int32)
-    lat_ids = jnp.where(row_ids < half_lat, row_ids, lat_total + half_lat - 1 - row_ids)
-    weight_own = lat_weights_of(lat_ids, lat_total)
-    grid_wide = grid_field.astype(jnp.float32)
-    partial_value = jnp.sum(weight_own[:, None, None] * grid_wide * grid_wide, axis=(0, 2))
+
+    def to_grid(values):
+        fourier = jnp.einsum(
+            "rnj,rnc->jrc", lat_basis, values, preferred_element_type=jnp.float32
+        ).astype(jnp.bfloat16)
+        outbound = fourier.reshape(devices, half_local, row_count, chan_width)
+        rows_in = lax.all_to_all(outbound, "lat", split_axis=0, concat_axis=2, tiled=True)[0]
+        signed = jnp.concatenate(
+            [rows_in[:, :, :chan_count], -rows_in[:, :, chan_count:]], axis=1
+        )
+        return jnp.einsum(
+            "jrk,rl->jkl", signed, wave_table, preferred_element_type=jnp.float32
+        ).astype(jnp.bfloat16)
+
+    grid_north = to_grid(masked)
+    grid_south = to_grid(flipped)
+    j_ids = my_index * half_local + jnp.arange(half_local, dtype=jnp.int32)
+    weight_north = lat_weights_of(j_ids, lat_total)
+    weight_south = lat_weights_of(lat_total - 1 - j_ids, lat_total)
+
+    def sum_squares(grid_field, weight):
+        grid_wide = grid_field.astype(jnp.float32)
+        return jnp.sum(weight[:, None, None] * grid_wide * grid_wide, axis=(0, 2))
+
+    partial_value = sum_squares(grid_north, weight_north) + sum_squares(grid_south, weight_south)
     gathered = lax.all_to_all(
         jnp.broadcast_to(partial_value[None], (devices, chan_count)), "lat", 0, 0, tiled=True
     )
@@ -170,15 +214,21 @@
     weight_all = lat_weights_of(jnp.arange(lat_total, dtype=jnp.int32), lat_total)
     variance = global_sum / (NLON * jnp.sum(weight_all))
     col_scale = col_gain * lax.rsqrt(variance + 1e-05)
-    weighted_local = column_network(
-        weight_own, grid_field, col_scale, in_weight, in_bias, out_weight, wave_table
-    )
-    returning = weighted_local.reshape(lat_local, devices, row_count, chan_width)
-    weighted = lax.all_to_all(returning, "lat", split_axis=1, concat_axis=0, tiled=True)[:, 0]
-    weighted = weighted.reshape(2, half_lat, row_count, chan_width).transpose(2, 0, 1, 3)
+
+    def to_spectral(grid_field, weight):
+        weighted_local = column_network(
+            weight, grid_field, col_scale, in_weight, in_bias, out_weight, wave_table
+        )
+        returning = weighted_local.reshape(half_local, devices, row_count, chan_width)
+        weighted = lax.all_to_all(returning, "lat", split_axis=1, concat_axis=0, tiled=True)
+        return weighted.reshape(half_lat, row_count, chan_width).transpose(1, 0, 2)
+
+    north = to_spectral(grid_north, weight_north)
+    south = to_spectral(grid_south, weight_south)
+    east = east_sum(lat_basis, north)
     factor = 2.0 * math.sqrt(degrees * wave_total / lat_total)
     damp_all = jnp.concatenate([damping, damping])
-    return inverse_legendre(wave_own, lat_basis, weighted, spectral, damp_all, factor)
+    return inverse_legendre(wave_own, lat_basis, south, east, spectral, damp_all, factor)
 
 
 def solution(mesh):

time: 263 us -> 264 us (level)
  waiting for transfers between devices: 124 us -> 92.4 us
  Pallas kernels: 62.3 us -> 78.6 us
  starting transfers between devices: 14.8 us -> 23.3 us
  matrix products: 12.1 us -> 18.8 us
  other arithmetic: 26.9 us -> 22.3 us
  local copies, waits for them, and re-layouts: 21.8 us -> 25.7 us
    all_to_all x2 -> x4, waiting for transfers between devices: 121 us -> 91.2 us  [the longest x2 51.2 us: to_grid(): lax.all_to_all(outbound, 'lat', split_axis=0, concat_axis=2, tiled=True)[0]]
    pallas_call x0 -> x1, Pallas kernels: none -> 12.6 us  [east_sum(): pl.pallas_call(east_kernel, grid=(rows,), in_specs=[pl.BlockSpec((1, degr...]
    all_to_all x2 -> x4, starting transfers between devices: 10.7 us -> 19.4 us  [the longest x2 11.1 us: to_grid(): lax.all_to_all(outbound, 'lat', split_axis=0, concat_axis=2, tiled=True)[0]]
    dot_general x2 -> x4, matrix products: 12.1 us -> 18.8 us  [the longest x2 9.69 us: to_grid(): jnp.einsum('rnj,rnc->jrc', lat_basis, values, preferred_element_type=jnp....]
    another operation x2 -> x1, other arithmetic: 21.3 us -> 15 us
    reshape x1 -> x4, local copies, waits for them, and re-layouts: 2.09 us -> 7.48 us  [the longest x2 4.78 us: to_spectral(): return weighted.reshape(half_lat, row_count, chan_width).transpose(1, 0, 2)]
    another operation x1 -> x0, local copies, waits for them, and re-layouts: 2.77 us -> none  [on_device(): weighted.reshape(2, half_lat, row_count, chan_width).transpose(2, 0, 1, 3)]
    pallas_call x1 -> x2, Pallas kernels: 47.1 us -> 48.8 us  [column_network(): pl.pallas_call(column_kernel, grid=(lat_local,), in_specs=[pl.BlockSpec(m...]
  transfers between devices with their start and end apart: 3 -> 5, of which waited for: 3 -> 5; matrix products, arithmetic and copies ran while one was open for 10% -> 15% of each run, Pallas kernels for 0% -> 9%
where the time goes in v3:
time: 264 us; the launch traced here: 262 us
  waiting for transfers between devices  92.4 us (35%)
  Pallas kernels  78.6 us (30%)
  local copies, waits for them, and re-layouts  25.7 us (10%)
  starting transfers between devices  23.3 us (9%)
  other arithmetic  22.3 us (8%)
  matrix products  18.8 us (7%)
    all_to_all x2, waiting for transfers between devices, to_grid(): lax.all_to_all(outbound, 'lat', split_axis=0, concat_axis=2, tiled=True)[0]  51.2 us
    pallas_call x2, Pallas kernels, column_network(): pl.pallas_call(column_kernel, grid=(lat_local,), in_specs=[pl.BlockSpec(m...  48.8 us
    all_to_all x2, waiting for transfers between devices, to_spectral(): lax.all_to_all(returning, 'lat', split_axis=1, concat_axis=0, tiled=True)  40 us
    pallas_call x1, Pallas kernels, inverse_legendre(): pl.pallas_call(functools.partial(inverse_kernel, factor=factor), grid=(ro...  17.2 us
    another operation x1, other arithmetic  15 us
    pallas_call x1, Pallas kernels, east_sum(): pl.pallas_call(east_kernel, grid=(rows,), in_specs=[pl.BlockSpec((1, degr...  12.6 us
    unnamed x33, local copies, waits for them, and re-layouts  12.1 us
    all_to_all x2, starting transfers between devices, to_grid(): lax.all_to_all(outbound, 'lat', split_axis=0, concat_axis=2, tiled=True)[0]  11.1 us
  transfers between devices with their start and end apart: 5, of which 5 were waited for; matrix products, arithmetic and copies ran while one was open for 15% of the time, Pallas kernels for 9%

profile of v3, /device:TPU:0, one launch (start us, length us, event | category | flops | bytes accessed | tf_op | source)
XLA Modules:
  0.0 262.1 jit_solution(998370013736209061)
XLA Ops:
  1.1 5.6 %fusion.22 = bf16[192,16,256]{2,0,1:T(8,128)(2,1)S(1)} fusion(bf16[16,512,192]{1,2,0:T(8,128)(2,1)} %param.9, pred[16,512]{1,0:T(8,128)(4,1)S(1)} %get-tuple-element.12, bf16[16,512,256]{2,1,0:T(8,128)(2,1)} %spec_ref.1, pred[16,512]{1,0:T(8,128)(4,1)S(1)} %get-tuple-element.11), kind=kOutput, calls=%fused_computation.35 | convolution fusion | flops 816578560 | bytes 8929280 | tf_op jit(solution)/shard_map/rnj,rnc->jrc/dot_general | solution.py:187
  6.7 2.0 copy.59
  8.7 7.3 %all-to-all-start = ((bf16[32,6,16,256]{3,2,1,0:T(8,128)(2,1)}), bf16[32,6,16,256]{3,2,1,0:T(8,128)(2,1)S(1)}, u32[]{:S(2)}, u32[]{:S(2)}) async-start(bf16[32,6,16,256]{3,2,1,0:T(8,128)(2,1)} %bitcast.1), calls=%async_computation | async-start | bytes 3145728 | tf_op jit(solution)/shard_map/all_to_all | solution.py:191
  16.0 4.1 %fusion.23 = bf16[192,16,256]{2,0,1:T(8,128)(2,1)S(1)} fusion(bf16[16,512,192]{1,2,0:T(8,128)(2,1)} %param.9, bf16[16,512,256]{2,1,0:T(8,128)(2,1)} %spec_ref.1, pred[16,512]{1,0:T(8,128)(4,1)S(1)} %get-tuple-element.11), kind=kOutput, calls=%fused_computation.36 | convolution fusion | flops 808189952 | bytes 8921088 | tf_op jit(solution)/shard_map/rnj,rnc->jrc/dot_general | solution.py:187
  20.1 2.1 copy.63
  22.2 31.6 %all-to-all-done = bf16[32,6,16,256]{3,2,1,0:T(8,128)(2,1)S(1)} async-done(((bf16[32,6,16,256]{3,2,1,0:T(8,128)(2,1)}), bf16[32,6,16,256]{3,2,1,0:T(8,128)(2,1)S(1)}, u32[]{:S(2)}, u32[]{:S(2)}) %all-to-all-start) | async-done | bytes 1572896 | tf_op jit(solution)/shard_map/all_to_all | solution.py:191
  54.9 3.8 %all-to-all-start.1 = ((bf16[32,6,16,256]{3,2,1,0:T(8,128)(2,1)}), bf16[32,6,16,256]{3,2,1,0:T(8,128)(2,1)S(1)}, u32[]{:S(2)}, u32[]{:S(2)}) async-start(bf16[32,6,16,256]{3,2,1,0:T(8,128)(2,1)} %bitcast.7), calls=%async_computation.1 | async-start | bytes 3145728 | tf_op jit(solution)/shard_map/all_to_all | solution.py:191
  58.8 15.0 %cosine_convert_fusion = (bf16[512,1536]{1,0:T(8,128)(2,1)}, bf16[512,1536]{1,0:T(8,128)(2,1)}) fusion(s32[512]{0:T(512)S(1)} %fusion.33), kind=kLoop, calls=%fused_computation.18 | loop fusion | flops 8650752 | bytes 3147776 | tf_op jit(solution)/shard_map/convert
  76.8 19.6 %all-to-all-done.1 = bf16[32,6,16,256]{3,2,1,0:T(8,128)(2,1)S(1)} async-done(((bf16[32,6,16,256]{3,2,1,0:T(8,128)(2,1)}), bf16[32,6,16,256]{3,2,1,0:T(8,128)(2,1)S(1)}, u32[]{:S(2)}, u32[]{:S(2)}) %all-to-all-start.1) | async-done | bytes 1572896 | tf_op jit(solution)/shard_map/all_to_all | solution.py:191
  98.6 5.0 %fusion.1 = (f32[128]{0:T(128)S(1)}, bf16[6,128,1536]{2,1,0:T(8,128)(2,1)S(1)}) fusion(f32[6]{0:T(128)S(1)} %get-tuple-element.18.weight_ref, bf16[512,1536]{1,0:T(8,128)(2,1)} %get-tuple-element.10, bf16[512,1536]{1,0:T(8,128)(2,1)} %get-tuple-element.9, bf16[6,512,128]{1,2,0:T(8,128)(2,1)} %neg.10, bf16[6,512,128]{1,2,0:T(8,128)(2,1)S(1)} %copy-done.5), kind=kOutput, calls=%fused_computation.5 | convolution fusion | flops 2431254528 | bytes 7078424 | tf_op jit(solution)/shard_map/jrk,rl->jkl/dot_general | solution.py:195
  103.7 4.1 %fusion = (f32[128]{0:T(128)S(1)}, bf16[6,128,1536]{2,1,0:T(8,128)(2,1)}) fusion(f32[6]{0:T(128)S(1)} %get-tuple-element.17.weight_ref, bf16[512,1536]{1,0:T(8,128)(2,1)S(1)} %copy-done.4, bf16[512,1536]{1,0:T(8,128)(2,1)S(1)} %copy-done.3, bf16[6,512,128]{1,2,0:T(8,128)(2,1)S(1)} %neg.11, bf16[6,512,128]{1,2,0:T(8,128)(2,1)S(1)} %copy-done.6), kind=kOutput, calls=%fused_computation.4 | convolution fusion | flops 2431254528 | bytes 7078424 | tf_op jit(solution)/shard_map/jrk,rl->jkl/dot_general | solution.py:195
  108.4 4.0 %all-to-all-start.2 = ((f32[32,1,128]{2,1,0:T(1,128)}), f32[32,1,128]{2,1,0:T(1,128)S(1)}, u32[]{:S(2)}, u32[]{:S(2)}) async-start(f32[32,1,128]{2,1,0:T(1,128)} %broadcast_in_dim.73), calls=%async_computation.2 | async-start | bytes 32768 | tf_op jit(solution)/shard_map/all_to_all | solution.py:210
  112.4 3.8 %pad_maximum_fusion.table_ref = bf16[1024,1536]{1,0:T(8,128)(2,1)} fusion(bf16[512,1536]{1,0:T(8,128)(2,1)} %get-tuple-element.10, bf16[512,1536]{1,0:T(8,128)(2,1)} %get-tuple-element.9), kind=kLoop, calls=%fused_computation.14 | loop fusion | flops 6291456 | bytes 6291456 | tf_op jit(solution)/shard_map/concatenate | solution.py:29
  121.1 24.4 %shard_map.83 = bf16[6,512,256]{2,1,0:T(8,128)(2,1)S(1)} custom-call(f32[6]{0:T(128)S(1)} %get-tuple-element.17.weight_ref, bf16[6,128,1536]{2,1,0:T(8,128)(2,1)S(1)} %copy-done, f32[128,1]{1,0:T(8,128)S(1)} %copy.70.scale_ref, bf16[1024,128]{1,0:T(8,128)(2,1)S(1)} %bitcast.52, f32[1024,1]{1,0:T(8,128)S(1)} %copy.71.bias_ref, ...), custom_call_target="tpu_custom_call" | custom-call | flops 7247757312 | bytes 7077888 | tf_op jit(solution)/shard_map/pallas_call | solution.py:71
  146.8 4.5 %all-to-all-start.4 = ((bf16[6,32,16,256]{3,2,0,1:T(8,128)(2,1)}), bf16[6,32,16,256]{3,2,0,1:T(8,128)(2,1)}, u32[]{:S(2)}, u32[]{:S(2)}) async-start(bf16[6,32,16,256]{3,2,0,1:T(8,128)(2,1)} %copy.76), calls=%async_computation.4 | async-start | bytes 3145728 | tf_op jit(solution)/shard_map/all_to_all | solution.py:223
  151.4 24.4 %shard_map.82 = bf16[6,512,256]{2,1,0:T(8,128)(2,1)S(1)} custom-call(f32[6]{0:T(128)S(1)} %get-tuple-element.18.weight_ref, bf16[6,128,1536]{2,1,0:T(8,128)(2,1)S(1)} %get-tuple-element.16.grid_ref, f32[128,1]{1,0:T(8,128)S(1)} %copy.70.scale_ref, bf16[1024,128]{1,0:T(8,128)(2,1)S(1)} %bitcast.53, f32[1024,1]{1,0:T(8,128)S(1)} %copy.71.bias_ref, ...), custom_call_target="tpu_custom_call" | custom-call | flops 7247757312 | bytes 7077888 | tf_op jit(solution)/shard_map/pallas_call | solution.py:71
  177.1 12.0 %all-to-all-done.4 = bf16[6,32,16,256]{3,2,0,1:T(8,128)(2,1)} async-done(((bf16[6,32,16,256]{3,2,0,1:T(8,128)(2,1)}), bf16[6,32,16,256]{3,2,0,1:T(8,128)(2,1)}, u32[]{:S(2)}, u32[]{:S(2)}) %all-to-all-start.4) | async-done | bytes 1572896 | tf_op jit(solution)/shard_map/all_to_all | solution.py:223
  189.1 3.8 %all-to-all-start.3 = ((bf16[6,32,16,256]{3,2,0,1:T(8,128)(2,1)}), bf16[6,32,16,256]{3,2,0,1:T(8,128)(2,1)S(1)}, u32[]{:S(2)}, u32[]{:S(2)}) async-start(bf16[6,32,16,256]{3,2,0,1:T(8,128)(2,1)} %copy.72), calls=%async_computation.3 | async-start | bytes 3145728 | tf_op jit(solution)/shard_map/all_to_all | solution.py:223
  192.9 6.0 %copy.79.basis_ref = bf16[16,512,192]{2,1,0:T(8,128)(2,1)} copy(bf16[16,512,192]{1,2,0:T(8,128)(2,1)} %param.9) | data formatting | bytes 6291456 | tf_op args[1]
  199.5 3.1 %copy.86 = bf16[192,16,256]{2,0,1:T(8,128)(2,1)} copy(bf16[192,16,256]{2,1,0:T(8,128)(2,1)} %bitcast.24) | data formatting | bytes 3145728 | tf_op jit(solution)/shard_map/reshape | solution.py:224
  202.6 28.1 %all-to-all-done.3 = bf16[6,32,16,256]{3,2,0,1:T(8,128)(2,1)S(1)} async-done(((bf16[6,32,16,256]{3,2,0,1:T(8,128)(2,1)}), bf16[6,32,16,256]{3,2,0,1:T(8,128)(2,1)S(1)}, u32[]{:S(2)}, u32[]{:S(2)}) %all-to-all-start.3) | async-done | bytes 1572896 | tf_op jit(solution)/shard_map/all_to_all | solution.py:223
  230.6 1.7 copy.87
  232.3 12.6 %shard_map.84.east_ref = f32[16,512,256]{2,1,0:T(8,128)} custom-call(bf16[16,512,192]{2,1,0:T(8,128)(2,1)} %copy.79.basis_ref, bf16[16,192,256]{2,1,0:T(8,128)(2,1)} %bitcast.59), custom_call_target="tpu_custom_call" | custom-call | flops 805306368 | bytes 13107200 | tf_op jit(solution)/shard_map/pallas_call | solution.py:109
  244.9 17.2 %shard_map.85 = f32[16,512,256]{2,1,0:T(8,128)} custom-call(s32[16]{0:T(128)} %copy-done.10, bf16[16,512,192]{2,1,0:T(8,128)(2,1)} %copy.79.basis_ref, bf16[16,192,256]{2,1,0:T(8,128)(2,1)} %bitcast.60, f32[16,512,256]{2,1,0:T(8,128)} %shard_map.84.east_ref, bf16[16,512,256]{2,1,0:T(8,128)(2,1)} %spec_ref.1, f32[1,256]{1,0:T(1,128)} %bitcast.65), custom_call_target="tpu_custom_call" | custom-call | flops 805306368 | bytes 25690112 | tf_op jit(solution)/shard_map/pallas_call | solution.py:143
  (55 shorter events, 15.6 us)
Async XLA Ops:
  1.0 5.7 %copy-start.10 = (s32[16]{0:T(128)}, s32[16]{0:T(128)S(1)}, u32[]{:S(2)}) copy-start(s32[16]{0:T(128)S(1)} %dynamic_slice.3.wave_ref) | copy-start | bytes 196
  8.7 45.0 %all-to-all-start = ((bf16[32,6,16,256]{3,2,1,0:T(8,128)(2,1)}), bf16[32,6,16,256]{3,2,1,0:T(8,128)(2,1)S(1)}, u32[]{:S(2)}, u32[]{:S(2)}) async-start(bf16[32,6,16,256]{3,2,1,0:T(8,128)(2,1)} %bitcast.1), calls=%async_computation | async-start | bytes 3145728 | tf_op jit(solution)/shard_map/all_to_all | solution.py:191
  53.8 1.1 copy-start.1
  54.9 41.5 %all-to-all-start.1 = ((bf16[32,6,16,256]{3,2,1,0:T(8,128)(2,1)}), bf16[32,6,16,256]{3,2,1,0:T(8,128)(2,1)S(1)}, u32[]{:S(2)}, u32[]{:S(2)}) async-start(bf16[32,6,16,256]{3,2,1,0:T(8,128)(2,1)} %bitcast.7), calls=%async_computation.1 | async-start | bytes 3145728 | tf_op jit(solution)/shard_map/all_to_all | solution.py:191
  58.7 15.1 %copy-start.2 = (bf16[32,6,16,256]{3,2,1,0:T(8,128)(2,1)S(1)}, bf16[32,6,16,256]{3,2,1,0:T(8,128)(2,1)}, u32[]{:S(2)}) copy-start(bf16[32,6,16,256]{3,2,1,0:T(8,128)(2,1)} %copy-done.1) | copy-start | bytes 4718596
  96.9 1.7 copy-start.5
  98.6 5.0 %copy-start.3 = (bf16[512,1536]{1,0:T(8,128)(2,1)S(1)}, bf16[512,1536]{1,0:T(8,128)(2,1)}, u32[]{:S(2)}) copy-start(bf16[512,1536]{1,0:T(8,128)(2,1)} %get-tuple-element.9) | copy-start | bytes 4718596
  98.6 5.0 %copy-start.4 = (bf16[512,1536]{1,0:T(8,128)(2,1)S(1)}, bf16[512,1536]{1,0:T(8,128)(2,1)}, u32[]{:S(2)}) copy-start(bf16[512,1536]{1,0:T(8,128)(2,1)} %get-tuple-element.10) | copy-start | bytes 4718596
  98.6 5.0 %copy-start.6 = (bf16[6,512,128]{1,2,0:T(8,128)(2,1)S(1)}, bf16[6,512,128]{1,2,0:T(8,128)(2,1)}, u32[]{:S(2)}) copy-start(bf16[6,512,128]{1,2,0:T(8,128)(2,1)} %copy.82) | copy-start | bytes 2359300
  108.4 10.9 %all-to-all-start.2 = ((f32[32,1,128]{2,1,0:T(1,128)}), f32[32,1,128]{2,1,0:T(1,128)S(1)}, u32[]{:S(2)}, u32[]{:S(2)}) async-start(f32[32,1,128]{2,1,0:T(1,128)} %broadcast_in_dim.73), calls=%async_computation.2 | async-start | bytes 32768 | tf_op jit(solution)/shard_map/all_to_all | solution.py:210
  112.3 3.9 %copy-start.7 = (bf16[128,1024]{1,0:T(8,128)(2,1)S(1)}, bf16[128,1024]{1,0:T(8,128)(2,1)}, u32[]{:S(2)}) copy-start(bf16[128,1024]{1,0:T(8,128)(2,1)} %param.11) | copy-start | bytes 786436
  112.3 4.0 %copy-start.8 = (bf16[1024,128]{1,0:T(8,128)(2,1)S(1)}, bf16[1024,128]{1,0:T(8,128)(2,1)}, u32[]{:S(2)}) copy-start(bf16[1024,128]{1,0:T(8,128)(2,1)} %param.13) | copy-start | bytes 786436
  112.3 4.2 %copy-start.9 = (f32[1024]{0:T(1024)S(1)}, f32[1024]{0:T(1024)}, u32[]{:S(2)}) copy-start(f32[1024]{0:T(1024)} %param.12) | copy-start | bytes 12292
  112.4 7.0 %copy-start.11 = (f32[128]{0:T(128)S(1)}, f32[128]{0:T(128)}, u32[]{:S(2)}) copy-start(f32[128]{0:T(128)} %param.14) | copy-start | bytes 1540
  119.4 1.7 copy-start
  146.8 42.3 %all-to-all-start.4 = ((bf16[6,32,16,256]{3,2,0,1:T(8,128)(2,1)}), bf16[6,32,16,256]{3,2,0,1:T(8,128)(2,1)}, u32[]{:S(2)}, u32[]{:S(2)}) async-start(bf16[6,32,16,256]{3,2,0,1:T(8,128)(2,1)} %copy.76), calls=%async_computation.4 | async-start | bytes 3145728 | tf_op jit(solution)/shard_map/all_to_all | solution.py:223
  189.1 41.5 %all-to-all-start.3 = ((bf16[6,32,16,256]{3,2,0,1:T(8,128)(2,1)}), bf16[6,32,16,256]{3,2,0,1:T(8,128)(2,1)S(1)}, u32[]{:S(2)}, u32[]{:S(2)}) async-start(bf16[6,32,16,256]{3,2,0,1:T(8,128)(2,1)} %copy.72), calls=%async_computation.3 | async-start | bytes 3145728 | tf_op jit(solution)/shard_map/all_to_all | solution.py:223
  192.9 6.0 %copy-start.12 = (f32[128]{0:T(128)S(1)}, f32[128]{0:T(128)}, u32[]{:S(2)}) copy-start(f32[128]{0:T(128)} %param.15) | copy-start | bytes 1540

commit v4 on v2

--- a/solution.py
+++ b/solution.py
@@ -83,6 +83,11 @@
         out_specs=pl.BlockSpec((1, two_waves // 2, 2 * chan), lambda j: (j, 0, 0)),
         out_shape=jax.ShapeDtypeStruct((lat_local, two_waves // 2, 2 * chan), jnp.bfloat16),
         compiler_params=pltpu.CompilerParams(vmem_limit_bytes=48 * 1024 * 1024),
+        cost_estimate=pl.CostEstimate(
+            flops=2 * lat_local * nlon * (2 * hid * chan + two_waves * chan),
+            transcendentals=lat_local * nlon * hid,
+            bytes_accessed=two_waves * nlon * 2 + lat_local * (chan * nlon * 2 + two_waves * chan * 2),
+        ),
     )(
         lat_w,
         grid_field,
@@ -94,37 +99,46 @@
     )
 
 
-def inverse_kernel(wave_ref, basis_ref, w_ref, spec_ref, damp_ref, o_ref, *, factor):
-    r = pl.program_id(0)
-    m = wave_ref[r]
-    basis = basis_ref[0]
-    east = jnp.dot(basis, w_ref[0, 0], preferred_element_type=jnp.float32)
-    west = jnp.dot(basis, w_ref[0, 1], preferred_element_type=jnp.float32)
-    degrees = basis.shape[0]
+def inverse_kernel(wave_ref, basis_ref, north_ref, south_ref, spec_ref, damp_ref, o_ref, *, factor):
+    block = basis_ref.shape[0]
+    degrees = basis_ref.shape[1]
     n = lax.broadcasted_iota(jnp.int32, (degrees, 1), 0)
-    parity = jnp.where((n + m) % 2 == 0, 1.0, -1.0).astype(jnp.float32)
-    legendre = factor * (east + parity * west)
     wave_factor = (n * (n + 1)).astype(jnp.float32) / (NN * NN)
-    damped = legendre - damp_ref[...] * wave_factor * spec_ref[0].astype(jnp.float32)
-    o_ref[0] = jnp.where(n >= m, damped, 0.0)
-
-
-def inverse_legendre(wave_own, lat_basis, weighted, spectral, damp_all, factor):
+    for b in range(block):
+        m = wave_ref[pl.program_id(0) * block + b]
+        basis = basis_ref[b]
+        east = jnp.dot(basis, north_ref[b], preferred_element_type=jnp.float32)
+        west = jnp.dot(basis, south_ref[b], preferred_element_type=jnp.float32)
+        parity = jnp.where((n + m) % 2 == 0, 1.0, -1.0).astype(jnp.float32)
+        legendre = factor * (east + parity * west)
+        damped = legendre - damp_ref[...] * wave_factor * spec_ref[b].astype(jnp.float32)
+        o_ref[b] = jnp.where(n >= m, damped, 0.0)
+
+
+def inverse_legendre(wave_own, lat_basis, north, south, spectral, damp_all, factor):
     rows, degrees, half_lat = lat_basis.shape
     width = spectral.shape[2]
+    block = 4 if rows % 4 == 0 else 1
+    three = lambda shape: pl.BlockSpec(shape, lambda r: (r, 0, 0))
     return pl.pallas_call(
         functools.partial(inverse_kernel, factor=factor),
-        grid=(rows,),
+        grid=(rows // block,),
         in_specs=[
             pl.BlockSpec(memory_space=pltpu.SMEM),
-            pl.BlockSpec((1, degrees, half_lat), lambda r: (r, 0, 0)),
-            pl.BlockSpec((1, 2, half_lat, width), lambda r: (r, 0, 0, 0)),
-            pl.BlockSpec((1, degrees, width), lambda r: (r, 0, 0)),
+            three((block, degrees, half_lat)),
+            three((block, half_lat, width)),
+            three((block, half_lat, width)),
+            three((block, degrees, width)),
             pl.BlockSpec((1, width), lambda r: (0, 0)),
         ],
-        out_specs=pl.BlockSpec((1, degrees, width), lambda r: (r, 0, 0)),
+        out_specs=three((block, degrees, width)),
         out_shape=jax.ShapeDtypeStruct((rows, degrees, width), jnp.float32),
-    )(wave_own, lat_basis, weighted, spectral, damp_all[None, :])
+        cost_estimate=pl.CostEstimate(
+            flops=4 * rows * degrees * half_lat * width,
+            transcendentals=0,
+            bytes_accessed=rows * (degrees * half_lat * 2 + half_lat * width * 4 + degrees * width * 6),
+        ),
+    )(wave_own, lat_basis, north, south, spectral, damp_all[None, :])
 
 
 def on_device(spectral, lat_basis, block_order, in_weight, in_bias, out_weight, col_gain, damping):
@@ -136,7 +150,7 @@
     chan_count = chan_width // 2
     half_lat = lat_basis.shape[2]
     lat_total = 2 * half_lat
-    lat_local = lat_total // devices
+    half_local = half_lat // devices
     wave_total = row_count * devices
     wave_all = wavenumbers(block_order, wave_total)
     wave_own = lax.dynamic_slice_in_dim(wave_all, my_index * row_count, row_count)
@@ -147,22 +161,31 @@
     )
     masked = jnp.where(inside[:, :, None], spectral, jnp.zeros_like(spectral))
     flipped = jnp.where(parity[:, :, None] > 0, masked, -masked)
+    wave_table = lon_table(wave_all)
+
     both = jnp.stack([masked, flipped], axis=0)
     fourier = jnp.einsum(
         "rnj,srnc->sjrc", lat_basis, both, preferred_element_type=jnp.float32
     ).astype(jnp.bfloat16)
-    outbound = fourier.reshape(devices, lat_local, row_count, chan_width)
-    wave_table = lon_table(wave_all)
+    outbound = fourier.reshape(2, devices, half_local, row_count, chan_width).transpose(
+        1, 0, 2, 3, 4
+    ).reshape(devices, 2 * half_local, row_count, chan_width)
     rows_in = lax.all_to_all(outbound, "lat", split_axis=0, concat_axis=2, tiled=True)[0]
     signed = jnp.concatenate([rows_in[:, :, :chan_count], -rows_in[:, :, chan_count:]], axis=1)
     grid_field = jnp.einsum(
         "jrk,rl->jkl", signed, wave_table, preferred_element_type=jnp.float32
     ).astype(jnp.bfloat16)
-    row_ids = my_index * lat_local + jnp.arange(lat_local, dtype=jnp.int32)
-    lat_ids = jnp.where(row_ids < half_lat, row_ids, lat_total + half_lat - 1 - row_ids)
-    weight_own = lat_weights_of(lat_ids, lat_total)
-    grid_wide = grid_field.astype(jnp.float32)
-    partial_value = jnp.sum(weight_own[:, None, None] * grid_wide * grid_wide, axis=(0, 2))
+    grid_north = grid_field[:half_local]
+    grid_south = grid_field[half_local:]
+    j_ids = my_index * half_local + jnp.arange(half_local, dtype=jnp.int32)
+    weight_north = lat_weights_of(j_ids, lat_total)
+    weight_south = lat_weights_of(lat_total - 1 - j_ids, lat_total)
+
+    def sum_squares(grid_field, weight):
+        grid_wide = grid_field.astype(jnp.float32)
+        return jnp.sum(weight[:, None, None] * grid_wide * grid_wide, axis=(0, 2))
+
+    partial_value = sum_squares(grid_north, weight_north) + sum_squares(grid_south, weight_south)
     gathered = lax.all_to_all(
         jnp.broadcast_to(partial_value[None], (devices, chan_count)), "lat", 0, 0, tiled=True
     )
@@ -170,15 +193,20 @@
     weight_all = lat_weights_of(jnp.arange(lat_total, dtype=jnp.int32), lat_total)
     variance = global_sum / (NLON * jnp.sum(weight_all))
     col_scale = col_gain * lax.rsqrt(variance + 1e-05)
-    weighted_local = column_network(
-        weight_own, grid_field, col_scale, in_weight, in_bias, out_weight, wave_table
-    )
-    returning = weighted_local.reshape(lat_local, devices, row_count, chan_width)
-    weighted = lax.all_to_all(returning, "lat", split_axis=1, concat_axis=0, tiled=True)[:, 0]
-    weighted = weighted.reshape(2, half_lat, row_count, chan_width).transpose(2, 0, 1, 3)
+
+    def to_spectral(grid_field, weight):
+        weighted_local = column_network(
+            weight, grid_field, col_scale, in_weight, in_bias, out_weight, wave_table
+        )
+        returning = weighted_local.reshape(half_local, devices, row_count, chan_width)
+        weighted = lax.all_to_all(returning, "lat", split_axis=1, concat_axis=0, tiled=True)
+        return weighted.reshape(half_lat, row_count, chan_width).transpose(1, 0, 2)
+
+    north = to_spectral(grid_north, weight_north)
+    south = to_spectral(grid_south, weight_south)
     factor = 2.0 * math.sqrt(degrees * wave_total / lat_total)
     damp_all = jnp.concatenate([damping, damping])
-    return inverse_legendre(wave_own, lat_basis, weighted, spectral, damp_all, factor)
+    return inverse_legendre(wave_own, lat_basis, north, south, spectral, damp_all, factor)
 
 
 def solution(mesh):

time: 263 us -> 248 us (0.943)
  waiting for transfers between devices: 124 us -> 95.5 us
  local copies, waits for them, and re-layouts: 21.8 us -> 37.5 us
  starting transfers between devices: 14.8 us -> 18.5 us
  Pallas kernels: 62.3 us -> 58.7 us
    all_to_all x1 -> x2, waiting for transfers between devices: 64.9 us -> 40.3 us  [to_spectral(): lax.all_to_all(returning, 'lat', split_axis=1, concat_axis=0, tiled=True)]
    unnamed x21 -> x29, local copies, waits for them, and re-layouts: 10.5 us -> 16.2 us
    reshape x1 -> x4, local copies, waits for them, and re-layouts: 2.09 us -> 7.52 us  [the longest x2 4.79 us: to_spectral(): return weighted.reshape(half_lat, row_count, chan_width).transpose(1, 0, 2)]
    pallas_call x1, Pallas kernels: 15.2 us -> 10.2 us  [inverse_legendre(): pl.pallas_call(functools.partial(inverse_kernel, factor=factor), grid=(ro...]
    slice x0 -> x1, local copies, waits for them, and re-layouts: none -> 4.29 us  [on_device(): grid_south = grid_field[half_local:]]
    all_to_all x1, waiting for transfers between devices: 56.4 us -> 52.5 us  [on_device(): lax.all_to_all(outbound, 'lat', split_axis=0, concat_axis=2, tiled=True)[0]]
    all_to_all x1 -> x2, starting transfers between devices: 3.43 us -> 6.97 us  [to_spectral(): lax.all_to_all(returning, 'lat', split_axis=1, concat_axis=0, tiled=True)]
    another operation x1 -> x0, local copies, waits for them, and re-layouts: 2.77 us -> none  [on_device(): weighted.reshape(2, half_lat, row_count, chan_width).transpose(2, 0, 1, 3)]
  transfers between devices with their start and end apart: 3 -> 4, of which waited for: 3 -> 4; matrix products, arithmetic and copies ran while one was open for 10% -> 13% of each run, Pallas kernels for 0% -> 10%
where the time goes in v4:
time: 248 us; the launch traced here: 247 us
  waiting for transfers between devices  95.5 us (39%)
  Pallas kernels  58.7 us (24%)
  local copies, waits for them, and re-layouts  37.5 us (15%)
  other arithmetic  26.8 us (11%)
  starting transfers between devices  18.5 us (7%)
  matrix products  9.53 us (4%)
    all_to_all x1, waiting for transfers between devices, on_device(): lax.all_to_all(outbound, 'lat', split_axis=0, concat_axis=2, tiled=True)[0]  52.5 us
    pallas_call x2, Pallas kernels, column_network(): pl.pallas_call(column_kernel, grid=(lat_local,), in_specs=[pl.BlockSpec(m...  48.5 us
    all_to_all x2, waiting for transfers between devices, to_spectral(): lax.all_to_all(returning, 'lat', split_axis=1, concat_axis=0, tiled=True)  40.3 us
    unnamed x29, local copies, waits for them, and re-layouts  16.2 us
    another operation x1, other arithmetic  13.5 us
    pallas_call x1, Pallas kernels, inverse_legendre(): pl.pallas_call(functools.partial(inverse_kernel, factor=factor), grid=(ro...  10.2 us
    dot_general x1, matrix products, on_device(): jnp.einsum('jrk,rl->jkl', signed, wave_table, preferred_element_type=jnp....  7.42 us
    all_to_all x1, starting transfers between devices, on_device(): lax.all_to_all(outbound, 'lat', split_axis=0, concat_axis=2, tiled=True)[0]  7.4 us
  transfers between devices with their start and end apart: 4, of which 4 were waited for; matrix products, arithmetic and copies ran while one was open for 13% of the time, Pallas kernels for 10%

profile of v4, /device:TPU:0, one launch (start us, length us, event | category | flops | bytes accessed | tf_op | source)
XLA Modules:
  0.0 247.4 jit_solution(8982430701025559648)
XLA Ops:
  1.1 6.2 %fusion.7 = (bf16[1,16,512,256]{3,2,0,1:T(8,128)(2,1)S(1)}, bf16[1,16,512,256]{3,2,0,1:T(8,128)(2,1)S(1)}) fusion(bf16[16,512,256]{2,1,0:T(8,128)(2,1)} %spec_ref.1, pred[16,512]{1,0:T(8,128)(4,1)S(1)} %get-tuple-element.15, pred[16,512]{1,0:T(8,128)(4,1)S(1)} %get-tuple-element.16), kind=kLoop, calls=%fused_computation.13 | loop fusion | flops 6291456 | bytes 12599296 | tf_op jit(solution)/shard_map/stack | solution.py:166
  7.4 2.1 convert_bitcast_fusion
  11.3 2.0 copy.53
  13.3 7.4 %all-to-all-start = ((bf16[32,12,16,256]{3,2,1,0:T(8,128)(2,1)}), bf16[32,12,16,256]{3,2,1,0:T(8,128)(2,1)}, u32[]{:S(2)}, u32[]{:S(2)}) async-start(bf16[32,12,16,256]{3,2,1,0:T(8,128)(2,1)} %bitcast.8), calls=%async_computation | async-start | bytes 6291456 | tf_op jit(solution)/shard_map/all_to_all | solution.py:173
  22.6 13.5 %cosine_convert_fusion = (bf16[512,1536]{1,0:T(8,128)(2,1)S(1)}, bf16[512,1536]{1,0:T(8,128)(2,1)S(1)}) fusion(s32[512]{0:T(512)S(1)} %fusion.31), kind=kLoop, calls=%fused_computation.23 | loop fusion | flops 8650752 | bytes 3147776 | tf_op jit(solution)/shard_map/convert
  37.8 1.8 pad_maximum_fusion.table_ref
  39.6 52.5 %all-to-all-done = bf16[32,12,16,256]{3,2,1,0:T(8,128)(2,1)} async-done(((bf16[32,12,16,256]{3,2,1,0:T(8,128)(2,1)}), bf16[32,12,16,256]{3,2,1,0:T(8,128)(2,1)}, u32[]{:S(2)}, u32[]{:S(2)}) %all-to-all-start) | async-done | bytes 3145760 | tf_op jit(solution)/shard_map/all_to_all | solution.py:173
  92.1 2.2 copy.54
  94.3 2.5 %fusion.38 = (bf16[12,512,128]{2,1,0:T(8,128)(2,1)}, bf16[12,512,128]{2,1,0:T(8,128)(2,1)}) fusion(bf16[12,512,256]{2,1,0:T(8,128)(2,1)S(1)} %bitcast.57), kind=kLoop, calls=%fused_computation.64 | loop fusion | bytes 6291456 | tf_op jit(solution)/shard_map/slice | solution.py:174
  100.0 2.7 %copy.70 = bf16[12,512,128]{1,2,0:T(8,128)(2,1)} copy(bf16[12,512,128]{2,1,0:T(8,128)(2,1)} %get-tuple-element.11) | data formatting | bytes 3145728
  102.7 7.4 %convolution_convert_fusion = bf16[12,128,1536]{2,1,0:T(8,128)(2,1)S(1)} fusion(bf16[12,512,128]{1,2,0:T(8,128)(2,1)} %neg.7, bf16[12,512,128]{1,2,0:T(8,128)(2,1)} %copy.70, bf16[512,1536]{1,0:T(8,128)(2,1)} %copy-done.4, bf16[512,1536]{1,0:T(8,128)(2,1)S(1)} %copy-done.3), kind=kOutput, calls=%fused_computation.10 | convolution fusion | flops 4846780416 | bytes 11010048 | tf_op jit(solution)/shard_map/jrk,rl->jkl/dot_general | solution.py:175
  110.2 2.2 copy-done.1
  114.4 4.1 %all-to-all-start.1 = ((f32[32,1,128]{2,1,0:T(1,128)}), f32[32,1,128]{2,1,0:T(1,128)S(1)}, u32[]{:S(2)}, u32[]{:S(2)}) async-start(f32[32,1,128]{2,1,0:T(1,128)} %broadcast_in_dim.73), calls=%async_computation.1 | async-start | bytes 32768 | tf_op jit(solution)/shard_map/all_to_all | solution.py:189
  118.5 4.3 %fusion.37 = (bf16[6,128,1536]{2,1,0:T(8,128)(2,1)}, bf16[6,128,1536]{2,1,0:T(8,128)(2,1)S(1)}) fusion(bf16[12,128,1536]{2,1,0:T(8,128)(2,1)} %copy-done.1), kind=kLoop, calls=%fused_computation.63 | loop fusion | bytes 9437184 | tf_op jit(solution)/shard_map/slice | solution.py:179
  122.8 2.7 %all-to-all-done.1 = f32[32,1,128]{2,1,0:T(1,128)S(1)} async-done(((f32[32,1,128]{2,1,0:T(1,128)}), f32[32,1,128]{2,1,0:T(1,128)S(1)}, u32[]{:S(2)}, u32[]{:S(2)}) %all-to-all-start.1) | async-done | bytes 16416 | tf_op jit(solution)/shard_map/all_to_all | solution.py:189
  127.3 24.2 %shard_map.83 = bf16[6,512,256]{2,1,0:T(8,128)(2,1)S(1)} custom-call(f32[6]{0:T(128)S(1)} %get-tuple-element.17.weight_ref, bf16[6,128,1536]{2,1,0:T(8,128)(2,1)S(1)} %copy-done, f32[128,1]{1,0:T(8,128)S(1)} %copy.60.scale_ref, bf16[1024,128]{1,0:T(8,128)(2,1)S(1)} %bitcast.53, f32[1024,1]{1,0:T(8,128)S(1)} %copy.61.bias_ref, ...), custom_call_target="tpu_custom_call" | custom-call | flops 7247757312 | bytes 7077888 | tf_op jit(solution)/shard_map/pallas_call | solution.py:71
  152.9 3.4 %all-to-all-start.3 = ((bf16[6,32,16,256]{3,2,0,1:T(8,128)(2,1)}), bf16[6,32,16,256]{3,2,0,1:T(8,128)(2,1)}, u32[]{:S(2)}, u32[]{:S(2)}) async-start(bf16[6,32,16,256]{3,2,0,1:T(8,128)(2,1)} %copy.66), calls=%async_computation.3 | async-start | bytes 3145728 | tf_op jit(solution)/shard_map/all_to_all | solution.py:202
  156.3 24.2 %shard_map.82 = bf16[6,512,256]{2,1,0:T(8,128)(2,1)S(1)} custom-call(f32[6]{0:T(128)S(1)} %get-tuple-element.18.weight_ref, bf16[6,128,1536]{2,1,0:T(8,128)(2,1)S(1)} %get-tuple-element.8.grid_ref, f32[128,1]{1,0:T(8,128)S(1)} %copy.60.scale_ref, bf16[1024,128]{1,0:T(8,128)(2,1)S(1)} %bitcast.54, f32[1024,1]{1,0:T(8,128)S(1)} %copy.61.bias_ref, ...), custom_call_target="tpu_custom_call" | custom-call | flops 7247757312 | bytes 7077888 | tf_op jit(solution)/shard_map/pallas_call | solution.py:71
  182.0 12.2 %all-to-all-done.3 = bf16[6,32,16,256]{3,2,0,1:T(8,128)(2,1)} async-done(((bf16[6,32,16,256]{3,2,0,1:T(8,128)(2,1)}), bf16[6,32,16,256]{3,2,0,1:T(8,128)(2,1)}, u32[]{:S(2)}, u32[]{:S(2)}) %all-to-all-start.3) | async-done | bytes 1572896 | tf_op jit(solution)/shard_map/all_to_all | solution.py:202
  194.2 3.6 %all-to-all-start.2 = ((bf16[6,32,16,256]{3,2,0,1:T(8,128)(2,1)}), bf16[6,32,16,256]{3,2,0,1:T(8,128)(2,1)S(1)}, u32[]{:S(2)}, u32[]{:S(2)}) async-start(bf16[6,32,16,256]{3,2,0,1:T(8,128)(2,1)} %copy.62), calls=%async_computation.2 | async-start | bytes 3145728 | tf_op jit(solution)/shard_map/all_to_all | solution.py:202
  197.8 5.9 %copy.68.basis_ref = bf16[16,512,192]{2,1,0:T(8,128)(2,1)} copy(bf16[16,512,192]{1,2,0:T(8,128)(2,1)} %param.9) | data formatting | bytes 6291456 | tf_op args[1]
  204.3 3.1 %copy.74 = bf16[192,16,256]{2,0,1:T(8,128)(2,1)} copy(bf16[192,16,256]{2,1,0:T(8,128)(2,1)} %bitcast.26) | data formatting | bytes 3145728 | tf_op jit(solution)/shard_map/reshape | solution.py:203
  207.4 28.1 %all-to-all-done.2 = bf16[6,32,16,256]{3,2,0,1:T(8,128)(2,1)S(1)} async-done(((bf16[6,32,16,256]{3,2,0,1:T(8,128)(2,1)}), bf16[6,32,16,256]{3,2,0,1:T(8,128)(2,1)S(1)}, u32[]{:S(2)}, u32[]{:S(2)}) %all-to-all-start.2) | async-done | bytes 1572896 | tf_op jit(solution)/shard_map/all_to_all | solution.py:202
  237.2 10.2 %shard_map.84 = f32[16,512,256]{2,1,0:T(8,128)} custom-call(s32[16]{0:T(128)} %copy-done.9, bf16[16,512,192]{2,1,0:T(8,128)(2,1)} %copy.68.basis_ref, bf16[16,192,256]{2,1,0:T(8,128)(2,1)} %bitcast.61, bf16[16,192,256]{2,1,0:T(8,128)(2,1)} %bitcast.60, bf16[16,512,256]{2,1,0:T(8,128)(2,1)} %spec_ref.1, f32[1,256]{1,0:T(1,128)} %bitcast.64), custom_call_target="tpu_custom_call" | custom-call | flops 1610612736 | bytes 18874368 | tf_op jit(solution)/shard_map/pallas_call | solution.py:123
  (46 shorter events, 17.9 us)
Async XLA Ops:
  1.0 6.4 %copy-start.9 = (s32[16]{0:T(128)}, s32[16]{0:T(128)S(1)}, u32[]{:S(2)}) copy-start(s32[16]{0:T(128)S(1)} %dynamic_slice.3.wave_ref) | copy-start | bytes 196
  1.1 6.3 %copy-start.5 = (bf16[16,512,192]{1,2,0:T(8,128)(2,1)S(1)}, bf16[16,512,192]{1,2,0:T(8,128)(2,1)}, u32[]{:S(2)}) copy-start(bf16[16,512,192]{1,2,0:T(8,128)(2,1)} %param.9) | copy-start | bytes 9437188
  13.3 7.4 %copy-start.8 = (f32[1024]{0:T(1024)S(1)}, f32[1024]{0:T(1024)}, u32[]{:S(2)}) copy-start(f32[1024]{0:T(1024)} %param.12) | copy-start | bytes 12292
  13.3 7.7 %copy-start.6 = (bf16[128,1024]{1,0:T(8,128)(2,1)S(1)}, bf16[128,1024]{1,0:T(8,128)(2,1)}, u32[]{:S(2)}) copy-start(bf16[128,1024]{1,0:T(8,128)(2,1)} %param.11) | copy-start | bytes 786436
  13.3 7.8 %copy-start.7 = (bf16[1024,128]{1,0:T(8,128)(2,1)S(1)}, bf16[1024,128]{1,0:T(8,128)(2,1)}, u32[]{:S(2)}) copy-start(bf16[1024,128]{1,0:T(8,128)(2,1)} %param.13) | copy-start | bytes 786436
  13.3 78.9 %all-to-all-start = ((bf16[32,12,16,256]{3,2,1,0:T(8,128)(2,1)}), bf16[32,12,16,256]{3,2,1,0:T(8,128)(2,1)}, u32[]{:S(2)}, u32[]{:S(2)}) async-start(bf16[32,12,16,256]{3,2,1,0:T(8,128)(2,1)} %bitcast.8), calls=%async_computation | async-start | bytes 6291456 | tf_op jit(solution)/shard_map/all_to_all | solution.py:173
  36.2 1.2 copy-start.2
  36.2 1.7 copy-start.4
  100.0 2.7 %copy-start.3 = (bf16[512,1536]{1,0:T(8,128)(2,1)S(1)}, bf16[512,1536]{1,0:T(8,128)(2,1)}, u32[]{:S(2)}) copy-start(bf16[512,1536]{1,0:T(8,128)(2,1)} %copy-done.2) | copy-start | bytes 4718596
  110.2 2.2 copy-start.1
  114.4 11.1 %all-to-all-start.1 = ((f32[32,1,128]{2,1,0:T(1,128)}), f32[32,1,128]{2,1,0:T(1,128)S(1)}, u32[]{:S(2)}, u32[]{:S(2)}) async-start(f32[32,1,128]{2,1,0:T(1,128)} %broadcast_in_dim.73), calls=%async_computation.1 | async-start | bytes 32768 | tf_op jit(solution)/shard_map/all_to_all | solution.py:189
  118.5 7.0 %copy-start.10 = (f32[128]{0:T(128)S(1)}, f32[128]{0:T(128)}, u32[]{:S(2)}) copy-start(f32[128]{0:T(128)} %param.14) | copy-start | bytes 1540
  125.6 1.7 copy-start
  152.9 41.3 %all-to-all-start.3 = ((bf16[6,32,16,256]{3,2,0,1:T(8,128)(2,1)}), bf16[6,32,16,256]{3,2,0,1:T(8,128)(2,1)}, u32[]{:S(2)}, u32[]{:S(2)}) async-start(bf16[6,32,16,256]{3,2,0,1:T(8,128)(2,1)} %copy.66), calls=%async_computation.3 | async-start | bytes 3145728 | tf_op jit(solution)/shard_map/all_to_all | solution.py:202
  194.2 41.3 %all-to-all-start.2 = ((bf16[6,32,16,256]{3,2,0,1:T(8,128)(2,1)}), bf16[6,32,16,256]{3,2,0,1:T(8,128)(2,1)S(1)}, u32[]{:S(2)}, u32[]{:S(2)}) async-start(bf16[6,32,16,256]{3,2,0,1:T(8,128)(2,1)} %copy.62), calls=%async_computation.2 | async-start | bytes 3145728 | tf_op jit(solution)/shard_map/all_to_all | solution.py:202
  197.7 5.9 %copy-start.11 = (f32[128]{0:T(128)S(1)}, f32[128]{0:T(128)}, u32[]{:S(2)}) copy-start(f32[128]{0:T(128)} %param.15) | copy-start | bytes 1540

commit v5 on v4

--- a/solution.py
+++ b/solution.py
@@ -34,26 +34,73 @@
     return jnp.cos(math.pi * ((latitude + 0.5) / lat_total - 0.5))
 
 
-def column_kernel(weight_ref, grid_ref, scale_ref, in_t_ref, bias_ref, out_t_ref, table_ref, o_ref):
+def grid_kernel(weight_ref, rows_ref, cos_t_ref, sin_t_ref, grid_ref, ssq_ref):
     j = pl.program_id(0)
-    chan = grid_ref.shape[1]
+    chan = grid_ref.shape[2]
+    rows = rows_ref[0]
+    wide = jnp.dot(cos_t_ref[...], rows[:, :chan], preferred_element_type=jnp.float32)
+    wide = wide + jnp.dot(sin_t_ref[...], rows[:, chan:], preferred_element_type=jnp.float32)
+    grid = wide.astype(jnp.bfloat16)
+    grid_ref[0] = grid
+    g = grid.astype(jnp.float32)
+    part = weight_ref[j] * jnp.sum(g * g, axis=0, keepdims=True)
+
+    @pl.when(j == 0)
+    def _():
+        ssq_ref[...] = part
+
+    @pl.when(j > 0)
+    def _():
+        ssq_ref[...] = ssq_ref[...] + part
+
+
+def grid_synthesis(lat_w, rows_in, cos_t, neg_sin_t):
+    lat_local, waves, width = rows_in.shape
+    chan = width // 2
+    nlon = cos_t.shape[0]
+    return pl.pallas_call(
+        grid_kernel,
+        grid=(lat_local,),
+        in_specs=[
+            pl.BlockSpec(memory_space=pltpu.SMEM),
+            pl.BlockSpec((1, waves, width), lambda j: (j, 0, 0)),
+            pl.BlockSpec((nlon, waves), lambda j: (0, 0)),
+            pl.BlockSpec((nlon, waves), lambda j: (0, 0)),
+        ],
+        out_specs=[
+            pl.BlockSpec((1, nlon, chan), lambda j: (j, 0, 0)),
+            pl.BlockSpec((1, chan), lambda j: (0, 0)),
+        ],
+        out_shape=[
+            jax.ShapeDtypeStruct((lat_local, nlon, chan), jnp.bfloat16),
+            jax.ShapeDtypeStruct((1, chan), jnp.float32),
+        ],
+        compiler_params=pltpu.CompilerParams(vmem_limit_bytes=48 * 1024 * 1024),
+        cost_estimate=pl.CostEstimate(
+            flops=2 * lat_local * nlon * waves * width,
+            transcendentals=0,
+            bytes_accessed=4 * nlon * waves + lat_local * (waves * width * 2 + nlon * chan * 2),
+        ),
+    )(lat_w, rows_in, cos_t, neg_sin_t)
+
+
+def column_kernel(weight_ref, grid_ref, scale_ref, in_w_ref, bias_ref, out_w_ref, table_ref, o_ref):
+    j = pl.program_id(0)
+    chan = grid_ref.shape[2]
     waves = table_ref.shape[0] // 2
     scale = scale_ref[...]
     acc = jnp.zeros((2 * waves, chan), jnp.float32)
     for c in range(NLON // LON_TILE):
         lo = c * LON_TILE
-        g = grid_ref[0, :, lo:lo + LON_TILE].astype(jnp.float32)
+        g = grid_ref[0, lo:lo + LON_TILE, :].astype(jnp.float32)
         normed = (g * scale).astype(jnp.bfloat16)
-        pre = jnp.dot(in_t_ref[...], normed, preferred_element_type=jnp.float32) + bias_ref[...]
+        pre = jnp.dot(normed, in_w_ref[...], preferred_element_type=jnp.float32) + bias_ref[...]
         hidden = jax.nn.gelu(pre).astype(jnp.bfloat16)
-        col = jnp.dot(out_t_ref[...], hidden, preferred_element_type=jnp.float32).astype(
+        col = jnp.dot(hidden, out_w_ref[...], preferred_element_type=jnp.float32).astype(
             jnp.bfloat16
         )
-        acc = acc + lax.dot_general(
-            table_ref[:, lo:lo + LON_TILE],
-            col,
-            (((1,), (1,)), ((), ())),
-            preferred_element_type=jnp.float32,
+        acc = acc + jnp.dot(
+            table_ref[:, lo:lo + LON_TILE], col, preferred_element_type=jnp.float32
         )
     inv_root = 1.0 / math.sqrt(NLON)
     w = weight_ref[j]
@@ -63,8 +110,8 @@
     o_ref[0, :, chan:] = (w * sin_part).astype(jnp.bfloat16)
 
 
-def column_network(lat_w, grid_field, col_scale, in_weight, in_bias, out_weight, wave_table):
-    lat_local, chan, nlon = grid_field.shape
+def column_network(lat_w, grid_t, col_scale, in_weight, in_bias, out_weight, wave_table):
+    lat_local, nlon, chan = grid_t.shape
     hid = in_weight.shape[1]
     two_waves = wave_table.shape[0]
     full = lambda shape: pl.BlockSpec(shape, lambda j: (0,) * len(shape))
@@ -73,11 +120,11 @@
         grid=(lat_local,),
         in_specs=[
             pl.BlockSpec(memory_space=pltpu.SMEM),
-            pl.BlockSpec((1, chan, nlon), lambda j: (j, 0, 0)),
-            full((chan, 1)),
+            pl.BlockSpec((1, nlon, chan), lambda j: (j, 0, 0)),
+            full((1, chan)),
+            full((chan, hid)),
+            full((1, hid)),
             full((hid, chan)),
-            full((hid, 1)),
-            full((chan, hid)),
             full((two_waves, nlon)),
         ],
         out_specs=pl.BlockSpec((1, two_waves // 2, 2 * chan), lambda j: (j, 0, 0)),
@@ -90,11 +137,11 @@
         ),
     )(
         lat_w,
-        grid_field,
-        col_scale[:, None],
-        in_weight.T,
-        in_bias[:, None],
-        out_weight.T,
+        grid_t,
+        col_scale[None, :],
+        in_weight,
+        in_bias[None, :],
+        out_weight,
         wave_table,
     )
 
@@ -171,28 +218,23 @@
         1, 0, 2, 3, 4
     ).reshape(devices, 2 * half_local, row_count, chan_width)
     rows_in = lax.all_to_all(outbound, "lat", split_axis=0, concat_axis=2, tiled=True)[0]
-    signed = jnp.concatenate([rows_in[:, :, :chan_count], -rows_in[:, :, chan_count:]], axis=1)
-    grid_field = jnp.einsum(
-        "jrk,rl->jkl", signed, wave_table, preferred_element_type=jnp.float32
-    ).astype(jnp.bfloat16)
-    grid_north = grid_field[:half_local]
-    grid_south = grid_field[half_local:]
     j_ids = my_index * half_local + jnp.arange(half_local, dtype=jnp.int32)
-    weight_north = lat_weights_of(j_ids, lat_total)
-    weight_south = lat_weights_of(lat_total - 1 - j_ids, lat_total)
-
-    def sum_squares(grid_field, weight):
-        grid_wide = grid_field.astype(jnp.float32)
-        return jnp.sum(weight[:, None, None] * grid_wide * grid_wide, axis=(0, 2))
-
-    partial_value = sum_squares(grid_north, weight_north) + sum_squares(grid_south, weight_south)
+    lat_ids = jnp.concatenate([j_ids, lat_total - 1 - j_ids])
+    weight_own = lat_weights_of(lat_ids, lat_total)
+    cos_t = wave_table[:wave_total].T
+    neg_sin_t = -wave_table[wave_total:].T
+    grid_t, partial_value = grid_synthesis(weight_own, rows_in, cos_t, neg_sin_t)
     gathered = lax.all_to_all(
-        jnp.broadcast_to(partial_value[None], (devices, chan_count)), "lat", 0, 0, tiled=True
+        jnp.broadcast_to(partial_value, (devices, chan_count)), "lat", 0, 0, tiled=True
     )
     global_sum = jnp.sum(gathered, axis=0)
     weight_all = lat_weights_of(jnp.arange(lat_total, dtype=jnp.int32), lat_total)
     variance = global_sum / (NLON * jnp.sum(weight_all))
     col_scale = col_gain * lax.rsqrt(variance + 1e-05)
+    grid_north = grid_t[:half_local]
+    grid_south = grid_t[half_local:]
+    weight_north = weight_own[:half_local]
+    weight_south = weight_own[half_local:]
 
     def to_spectral(grid_field, weight):
         weighted_local = column_network(

time: 248 us -> 244 us (0.984)
  waiting for transfers between devices: 95.5 us -> 79.6 us
  other arithmetic: 26.8 us -> 40.8 us
  Pallas kernels: 58.7 us -> 70.4 us
  matrix products: 9.53 us -> 2.11 us
  local copies, waits for them, and re-layouts: 37.5 us -> 30.3 us
    all_to_all x1, waiting for transfers between devices: 52.5 us -> 35.3 us  [on_device(): lax.all_to_all(outbound, 'lat', split_axis=0, concat_axis=2, tiled=True)[0]]
    slice x0 -> x1, other arithmetic: none -> 15 us  [on_device(): cos_t = wave_table[:wave_total].T]
    pallas_call x0 -> x1, Pallas kernels: none -> 14.3 us  [grid_synthesis(): pl.pallas_call(grid_kernel, grid=(lat_local,), in_specs=[pl.BlockSpec(mem...]
    another operation x1 -> x0, other arithmetic: 13.5 us -> none
    neg x1, other arithmetic: 1.46 us -> 13.4 us  [on_device(): neg_sin_t = -wave_table[wave_total:].T]
    unnamed x29 -> x17, local copies, waits for them, and re-layouts: 16.2 us -> 7.64 us
    dot_general x1 -> x0, matrix products: 7.42 us -> none  [on_device(): jnp.einsum('jrk,rl->jkl', signed, wave_table, preferred_element_type=jnp....]
    pallas_call x2, Pallas kernels: 48.5 us -> 45.9 us  [column_network(): pl.pallas_call(column_kernel, grid=(lat_local,), in_specs=[pl.BlockSpec(m...]
  transfers between devices with their start and end apart: 4 -> 4, of which waited for: 4 -> 4; matrix products, arithmetic and copies ran while one was open for 13% -> 21% of each run, Pallas kernels for 10% -> 9%
where the time goes in v5:
time: 244 us; the launch traced here: 243 us
  waiting for transfers between devices  79.6 us (33%)
  Pallas kernels  70.4 us (29%)
  other arithmetic  40.8 us (17%)
  local copies, waits for them, and re-layouts  30.3 us (12%)
  starting transfers between devices  18.5 us (8%)
    pallas_call x2, Pallas kernels, column_network(): pl.pallas_call(column_kernel, grid=(lat_local,), in_specs=[pl.BlockSpec(m...  45.9 us
    all_to_all x2, waiting for transfers between devices, to_spectral(): lax.all_to_all(returning, 'lat', split_axis=1, concat_axis=0, tiled=True)  41.6 us
    all_to_all x1, waiting for transfers between devices, on_device(): lax.all_to_all(outbound, 'lat', split_axis=0, concat_axis=2, tiled=True)[0]  35.3 us
    slice x1, other arithmetic, on_device(): cos_t = wave_table[:wave_total].T  15 us
    pallas_call x1, Pallas kernels, grid_synthesis(): pl.pallas_call(grid_kernel, grid=(lat_local,), in_specs=[pl.BlockSpec(mem...  14.3 us
    neg x1, other arithmetic, on_device(): neg_sin_t = -wave_table[wave_total:].T  13.4 us
    pallas_call x1, Pallas kernels, inverse_legendre(): pl.pallas_call(functools.partial(inverse_kernel, factor=factor), grid=(ro...  10.2 us
    unnamed x17, local copies, waits for them, and re-layouts  7.64 us
  transfers between devices with their start and end apart: 4, of which 4 were waited for; matrix products, arithmetic and copies ran while one was open for 21% of the time, Pallas kernels for 9%

profile of v5, /device:TPU:0, one launch (start us, length us, event | category | flops | bytes accessed | tf_op | source)
XLA Modules:
  0.0 242.6 jit_solution(9941487589385727372)
XLA Ops:
  1.1 6.2 %fusion.5 = (bf16[1,16,512,256]{3,2,0,1:T(8,128)(2,1)S(1)}, bf16[1,16,512,256]{3,2,0,1:T(8,128)(2,1)S(1)}) fusion(bf16[16,512,256]{2,1,0:T(8,128)(2,1)} %spec_ref.1, pred[16,512]{1,0:T(8,128)(4,1)S(1)} %get-tuple-element.18, pred[16,512]{1,0:T(8,128)(4,1)S(1)} %get-tuple-element.19), kind=kLoop, calls=%fused_computation.8 | loop fusion | flops 6291456 | bytes 12599296 | tf_op jit(solution)/shard_map/stack | solution.py:213
  7.4 2.1 convert_bitcast_fusion
  9.5 1.8 copy.48
  11.3 2.0 copy.49
  13.3 7.4 %all-to-all-start = ((bf16[32,12,16,256]{3,2,1,0:T(8,128)(2,1)}), bf16[32,12,16,256]{3,2,1,0:T(8,128)(2,1)}, u32[]{:S(2)}, u32[]{:S(2)}) async-start(bf16[32,12,16,256]{3,2,1,0:T(8,128)(2,1)} %bitcast.8), calls=%async_computation | async-start | bytes 6291456 | tf_op jit(solution)/shard_map/all_to_all | solution.py:220
  20.7 15.0 %cosine_convert_fusion = (bf16[512,1536]{1,0:T(8,128)(2,1)}, bf16[1536,512]{0,1:T(8,128)(2,1)S(1)}, bf16[512,1536]{1,0:T(8,128)(2,1)}) fusion(s32[512]{0:T(512)S(1)} %fusion.26), kind=kLoop, calls=%fused_computation.14 | loop fusion | flops 8650752 | bytes 4720640 | tf_op jit(solution)/shard_map/slice | solution.py:224
  36.4 13.4 %negate_bitcast_fusion = bf16[1536,512]{0,1:T(8,128)(2,1)} fusion(s32[512]{0:T(512)S(1)} %fusion.26), kind=kLoop, calls=%fused_computation.22 | loop fusion | flops 10223616 | bytes 1574912 | tf_op jit(solution)/shard_map/neg | solution.py:225
  53.1 3.7 %pad_maximum_fusion.table_ref = bf16[1024,1536]{1,0:T(8,128)(2,1)} fusion(bf16[512,1536]{1,0:T(8,128)(2,1)} %get-tuple-element.15, bf16[512,1536]{1,0:T(8,128)(2,1)} %get-tuple-element.13), kind=kLoop, calls=%fused_computation.11 | loop fusion | flops 6291456 | bytes 6291456 | tf_op jit(solution)/shard_map/concatenate | solution.py:29
  56.8 35.3 %all-to-all-done = bf16[32,12,16,256]{3,2,1,0:T(8,128)(2,1)} async-done(((bf16[32,12,16,256]{3,2,1,0:T(8,128)(2,1)}), bf16[32,12,16,256]{3,2,1,0:T(8,128)(2,1)}, u32[]{:S(2)}, u32[]{:S(2)}) %all-to-all-start) | async-done | bytes 3145760 | tf_op jit(solution)/shard_map/all_to_all | solution.py:220
  92.1 3.9 %copy.50 = bf16[1,12,32,16,256]{4,3,2,1,0:T(8,128)(2,1)} copy(bf16[1,12,32,16,256]{4,3,1,2,0:T(8,128)(2,1)} %bitcast.10) | data formatting | bytes 6291456 | tf_op jit(solution)/shard_map/all_to_all | solution.py:220
  96.0 14.3 %shard_map.82 = (bf16[12,1536,128]{2,1,0:T(8,128)(2,1)}, f32[1,128]{1,0:T(1,128)S(1)}) custom-call(f32[12]{0:T(128)S(1)} %multiply_cosine_fusion.weight_ref, bf16[12,512,256]{2,1,0:T(8,128)(2,1)} %bitcast.60, bf16[1536,512]{1,0:T(8,128)(2,1)S(1)} %copy.51.cos_t_ref, bf16[1536,512]{1,0:T(8,128)(2,1)S(1)} %copy.52.sin_t_ref), custom_call_target="tpu_custom_call" | custom-call | flops 4831838208 | bytes 11010048 | tf_op jit(solution)/shard_map/pallas_call | solution.py:61
  111.0 4.1 %all-to-all-start.1 = ((f32[32,1,128]{2,1,0:T(1,128)}), f32[32,1,128]{2,1,0:T(1,128)S(1)}, u32[]{:S(2)}, u32[]{:S(2)}) async-start(f32[32,1,128]{2,1,0:T(1,128)} %broadcast_in_dim.70), calls=%async_computation.1 | async-start | bytes 32768 | tf_op jit(solution)/shard_map/all_to_all | solution.py:227
  115.1 4.2 %fusion.33 = (bf16[6,1536,128]{2,1,0:T(8,128)(2,1)}, bf16[6,1536,128]{2,1,0:T(8,128)(2,1)S(1)}) fusion(bf16[12,1536,128]{2,1,0:T(8,128)(2,1)} %get-tuple-element.7), kind=kLoop, calls=%fused_computation.58 | loop fusion | bytes 9437184 | tf_op jit(solution)/shard_map/slice | solution.py:235
  119.3 2.7 %all-to-all-done.1 = f32[32,1,128]{2,1,0:T(1,128)S(1)} async-done(((f32[32,1,128]{2,1,0:T(1,128)}), f32[32,1,128]{2,1,0:T(1,128)S(1)}, u32[]{:S(2)}, u32[]{:S(2)}) %all-to-all-start.1) | async-done | bytes 16416 | tf_op jit(solution)/shard_map/all_to_all | solution.py:227
  123.8 23.0 %shard_map.84 = bf16[6,512,256]{2,1,0:T(8,128)(2,1)S(1)} custom-call(f32[6]{0:T(128)S(1)} %get-tuple-element.16.weight_ref, bf16[6,1536,128]{2,1,0:T(8,128)(2,1)S(1)} %copy-done, f32[1,128]{1,0:T(1,128)S(1)} %multiply_bitcast_fusion.scale_ref, bf16[128,1024]{1,0:T(8,128)(2,1)S(1)} %copy-done.1, f32[1,1024]{1,0:T(1,128)S(1)} %bitcast.54, ...), custom_call_target="tpu_custom_call" | custom-call | flops 7247757312 | bytes 7077888 | tf_op jit(solution)/shard_map/pallas_call | solution.py:118
  148.1 3.4 %all-to-all-start.3 = ((bf16[6,32,16,256]{3,2,0,1:T(8,128)(2,1)}), bf16[6,32,16,256]{3,2,0,1:T(8,128)(2,1)}, u32[]{:S(2)}, u32[]{:S(2)}) async-start(bf16[6,32,16,256]{3,2,0,1:T(8,128)(2,1)} %copy.56), calls=%async_computation.3 | async-start | bytes 3145728 | tf_op jit(solution)/shard_map/all_to_all | solution.py:244
  151.5 23.0 %shard_map.83 = bf16[6,512,256]{2,1,0:T(8,128)(2,1)S(1)} custom-call(f32[6]{0:T(128)S(1)} %get-tuple-element.17.weight_ref, bf16[6,1536,128]{2,1,0:T(8,128)(2,1)S(1)} %get-tuple-element.10.grid_ref, f32[1,128]{1,0:T(1,128)S(1)} %multiply_bitcast_fusion.scale_ref, bf16[128,1024]{1,0:T(8,128)(2,1)S(1)} %copy-done.1, f32[1,1024]{1,0:T(1,128)S(1)} %bitcast.55, ...), custom_call_target="tpu_custom_call" | custom-call | flops 7247757312 | bytes 7077888 | tf_op jit(solution)/shard_map/pallas_call | solution.py:118
  175.9 13.5 %all-to-all-done.3 = bf16[6,32,16,256]{3,2,0,1:T(8,128)(2,1)} async-done(((bf16[6,32,16,256]{3,2,0,1:T(8,128)(2,1)}), bf16[6,32,16,256]{3,2,0,1:T(8,128)(2,1)}, u32[]{:S(2)}, u32[]{:S(2)}) %all-to-all-start.3) | async-done | bytes 1572896 | tf_op jit(solution)/shard_map/all_to_all | solution.py:244
  189.4 3.6 %all-to-all-start.2 = ((bf16[6,32,16,256]{3,2,0,1:T(8,128)(2,1)}), bf16[6,32,16,256]{3,2,0,1:T(8,128)(2,1)S(1)}, u32[]{:S(2)}, u32[]{:S(2)}) async-start(bf16[6,32,16,256]{3,2,0,1:T(8,128)(2,1)} %copy.54), calls=%async_computation.2 | async-start | bytes 3145728 | tf_op jit(solution)/shard_map/all_to_all | solution.py:244
  193.0 5.9 %copy.58.basis_ref = bf16[16,512,192]{2,1,0:T(8,128)(2,1)} copy(bf16[16,512,192]{1,2,0:T(8,128)(2,1)} %param.9) | data formatting | bytes 6291456 | tf_op args[1]
  199.5 3.1 %copy.62 = bf16[192,16,256]{2,0,1:T(8,128)(2,1)} copy(bf16[192,16,256]{2,1,0:T(8,128)(2,1)} %bitcast.26) | data formatting | bytes 3145728 | tf_op jit(solution)/shard_map/reshape | solution.py:245
  202.6 28.1 %all-to-all-done.2 = bf16[6,32,16,256]{3,2,0,1:T(8,128)(2,1)S(1)} async-done(((bf16[6,32,16,256]{3,2,0,1:T(8,128)(2,1)}), bf16[6,32,16,256]{3,2,0,1:T(8,128)(2,1)S(1)}, u32[]{:S(2)}, u32[]{:S(2)}) %all-to-all-start.2) | async-done | bytes 1572896 | tf_op jit(solution)/shard_map/all_to_all | solution.py:244
  230.7 1.7 copy.63
  232.4 10.2 %shard_map.85 = f32[16,512,256]{2,1,0:T(8,128)} custom-call(s32[16]{0:T(128)} %copy-done.5, bf16[16,512,192]{2,1,0:T(8,128)(2,1)} %copy.58.basis_ref, bf16[16,192,256]{2,1,0:T(8,128)(2,1)} %bitcast.59, bf16[16,192,256]{2,1,0:T(8,128)(2,1)} %bitcast.58, bf16[16,512,256]{2,1,0:T(8,128)(2,1)} %spec_ref.1, f32[1,256]{1,0:T(1,128)} %bitcast.62), custom_call_target="tpu_custom_call" | custom-call | flops 1610612736 | bytes 18874368 | tf_op jit(solution)/shard_map/pallas_call | solution.py:170
  (33 shorter events, 10.0 us)
Async XLA Ops:
  1.0 6.4 %copy-start.5 = (s32[16]{0:T(128)}, s32[16]{0:T(128)S(1)}, u32[]{:S(2)}) copy-start(s32[16]{0:T(128)S(1)} %dynamic_slice.3.wave_ref) | copy-start | bytes 196
  1.1 6.3 %copy-start.4 = (bf16[16,512,192]{1,2,0:T(8,128)(2,1)S(1)}, bf16[16,512,192]{1,2,0:T(8,128)(2,1)}, u32[]{:S(2)}) copy-start(bf16[16,512,192]{1,2,0:T(8,128)(2,1)} %param.9) | copy-start | bytes 9437188
  13.3 78.9 %all-to-all-start = ((bf16[32,12,16,256]{3,2,1,0:T(8,128)(2,1)}), bf16[32,12,16,256]{3,2,1,0:T(8,128)(2,1)}, u32[]{:S(2)}, u32[]{:S(2)}) async-start(bf16[32,12,16,256]{3,2,1,0:T(8,128)(2,1)} %bitcast.8), calls=%async_computation | async-start | bytes 6291456 | tf_op jit(solution)/shard_map/all_to_all | solution.py:220
  111.0 11.1 %all-to-all-start.1 = ((f32[32,1,128]{2,1,0:T(1,128)}), f32[32,1,128]{2,1,0:T(1,128)S(1)}, u32[]{:S(2)}, u32[]{:S(2)}) async-start(f32[32,1,128]{2,1,0:T(1,128)} %broadcast_in_dim.70), calls=%async_computation.1 | async-start | bytes 32768 | tf_op jit(solution)/shard_map/all_to_all | solution.py:227
  115.1 7.0 %copy-start.6 = (f32[128]{0:T(128)S(1)}, f32[128]{0:T(128)}, u32[]{:S(2)}) copy-start(f32[128]{0:T(128)} %param.14) | copy-start | bytes 1540
  115.1 7.0 %copy-start.1 = (bf16[128,1024]{1,0:T(8,128)(2,1)S(1)}, bf16[128,1024]{1,0:T(8,128)(2,1)}, u32[]{:S(2)}) copy-start(bf16[128,1024]{1,0:T(8,128)(2,1)} %in_w_ref.3) | copy-start | bytes 786436
  115.1 7.0 %copy-start.2 = (bf16[1024,128]{1,0:T(8,128)(2,1)S(1)}, bf16[1024,128]{1,0:T(8,128)(2,1)}, u32[]{:S(2)}) copy-start(bf16[1024,128]{1,0:T(8,128)(2,1)} %out_w_ref.3) | copy-start | bytes 786436
  115.1 7.0 %copy-start.3 = (f32[1024]{0:T(1024)S(1)}, f32[1024]{0:T(1024)}, u32[]{:S(2)}) copy-start(f32[1024]{0:T(1024)} %param.12) | copy-start | bytes 12292
  122.1 1.7 copy-start
  148.1 41.3 %all-to-all-start.3 = ((bf16[6,32,16,256]{3,2,0,1:T(8,128)(2,1)}), bf16[6,32,16,256]{3,2,0,1:T(8,128)(2,1)}, u32[]{:S(2)}, u32[]{:S(2)}) async-start(bf16[6,32,16,256]{3,2,0,1:T(8,128)(2,1)} %copy.56), calls=%async_computation.3 | async-start | bytes 3145728 | tf_op jit(solution)/shard_map/all_to_all | solution.py:244
  189.4 41.3 %all-to-all-start.2 = ((bf16[6,32,16,256]{3,2,0,1:T(8,128)(2,1)}), bf16[6,32,16,256]{3,2,0,1:T(8,128)(2,1)S(1)}, u32[]{:S(2)}, u32[]{:S(2)}) async-start(bf16[6,32,16,256]{3,2,0,1:T(8,128)(2,1)} %copy.54), calls=%async_computation.2 | async-start | bytes 3145728 | tf_op jit(solution)/shard_map/all_to_all | solution.py:244
  192.9 6.0 %copy-start.7 = (f32[128]{0:T(128)S(1)}, f32[128]{0:T(128)}, u32[]{:S(2)}) copy-start(f32[128]{0:T(128)} %param.15) | copy-start | bytes 1540

commit v6 on v5

--- a/solution.py
+++ b/solution.py
@@ -37,7 +37,9 @@
 def grid_kernel(weight_ref, rows_ref, cos_t_ref, sin_t_ref, grid_ref, ssq_ref):
     j = pl.program_id(0)
     chan = grid_ref.shape[2]
-    rows = rows_ref[0]
+    sources, _, rows_per, width = rows_ref.shape
+    rows = rows_ref[:, 0].astype(jnp.float32).reshape(sources * rows_per, width)
+    rows = rows.astype(jnp.bfloat16)
     wide = jnp.dot(cos_t_ref[...], rows[:, :chan], preferred_element_type=jnp.float32)
     wide = wide + jnp.dot(sin_t_ref[...], rows[:, chan:], preferred_element_type=jnp.float32)
     grid = wide.astype(jnp.bfloat16)
@@ -55,7 +57,8 @@
 
 
 def grid_synthesis(lat_w, rows_in, cos_t, neg_sin_t):
-    lat_local, waves, width = rows_in.shape
+    sources, lat_local, rows_per, width = rows_in.shape
+    waves = sources * rows_per
     chan = width // 2
     nlon = cos_t.shape[0]
     return pl.pallas_call(
@@ -63,7 +66,7 @@
         grid=(lat_local,),
         in_specs=[
             pl.BlockSpec(memory_space=pltpu.SMEM),
-            pl.BlockSpec((1, waves, width), lambda j: (j, 0, 0)),
+            pl.BlockSpec((sources, 1, rows_per, width), lambda j: (0, j, 0, 0)),
             pl.BlockSpec((nlon, waves), lambda j: (0, 0)),
             pl.BlockSpec((nlon, waves), lambda j: (0, 0)),
         ],
@@ -84,8 +87,10 @@
     )(lat_w, rows_in, cos_t, neg_sin_t)
 
 
-def column_kernel(weight_ref, grid_ref, scale_ref, in_w_ref, bias_ref, out_w_ref, table_ref, o_ref):
-    j = pl.program_id(0)
+def column_kernel(
+    weight_ref, grid_ref, scale_ref, in_w_ref, bias_ref, out_w_ref, table_ref, o_ref, *, first
+):
+    j = pl.program_id(0) + first
     chan = grid_ref.shape[2]
     waves = table_ref.shape[0] // 2
     scale = scale_ref[...]
@@ -110,17 +115,19 @@
     o_ref[0, :, chan:] = (w * sin_part).astype(jnp.bfloat16)
 
 
-def column_network(lat_w, grid_t, col_scale, in_weight, in_bias, out_weight, wave_table):
-    lat_local, nlon, chan = grid_t.shape
+def column_network(
+    lat_w, grid_t, first, lat_local, col_scale, in_weight, in_bias, out_weight, wave_table
+):
+    nlon, chan = grid_t.shape[1:]
     hid = in_weight.shape[1]
     two_waves = wave_table.shape[0]
     full = lambda shape: pl.BlockSpec(shape, lambda j: (0,) * len(shape))
     return pl.pallas_call(
-        column_kernel,
+        functools.partial(column_kernel, first=first),
         grid=(lat_local,),
         in_specs=[
             pl.BlockSpec(memory_space=pltpu.SMEM),
-            pl.BlockSpec((1, nlon, chan), lambda j: (j, 0, 0)),
+            pl.BlockSpec((1, nlon, chan), lambda j: (j + first, 0, 0)),
             full((1, chan)),
             full((chan, hid)),
             full((1, hid)),
@@ -217,7 +224,7 @@
     outbound = fourier.reshape(2, devices, half_local, row_count, chan_width).transpose(
         1, 0, 2, 3, 4
     ).reshape(devices, 2 * half_local, row_count, chan_width)
-    rows_in = lax.all_to_all(outbound, "lat", split_axis=0, concat_axis=2, tiled=True)[0]
+    rows_in = lax.all_to_all(outbound, "lat", split_axis=0, concat_axis=0, tiled=True)
     j_ids = my_index * half_local + jnp.arange(half_local, dtype=jnp.int32)
     lat_ids = jnp.concatenate([j_ids, lat_total - 1 - j_ids])
     weight_own = lat_weights_of(lat_ids, lat_total)
@@ -231,21 +238,20 @@
     weight_all = lat_weights_of(jnp.arange(lat_total, dtype=jnp.int32), lat_total)
     variance = global_sum / (NLON * jnp.sum(weight_all))
     col_scale = col_gain * lax.rsqrt(variance + 1e-05)
-    grid_north = grid_t[:half_local]
-    grid_south = grid_t[half_local:]
-    weight_north = weight_own[:half_local]
-    weight_south = weight_own[half_local:]
-
-    def to_spectral(grid_field, weight):
+    lat_local = 2 * half_local
+    lead = lat_local // 3
+
+    def to_spectral(first, count):
         weighted_local = column_network(
-            weight, grid_field, col_scale, in_weight, in_bias, out_weight, wave_table
+            weight_own, grid_t, first, count, col_scale, in_weight, in_bias, out_weight, wave_table
         )
-        returning = weighted_local.reshape(half_local, devices, row_count, chan_width)
-        weighted = lax.all_to_all(returning, "lat", split_axis=1, concat_axis=0, tiled=True)
-        return weighted.reshape(half_lat, row_count, chan_width).transpose(1, 0, 2)
-
-    north = to_spectral(grid_north, weight_north)
-    south = to_spectral(grid_south, weight_south)
+        returning = weighted_local.reshape(count, devices, row_count, chan_width)
+        return lax.all_to_all(returning, "lat", split_axis=1, concat_axis=1, tiled=True)
+
+    weighted = jnp.concatenate([to_spectral(0, lead), to_spectral(lead, lat_local - lead)], axis=0)
+    weighted = weighted.reshape(2, half_local, devices, row_count, chan_width)
+    north = weighted[0].transpose(2, 1, 0, 3).reshape(row_count, half_lat, chan_width)
+    south = weighted[1].transpose(2, 1, 0, 3).reshape(row_count, half_lat, chan_width)
     factor = 2.0 * math.sqrt(degrees * wave_total / lat_total)
     damp_all = jnp.concatenate([damping, damping])
     return inverse_legendre(wave_own, lat_basis, north, south, spectral, damp_all, factor)

time: 244 us -> 242 us (level)
  local copies, waits for them, and re-layouts: 30.3 us -> 20.8 us
  waiting for transfers between devices: 79.6 us -> 86.4 us
    all_to_all x3, waiting for transfers between devices: 76.9 us -> 82.8 us  [the longest x2 42.4 us: to_spectral(): lax.all_to_all(returning, 'lat', split_axis=1, concat_axis=1, tiled=True)]
    slice x2 -> x0, local copies, waits for them, and re-layouts: 4.27 us -> none  [the longest x1 4.19 us: on_device(): grid_south = grid_t[half_local:]]
    all_to_all x1 -> x0, local copies, waits for them, and re-layouts: 3.93 us -> none  [on_device(): lax.all_to_all(outbound, 'lat', split_axis=0, concat_axis=2, tiled=True)[0]]
  transfers between devices with their start and end apart: 4 -> 4, of which waited for: 4 -> 3; matrix products, arithmetic and copies ran while one was open for 21% -> 17% of each run, Pallas kernels for 9% -> 12%
where the time goes in v6:
time: 242 us; the launch traced here: 241 us
  waiting for transfers between devices  86.4 us (36%)
  Pallas kernels  69.3 us (29%)
  other arithmetic  40.7 us (17%)
  local copies, waits for them, and re-layouts  20.8 us (9%)
  starting transfers between devices  20.5 us (8%)
    pallas_call x2, Pallas kernels, column_network(): pl.pallas_call(functools.partial(column_kernel, first=first), grid=(lat_l...  44.7 us
    all_to_all x2, waiting for transfers between devices, to_spectral(): lax.all_to_all(returning, 'lat', split_axis=1, concat_axis=1, tiled=True)  42.4 us
    all_to_all x1, waiting for transfers between devices, on_device(): lax.all_to_all(outbound, 'lat', split_axis=0, concat_axis=0, tiled=True)  40.4 us
    slice x1, other arithmetic, on_device(): cos_t = wave_table[:wave_total].T  15 us
    pallas_call x1, Pallas kernels, grid_synthesis(): pl.pallas_call(grid_kernel, grid=(lat_local,), in_specs=[pl.BlockSpec(mem...  14.4 us
    neg x1, other arithmetic, on_device(): neg_sin_t = -wave_table[wave_total:].T  13.4 us
    pallas_call x1, Pallas kernels, inverse_legendre(): pl.pallas_call(functools.partial(inverse_kernel, factor=factor), grid=(ro...  10.2 us
    all_to_all x2, starting transfers between devices, to_spectral(): lax.all_to_all(returning, 'lat', split_axis=1, concat_axis=1, tiled=True)  9.15 us
  transfers between devices with their start and end apart: 4, of which 3 were waited for; matrix products, arithmetic and copies ran while one was open for 17% of the time, Pallas kernels for 12%

profile of v6, /device:TPU:0, one launch (start us, length us, event | category | flops | bytes accessed | tf_op | source)
XLA Modules:
  0.0 240.7 jit_solution(2335395317023959505)
XLA Ops:
  1.1 6.2 %fusion.5 = (bf16[1,16,512,256]{3,2,0,1:T(8,128)(2,1)S(1)}, bf16[1,16,512,256]{3,2,0,1:T(8,128)(2,1)S(1)}) fusion(bf16[16,512,256]{2,1,0:T(8,128)(2,1)} %spec_ref.1, pred[16,512]{1,0:T(8,128)(4,1)S(1)} %get-tuple-element.16, pred[16,512]{1,0:T(8,128)(4,1)S(1)} %get-tuple-element.17), kind=kLoop, calls=%fused_computation.8 | loop fusion | flops 6291456 | bytes 12599296 | tf_op jit(solution)/shard_map/stack | solution.py:220
  7.4 2.1 convert_bitcast_fusion
  9.5 1.8 copy.37
  11.3 2.0 copy.38
  13.3 7.4 %all-to-all-start = ((bf16[32,12,16,256]{3,2,1,0:T(8,128)(2,1)}), bf16[32,12,16,256]{3,2,1,0:T(8,128)(2,1)}, u32[]{:S(2)}, u32[]{:S(2)}) async-start(bf16[32,12,16,256]{3,2,1,0:T(8,128)(2,1)} %bitcast.8), calls=%async_computation | async-start | bytes 6291456 | tf_op jit(solution)/shard_map/all_to_all | solution.py:227
  20.7 15.0 %cosine_convert_fusion = (bf16[512,1536]{1,0:T(8,128)(2,1)}, bf16[1536,512]{0,1:T(8,128)(2,1)S(1)}, bf16[512,1536]{1,0:T(8,128)(2,1)}) fusion(s32[512]{0:T(512)S(1)} %fusion.26), kind=kLoop, calls=%fused_computation.14 | loop fusion | flops 8650752 | bytes 4720640 | tf_op jit(solution)/shard_map/slice | solution.py:231
  36.4 13.4 %negate_bitcast_fusion = bf16[1536,512]{0,1:T(8,128)(2,1)} fusion(s32[512]{0:T(512)S(1)} %fusion.26), kind=kLoop, calls=%fused_computation.21 | loop fusion | flops 10223616 | bytes 1574912 | tf_op jit(solution)/shard_map/neg | solution.py:232
  49.8 1.7 copy.40.sin_t_ref
  51.7 40.4 %all-to-all-done.rows_ref = bf16[32,12,16,256]{3,2,1,0:T(8,128)(2,1)} async-done(((bf16[32,12,16,256]{3,2,1,0:T(8,128)(2,1)}), bf16[32,12,16,256]{3,2,1,0:T(8,128)(2,1)}, u32[]{:S(2)}, u32[]{:S(2)}) %all-to-all-start) | async-done | bytes 3145760 | tf_op jit(solution)/shard_map/all_to_all | solution.py:227
  92.1 14.4 %shard_map.82 = (bf16[12,1536,128]{2,1,0:T(8,128)(2,1)}, f32[1,128]{1,0:T(1,128)S(1)}) custom-call(f32[12]{0:T(128)S(1)} %multiply_cosine_fusion.weight_ref, bf16[32,12,16,256]{3,2,1,0:T(8,128)(2,1)} %all-to-all-done.rows_ref, bf16[1536,512]{1,0:T(8,128)(2,1)S(1)} %copy.39.cos_t_ref, bf16[1536,512]{1,0:T(8,128)(2,1)S(1)} %copy.40.sin_t_ref), custom_call_target="tpu_custom_call" | custom-call | flops 4831838208 | bytes 11010048 | tf_op jit(solution)/shard_map/pallas_call | solution.py:64
  107.1 3.9 %all-to-all-start.1 = ((f32[32,1,128]{2,1,0:T(1,128)}), f32[32,1,128]{2,1,0:T(1,128)S(1)}, u32[]{:S(2)}, u32[]{:S(2)}) async-start(f32[32,1,128]{2,1,0:T(1,128)} %broadcast_in_dim.70), calls=%async_computation.1 | async-start | bytes 32768 | tf_op jit(solution)/shard_map/all_to_all | solution.py:234
  111.1 2.1 pad_maximum_fusion.table_ref
  114.6 3.7 %all-to-all-done.1 = f32[32,1,128]{2,1,0:T(1,128)S(1)} async-done(((f32[32,1,128]{2,1,0:T(1,128)}), f32[32,1,128]{2,1,0:T(1,128)S(1)}, u32[]{:S(2)}, u32[]{:S(2)}) %all-to-all-start.1) | async-done | bytes 16416 | tf_op jit(solution)/shard_map/all_to_all | solution.py:234
  119.2 15.2 %shard_map.83 = bf16[4,512,256]{2,1,0:T(8,128)(2,1)S(1)} custom-call(f32[12]{0:T(128)S(1)} %multiply_cosine_fusion.weight_ref, bf16[12,1536,128]{2,1,0:T(8,128)(2,1)} %get-tuple-element.7.grid_ref, f32[1,128]{1,0:T(1,128)S(1)} %multiply_bitcast_fusion.scale_ref, bf16[128,1024]{1,0:T(8,128)(2,1)S(1)} %copy-done, f32[1,1024]{1,0:T(1,128)S(1)} %bitcast.40, ...), custom_call_target="tpu_custom_call" | custom-call | flops 4831838208 | bytes 5767168 | tf_op jit(solution)/shard_map/pallas_call | solution.py:125
  135.6 3.6 %all-to-all-start.2 = ((bf16[4,32,16,256]{3,2,0,1:T(8,128)(2,1)}), bf16[4,32,16,256]{3,2,0,1:T(8,128)(2,1)}, u32[]{:S(2)}, u32[]{:S(2)}) async-start(bf16[4,32,16,256]{3,2,0,1:T(8,128)(2,1)} %copy.42), calls=%async_computation.2 | async-start | bytes 2097152 | tf_op jit(solution)/shard_map/all_to_all | solution.py:249
  140.1 29.4 %shard_map.84 = bf16[8,512,256]{2,1,0:T(8,128)(2,1)S(1)} custom-call(f32[12]{0:T(128)S(1)} %multiply_cosine_fusion.weight_ref, bf16[12,1536,128]{2,1,0:T(8,128)(2,1)} %get-tuple-element.7.grid_ref, f32[1,128]{1,0:T(1,128)S(1)} %multiply_bitcast_fusion.scale_ref, bf16[128,1024]{1,0:T(8,128)(2,1)S(1)} %copy-done, f32[1,1024]{1,0:T(1,128)S(1)} %bitcast.41, ...), custom_call_target="tpu_custom_call" | custom-call | flops 9663676416 | bytes 8388608 | tf_op jit(solution)/shard_map/pallas_call | solution.py:125
  169.5 1.6 copy.43
  171.1 5.6 %all-to-all-start.3 = ((bf16[8,32,16,256]{3,2,0,1:T(8,128)(2,1)}), bf16[8,32,16,256]{3,2,0,1:T(8,128)(2,1)S(1)}, u32[]{:S(2)}, u32[]{:S(2)}) async-start(bf16[8,32,16,256]{3,2,0,1:T(8,128)(2,1)} %copy.43), calls=%async_computation.3 | async-start | bytes 4194304 | tf_op jit(solution)/shard_map/all_to_all | solution.py:249
  176.7 5.9 %copy.44.basis_ref = bf16[16,512,192]{2,1,0:T(8,128)(2,1)} copy(bf16[16,512,192]{1,2,0:T(8,128)(2,1)} %param.9) | data formatting | bytes 6291456 | tf_op args[1]
  183.3 42.4 %all-to-all-done.3 = bf16[8,32,16,256]{3,2,0,1:T(8,128)(2,1)S(1)} async-done(((bf16[8,32,16,256]{3,2,0,1:T(8,128)(2,1)}), bf16[8,32,16,256]{3,2,0,1:T(8,128)(2,1)S(1)}, u32[]{:S(2)}, u32[]{:S(2)}) %all-to-all-start.3) | async-done | bytes 2097184 | tf_op jit(solution)/shard_map/all_to_all | solution.py:249
  225.6 1.5 fusion.33
  227.1 1.7 copy.45.north_ref
  228.8 1.7 copy.46.south_ref
  230.5 10.2 %shard_map.85 = f32[16,512,256]{2,1,0:T(8,128)} custom-call(s32[16]{0:T(128)} %copy-done.5, bf16[16,512,192]{2,1,0:T(8,128)(2,1)} %copy.44.basis_ref, bf16[16,192,256]{2,1,0:T(8,128)(2,1)} %copy.45.north_ref, bf16[16,192,256]{2,1,0:T(8,128)(2,1)} %copy.46.south_ref, bf16[16,512,256]{2,1,0:T(8,128)(2,1)} %spec_ref.1, f32[1,256]{1,0:T(1,128)} %bitcast.46), custom_call_target="tpu_custom_call" | custom-call | flops 1610612736 | bytes 18874368 | tf_op jit(solution)/shard_map/pallas_call | solution.py:177
  (31 shorter events, 6.9 us)
Async XLA Ops:
  1.0 6.4 %copy-start.5 = (s32[16]{0:T(128)}, s32[16]{0:T(128)S(1)}, u32[]{:S(2)}) copy-start(s32[16]{0:T(128)S(1)} %dynamic_slice.3.wave_ref) | copy-start | bytes 196
  1.1 6.3 %copy-start.4 = (bf16[16,512,192]{1,2,0:T(8,128)(2,1)S(1)}, bf16[16,512,192]{1,2,0:T(8,128)(2,1)}, u32[]{:S(2)}) copy-start(bf16[16,512,192]{1,2,0:T(8,128)(2,1)} %param.9) | copy-start | bytes 9437188
  13.3 78.9 %all-to-all-start = ((bf16[32,12,16,256]{3,2,1,0:T(8,128)(2,1)}), bf16[32,12,16,256]{3,2,1,0:T(8,128)(2,1)}, u32[]{:S(2)}, u32[]{:S(2)}) async-start(bf16[32,12,16,256]{3,2,1,0:T(8,128)(2,1)} %bitcast.8), calls=%async_computation | async-start | bytes 6291456 | tf_op jit(solution)/shard_map/all_to_all | solution.py:227
  107.1 11.1 %all-to-all-start.1 = ((f32[32,1,128]{2,1,0:T(1,128)}), f32[32,1,128]{2,1,0:T(1,128)S(1)}, u32[]{:S(2)}, u32[]{:S(2)}) async-start(f32[32,1,128]{2,1,0:T(1,128)} %broadcast_in_dim.70), calls=%async_computation.1 | async-start | bytes 32768 | tf_op jit(solution)/shard_map/all_to_all | solution.py:234
  111.1 7.2 %copy-start.6 = (f32[128]{0:T(128)S(1)}, f32[128]{0:T(128)}, u32[]{:S(2)}) copy-start(f32[128]{0:T(128)} %param.14) | copy-start | bytes 1540
  111.1 7.2 %copy-start = (bf16[128,1024]{1,0:T(8,128)(2,1)S(1)}, bf16[128,1024]{1,0:T(8,128)(2,1)}, u32[]{:S(2)}) copy-start(bf16[128,1024]{1,0:T(8,128)(2,1)} %in_w_ref.3) | copy-start | bytes 786436
  111.1 7.2 %copy-start.3 = (f32[1024]{0:T(1024)S(1)}, f32[1024]{0:T(1024)}, u32[]{:S(2)}) copy-start(f32[1024]{0:T(1024)} %param.12) | copy-start | bytes 12292
  118.3 1.0 copy-start.1
  135.6 35.6 %all-to-all-start.2 = ((bf16[4,32,16,256]{3,2,0,1:T(8,128)(2,1)}), bf16[4,32,16,256]{3,2,0,1:T(8,128)(2,1)}, u32[]{:S(2)}, u32[]{:S(2)}) async-start(bf16[4,32,16,256]{3,2,0,1:T(8,128)(2,1)} %copy.42), calls=%async_computation.2 | async-start | bytes 2097152 | tf_op jit(solution)/shard_map/all_to_all | solution.py:249
  139.1 1.0 copy-start.2
  171.1 54.5 %all-to-all-start.3 = ((bf16[8,32,16,256]{3,2,0,1:T(8,128)(2,1)}), bf16[8,32,16,256]{3,2,0,1:T(8,128)(2,1)S(1)}, u32[]{:S(2)}, u32[]{:S(2)}) async-start(bf16[8,32,16,256]{3,2,0,1:T(8,128)(2,1)} %copy.43), calls=%async_computation.3 | async-start | bytes 4194304 | tf_op jit(solution)/shard_map/all_to_all | solution.py:249
  176.7 5.9 %copy-start.7 = (f32[128]{0:T(128)S(1)}, f32[128]{0:T(128)}, u32[]{:S(2)}) copy-start(f32[128]{0:T(128)} %param.15) | copy-start | bytes 1540

commit v7 on v4

--- a/solution.py
+++ b/solution.py
@@ -34,26 +34,40 @@
     return jnp.cos(math.pi * ((latitude + 0.5) / lat_total - 0.5))
 
 
-def column_kernel(weight_ref, grid_ref, scale_ref, in_t_ref, bias_ref, out_t_ref, table_ref, o_ref):
+def column_kernel(
+    weight_ref, rows_ref, scale_ref, in_w_ref, bias_ref, out_w_ref,
+    table_ref, o_ref,
+):
     j = pl.program_id(0)
-    chan = grid_ref.shape[1]
+    sources, _, rows_per, width = rows_ref.shape
+    chan = width // 2
     waves = table_ref.shape[0] // 2
+    rows = rows_ref[:, 0].astype(jnp.float32).reshape(sources * rows_per, width)
+    rows = rows.astype(jnp.bfloat16)
+    real = rows[:, :chan]
+    imag = rows[:, chan:]
     scale = scale_ref[...]
     acc = jnp.zeros((2 * waves, chan), jnp.float32)
     for c in range(NLON // LON_TILE):
         lo = c * LON_TILE
-        g = grid_ref[0, :, lo:lo + LON_TILE].astype(jnp.float32)
+        first_dims = (((0,), (0,)), ((), ()))
+        wide = lax.dot_general(
+            table_ref[:waves, lo:lo + LON_TILE], real, first_dims,
+            preferred_element_type=jnp.float32,
+        )
+        wide = wide - lax.dot_general(
+            table_ref[waves:, lo:lo + LON_TILE], imag, first_dims,
+            preferred_element_type=jnp.float32,
+        )
+        g = wide.astype(jnp.bfloat16).astype(jnp.float32)
         normed = (g * scale).astype(jnp.bfloat16)
-        pre = jnp.dot(in_t_ref[...], normed, preferred_element_type=jnp.float32) + bias_ref[...]
+        pre = jnp.dot(normed, in_w_ref[...], preferred_element_type=jnp.float32) + bias_ref[...]
         hidden = jax.nn.gelu(pre).astype(jnp.bfloat16)
-        col = jnp.dot(out_t_ref[...], hidden, preferred_element_type=jnp.float32).astype(
+        col = jnp.dot(hidden, out_w_ref[...], preferred_element_type=jnp.float32).astype(
             jnp.bfloat16
         )
-        acc = acc + lax.dot_general(
-            table_ref[:, lo:lo + LON_TILE],
-            col,
-            (((1,), (1,)), ((), ())),
-            preferred_element_type=jnp.float32,
+        acc = acc + jnp.dot(
+            table_ref[:, lo:lo + LON_TILE], col, preferred_element_type=jnp.float32
         )
     inv_root = 1.0 / math.sqrt(NLON)
     w = weight_ref[j]
@@ -63,8 +77,13 @@
     o_ref[0, :, chan:] = (w * sin_part).astype(jnp.bfloat16)
 
 
-def column_network(lat_w, grid_field, col_scale, in_weight, in_bias, out_weight, wave_table):
-    lat_local, chan, nlon = grid_field.shape
+def column_network(
+    lat_w, rows_in, col_scale, in_weight, in_bias, out_weight, wave_table
+):
+    sources, lat_local, rows_per, width = rows_in.shape
+    chan = width // 2
+    waves = sources * rows_per
+    nlon = wave_table.shape[1]
     hid = in_weight.shape[1]
     two_waves = wave_table.shape[0]
     full = lambda shape: pl.BlockSpec(shape, lambda j: (0,) * len(shape))
@@ -73,28 +92,28 @@
         grid=(lat_local,),
         in_specs=[
             pl.BlockSpec(memory_space=pltpu.SMEM),
-            pl.BlockSpec((1, chan, nlon), lambda j: (j, 0, 0)),
-            full((chan, 1)),
+            pl.BlockSpec((sources, 1, rows_per, width), lambda j: (0, j, 0, 0)),
+            full((1, chan)),
+            full((chan, hid)),
+            full((1, hid)),
             full((hid, chan)),
-            full((hid, 1)),
-            full((chan, hid)),
             full((two_waves, nlon)),
         ],
         out_specs=pl.BlockSpec((1, two_waves // 2, 2 * chan), lambda j: (j, 0, 0)),
         out_shape=jax.ShapeDtypeStruct((lat_local, two_waves // 2, 2 * chan), jnp.bfloat16),
         compiler_params=pltpu.CompilerParams(vmem_limit_bytes=48 * 1024 * 1024),
         cost_estimate=pl.CostEstimate(
-            flops=2 * lat_local * nlon * (2 * hid * chan + two_waves * chan),
+            flops=2 * lat_local * nlon * (2 * hid * chan + two_waves * chan + waves * width),
             transcendentals=lat_local * nlon * hid,
-            bytes_accessed=two_waves * nlon * 2 + lat_local * (chan * nlon * 2 + two_waves * chan * 2),
+            bytes_accessed=2 * two_waves * nlon + lat_local * (waves * width * 2 + two_waves * chan * 2),
         ),
     )(
         lat_w,
-        grid_field,
-        col_scale[:, None],
-        in_weight.T,
-        in_bias[:, None],
-        out_weight.T,
+        rows_in,
+        col_scale[None, :],
+        in_weight,
+        in_bias[None, :],
+        out_weight,
         wave_table,
     )
 
@@ -162,48 +181,48 @@
     masked = jnp.where(inside[:, :, None], spectral, jnp.zeros_like(spectral))
     flipped = jnp.where(parity[:, :, None] > 0, masked, -masked)
     wave_table = lon_table(wave_all)
-
-    both = jnp.stack([masked, flipped], axis=0)
-    fourier = jnp.einsum(
-        "rnj,srnc->sjrc", lat_basis, both, preferred_element_type=jnp.float32
-    ).astype(jnp.bfloat16)
-    outbound = fourier.reshape(2, devices, half_local, row_count, chan_width).transpose(
-        1, 0, 2, 3, 4
-    ).reshape(devices, 2 * half_local, row_count, chan_width)
-    rows_in = lax.all_to_all(outbound, "lat", split_axis=0, concat_axis=2, tiled=True)[0]
-    signed = jnp.concatenate([rows_in[:, :, :chan_count], -rows_in[:, :, chan_count:]], axis=1)
-    grid_field = jnp.einsum(
-        "jrk,rl->jkl", signed, wave_table, preferred_element_type=jnp.float32
-    ).astype(jnp.bfloat16)
-    grid_north = grid_field[:half_local]
-    grid_south = grid_field[half_local:]
     j_ids = my_index * half_local + jnp.arange(half_local, dtype=jnp.int32)
     weight_north = lat_weights_of(j_ids, lat_total)
     weight_south = lat_weights_of(lat_total - 1 - j_ids, lat_total)
-
-    def sum_squares(grid_field, weight):
-        grid_wide = grid_field.astype(jnp.float32)
-        return jnp.sum(weight[:, None, None] * grid_wide * grid_wide, axis=(0, 2))
-
-    partial_value = sum_squares(grid_north, weight_north) + sum_squares(grid_south, weight_south)
+    j_all = jnp.arange(half_lat, dtype=jnp.int32)
+    weight_all = lat_weights_of(jnp.arange(lat_total, dtype=jnp.int32), lat_total)
+    real_coef = jnp.where(wave_own == 0, float(NLON), NLON / 2.0)
+    imag_coef = jnp.where(wave_own == 0, 0.0, NLON / 2.0)
+
+    def hemisphere(values, lat_weight):
+        fourier = jnp.einsum(
+            "rnj,rnc->jrc", lat_basis, values, preferred_element_type=jnp.float32
+        ).astype(jnp.bfloat16)
+        wide = fourier.astype(jnp.float32)
+        per_lat = jnp.sum(
+            real_coef[None, :, None] * wide[:, :, :chan_count] ** 2
+            + imag_coef[None, :, None] * wide[:, :, chan_count:] ** 2,
+            axis=1,
+        )
+        part = jnp.sum(lat_weight[:, None] * per_lat, axis=0)
+        return fourier.reshape(devices, half_local, row_count, chan_width), part
+
+    out_north, part_north = hemisphere(masked, lat_weights_of(j_all, lat_total))
+    out_south, part_south = hemisphere(flipped, lat_weights_of(lat_total - 1 - j_all, lat_total))
+    partial_value = part_north + part_south
     gathered = lax.all_to_all(
         jnp.broadcast_to(partial_value[None], (devices, chan_count)), "lat", 0, 0, tiled=True
     )
     global_sum = jnp.sum(gathered, axis=0)
-    weight_all = lat_weights_of(jnp.arange(lat_total, dtype=jnp.int32), lat_total)
     variance = global_sum / (NLON * jnp.sum(weight_all))
     col_scale = col_gain * lax.rsqrt(variance + 1e-05)
 
-    def to_spectral(grid_field, weight):
+    def round_trip(outbound, lat_weight):
+        rows_in = lax.all_to_all(outbound, "lat", split_axis=0, concat_axis=0, tiled=True)
         weighted_local = column_network(
-            weight, grid_field, col_scale, in_weight, in_bias, out_weight, wave_table
+            lat_weight, rows_in, col_scale, in_weight, in_bias, out_weight, wave_table
         )
         returning = weighted_local.reshape(half_local, devices, row_count, chan_width)
-        weighted = lax.all_to_all(returning, "lat", split_axis=1, concat_axis=0, tiled=True)
-        return weighted.reshape(half_lat, row_count, chan_width).transpose(1, 0, 2)
-
-    north = to_spectral(grid_north, weight_north)
-    south = to_spectral(grid_south, weight_south)
+        back = lax.all_to_all(returning, "lat", split_axis=1, concat_axis=1, tiled=True)
+        return back.transpose(2, 1, 0, 3).reshape(row_count, half_lat, chan_width)
+
+    north = round_trip(out_north, weight_north)
+    south = round_trip(out_south, weight_south)
     factor = 2.0 * math.sqrt(degrees * wave_total / lat_total)
     damp_all = jnp.concatenate([damping, damping])
     return inverse_legendre(wave_own, lat_basis, north, south, spectral, damp_all, factor)

time: 248 us -> 221 us (0.89)
  waiting for transfers between devices: 95.5 us -> 73.9 us
  local copies, waits for them, and re-layouts: 37.5 us -> 19.9 us
  Pallas kernels: 58.7 us -> 72.7 us
  other arithmetic: 26.8 us -> 18.7 us
  starting transfers between devices: 18.5 us -> 23.4 us
    all_to_all x3 -> x4, waiting for transfers between devices: 92.8 us -> 68.8 us  [the longest x2 35.8 us: round_trip(): lax.all_to_all(outbound, 'lat', split_axis=0, concat_axis=0, tiled=True)]
    pallas_call x2, Pallas kernels: 48.5 us -> 62.5 us  [column_network(): pl.pallas_call(column_kernel, grid=(lat_local,), in_specs=[pl.BlockSpec(m...]
    unnamed x29 -> x19, local copies, waits for them, and re-layouts: 16.2 us -> 7.67 us
    slice x2 -> x0, local copies, waits for them, and re-layouts: 6.81 us -> none  [the longest x1 4.29 us: on_device(): grid_south = grid_field[half_local:]]
    another operation x2 -> x1, other arithmetic: 19.7 us -> 13.5 us
    all_to_all x1, starting transfers between devices: 4.11 us -> 7.28 us  [on_device(): lax.all_to_all(jnp.broadcast_to(partial_value[None], (devices, chan_count...]
    all_to_all x3 -> x4, starting transfers between devices: 14.4 us -> 16.1 us  [the longest x2 9.87 us: round_trip(): lax.all_to_all(returning, 'lat', split_axis=1, concat_axis=1, tiled=True)]
  transfers between devices with their start and end apart: 4 -> 5, of which waited for: 4 -> 4; matrix products, arithmetic and copies ran while one was open for 13% -> 15% of each run, Pallas kernels for 10% -> 28%
where the time goes in v7:
time: 221 us; the launch traced here: 220 us
  waiting for transfers between devices  73.9 us (33%)
  Pallas kernels  72.7 us (33%)
  starting transfers between devices  23.4 us (11%)
  local copies, waits for them, and re-layouts  19.9 us (9%)
  other arithmetic  18.7 us (8%)
  matrix products  10.9 us (5%)
    pallas_call x2, Pallas kernels, column_network(): pl.pallas_call(column_kernel, grid=(lat_local,), in_specs=[pl.BlockSpec(m...  62.5 us
    all_to_all x2, waiting for transfers between devices, round_trip(): lax.all_to_all(outbound, 'lat', split_axis=0, concat_axis=0, tiled=True)  35.8 us
    all_to_all x2, waiting for transfers between devices, round_trip(): lax.all_to_all(returning, 'lat', split_axis=1, concat_axis=1, tiled=True)  33 us
    another operation x1, other arithmetic  13.5 us
    dot_general x2, matrix products, hemisphere(): jnp.einsum('rnj,rnc->jrc', lat_basis, values, preferred_element_type=jnp....  10.9 us
    pallas_call x1, Pallas kernels, inverse_legendre(): pl.pallas_call(functools.partial(inverse_kernel, factor=factor), grid=(ro...  10.2 us
    all_to_all x2, starting transfers between devices, round_trip(): lax.all_to_all(returning, 'lat', split_axis=1, concat_axis=1, tiled=True)  9.87 us
    unnamed x19, local copies, waits for them, and re-layouts  7.67 us
  transfers between devices with their start and end apart: 5, of which 4 were waited for; matrix products, arithmetic and copies ran while one was open for 15% of the time, Pallas kernels for 28%

profile of v7, /device:TPU:0, one launch (start us, length us, event | category | flops | bytes accessed | tf_op | source)
XLA Modules:
  0.0 220.3 jit_solution(9419939503536075126)
XLA Ops:
  1.2 4.6 %fusion.38 = (f32[192,16,256]{2,0,1:T(8,128)S(1)}, bf16[192,16,256]{2,0,1:T(8,128)(2,1)S(1)}) fusion(bf16[16,512,192]{1,2,0:T(8,128)(2,1)} %param.9, bf16[16,512,256]{2,1,0:T(8,128)(2,1)} %spec_ref.1, pred[16,512]{1,0:T(8,128)(4,1)S(1)} %get-tuple-element.12), kind=kOutput, calls=%fused_computation.72 | convolution fusion | flops 808976384 | bytes 12066816 | tf_op jit(solution)/shard_map/rnj,rnc->jrc/dot_general | solution.py:193
  6.5 6.3 %fusion.37 = (f32[192,16,256]{2,0,1:T(8,128)S(1)}, bf16[192,16,256]{2,0,1:T(8,128)(2,1)S(1)}) fusion(bf16[16,512,192]{1,2,0:T(8,128)(2,1)S(1)} %copy-done.5, pred[16,512]{1,0:T(8,128)(4,1)S(1)} %get-tuple-element.11, bf16[16,512,256]{2,1,0:T(8,128)(2,1)S(1)} %copy-done.4, pred[16,512]{1,0:T(8,128)(4,1)S(1)} %get-tuple-element.12), kind=kOutput, calls=%fused_computation.71 | convolution fusion | flops 817364992 | bytes 12075008 | tf_op jit(solution)/shard_map/rnj,rnc->jrc/dot_general | solution.py:193
  14.3 7.3 %all-to-all-start.1 = ((f32[32,1,128]{2,1,0:T(1,128)}), f32[32,1,128]{2,1,0:T(1,128)S(1)}, u32[]{:S(2)}, u32[]{:S(2)}) async-start(f32[32,1,128]{2,1,0:T(1,128)} %broadcast_in_dim.92), calls=%async_computation.1 | async-start | bytes 32768 | tf_op jit(solution)/shard_map/all_to_all | solution.py:208
  21.6 2.0 copy.31
  23.6 5.1 %all-to-all-done.1 = f32[32,1,128]{2,1,0:T(1,128)S(1)} async-done(((f32[32,1,128]{2,1,0:T(1,128)}), f32[32,1,128]{2,1,0:T(1,128)S(1)}, u32[]{:S(2)}, u32[]{:S(2)}) %all-to-all-start.1) | async-done | bytes 16416 | tf_op jit(solution)/shard_map/all_to_all | solution.py:208
  28.7 2.7 %all-to-all-start.3 = ((bf16[32,6,16,256]{3,2,1,0:T(8,128)(2,1)}), bf16[32,6,16,256]{3,2,1,0:T(8,128)(2,1)S(1)}, u32[]{:S(2)}, u32[]{:S(2)}) async-start(bf16[32,6,16,256]{3,2,1,0:T(8,128)(2,1)} %bitcast.9), calls=%async_computation.3 | async-start | bytes 3145728 | tf_op jit(solution)/shard_map/all_to_all | solution.py:216
  31.4 2.0 copy.28
  33.4 35.8 %all-to-all-done.3.rows_ref = bf16[32,6,16,256]{3,2,1,0:T(8,128)(2,1)S(1)} async-done(((bf16[32,6,16,256]{3,2,1,0:T(8,128)(2,1)}), bf16[32,6,16,256]{3,2,1,0:T(8,128)(2,1)S(1)}, u32[]{:S(2)}, u32[]{:S(2)}) %all-to-all-start.3) | async-done | bytes 1572896 | tf_op jit(solution)/shard_map/all_to_all | solution.py:216
  69.2 3.6 %all-to-all-start = ((bf16[32,6,16,256]{3,2,1,0:T(8,128)(2,1)}), bf16[32,6,16,256]{3,2,1,0:T(8,128)(2,1)S(1)}, u32[]{:S(2)}, u32[]{:S(2)}) async-start(bf16[32,6,16,256]{3,2,1,0:T(8,128)(2,1)} %bitcast.25), calls=%async_computation | async-start | bytes 3145728 | tf_op jit(solution)/shard_map/all_to_all | solution.py:216
  74.2 13.5 %cosine_convert_fusion = (bf16[512,1536]{1,0:T(8,128)(2,1)S(1)}, bf16[512,1536]{1,0:T(8,128)(2,1)S(1)}) fusion(s32[512]{0:T(512)S(1)} %fusion.31), kind=kLoop, calls=%fused_computation.10 | loop fusion | flops 8650752 | bytes 3147776 | tf_op jit(solution)/shard_map/convert
  87.7 1.9 pad_maximum_fusion.table_ref
  89.7 0.9 copy-done.1
  90.6 31.2 %shard_map.83 = bf16[6,512,256]{2,1,0:T(8,128)(2,1)S(1)} custom-call(f32[6]{0:T(128)S(1)} %multiply_cosine_fusion.2.weight_ref, bf16[32,6,16,256]{3,2,1,0:T(8,128)(2,1)S(1)} %all-to-all-done.3.rows_ref, f32[1,128]{1,0:T(1,128)S(1)} %multiply_bitcast_fusion.scale_ref, bf16[128,1024]{1,0:T(8,128)(2,1)S(1)} %copy-done, f32[1,1024]{1,0:T(1,128)S(1)} %bitcast.23, ...), custom_call_target="tpu_custom_call" | custom-call | flops 9663676416 | bytes 6291456 | tf_op jit(solution)/shard_map/pallas_call | solution.py:90
  121.8 1.4 copy.32
  123.2 6.1 %all-to-all-start.4 = ((bf16[6,32,16,256]{3,2,0,1:T(8,128)(2,1)}), bf16[6,32,16,256]{3,2,0,1:T(8,128)(2,1)}, u32[]{:S(2)}, u32[]{:S(2)}) async-start(bf16[6,32,16,256]{3,2,0,1:T(8,128)(2,1)} %copy.32), calls=%async_computation.4 | async-start | bytes 3145728 | tf_op jit(solution)/shard_map/all_to_all | solution.py:221
  129.4 31.2 %shard_map.82 = bf16[6,512,256]{2,1,0:T(8,128)(2,1)S(1)} custom-call(f32[6]{0:T(128)S(1)} %multiply_cosine_fusion.3.weight_ref, bf16[32,6,16,256]{3,2,1,0:T(8,128)(2,1)S(1)} %all-to-all-done.rows_ref, f32[1,128]{1,0:T(1,128)S(1)} %multiply_bitcast_fusion.scale_ref, bf16[128,1024]{1,0:T(8,128)(2,1)S(1)} %copy-done, f32[1,1024]{1,0:T(1,128)S(1)} %bitcast.24, ...), custom_call_target="tpu_custom_call" | custom-call | flops 9663676416 | bytes 6291456 | tf_op jit(solution)/shard_map/pallas_call | solution.py:90
  160.6 1.4 copy.30
  162.0 4.9 %all-to-all-done.4 = bf16[6,32,16,256]{3,2,0,1:T(8,128)(2,1)} async-done(((bf16[6,32,16,256]{3,2,0,1:T(8,128)(2,1)}), bf16[6,32,16,256]{3,2,0,1:T(8,128)(2,1)}, u32[]{:S(2)}, u32[]{:S(2)}) %all-to-all-start.4) | async-done | bytes 1572896 | tf_op jit(solution)/shard_map/all_to_all | solution.py:221
  166.9 3.7 %all-to-all-start.2 = ((bf16[6,32,16,256]{3,2,0,1:T(8,128)(2,1)}), bf16[6,32,16,256]{3,2,0,1:T(8,128)(2,1)S(1)}, u32[]{:S(2)}, u32[]{:S(2)}) async-start(bf16[6,32,16,256]{3,2,0,1:T(8,128)(2,1)} %copy.30), calls=%async_computation.2 | async-start | bytes 3145728 | tf_op jit(solution)/shard_map/all_to_all | solution.py:221
  170.7 6.0 %copy.33.basis_ref = bf16[16,512,192]{2,1,0:T(8,128)(2,1)} copy(bf16[16,512,192]{1,2,0:T(8,128)(2,1)} %param.9) | data formatting | bytes 6291456 | tf_op args[1]
  177.2 3.1 %copy.35.south_ref = bf16[16,192,256]{2,1,0:T(8,128)(2,1)} copy(bf16[16,192,256]{2,0,1:T(8,128)(2,1)} %bitcast.12) | data formatting | bytes 3145728 | tf_op jit(solution)/shard_map/reshape | solution.py:222
  180.3 28.1 %all-to-all-done.2 = bf16[6,32,16,256]{3,2,0,1:T(8,128)(2,1)S(1)} async-done(((bf16[6,32,16,256]{3,2,0,1:T(8,128)(2,1)}), bf16[6,32,16,256]{3,2,0,1:T(8,128)(2,1)S(1)}, u32[]{:S(2)}, u32[]{:S(2)}) %all-to-all-start.2) | async-done | bytes 1572896 | tf_op jit(solution)/shard_map/all_to_all | solution.py:221
  208.4 1.7 copy.34.north_ref
  210.1 10.2 %shard_map.84 = f32[16,512,256]{2,1,0:T(8,128)} custom-call(s32[16]{0:T(128)} %copy-done.6, bf16[16,512,192]{2,1,0:T(8,128)(2,1)} %copy.33.basis_ref, bf16[16,192,256]{2,1,0:T(8,128)(2,1)} %copy.34.north_ref, bf16[16,192,256]{2,1,0:T(8,128)(2,1)} %copy.35.south_ref, bf16[16,512,256]{2,1,0:T(8,128)(2,1)} %spec_ref.1, f32[1,256]{1,0:T(1,128)} %bitcast.28), custom_call_target="tpu_custom_call" | custom-call | flops 1610612736 | bytes 18874368 | tf_op jit(solution)/shard_map/pallas_call | solution.py:142
  (36 shorter events, 4.7 us)
Async XLA Ops:
  1.0 4.8 %copy-start.6 = (s32[16]{0:T(128)}, s32[16]{0:T(128)S(1)}, u32[]{:S(2)}) copy-start(s32[16]{0:T(128)S(1)} %get-tuple-element.8.wave_ref) | copy-start | bytes 196
  1.2 4.6 %copy-start.4 = (bf16[16,512,256]{2,1,0:T(8,128)(2,1)S(1)}, bf16[16,512,256]{2,1,0:T(8,128)(2,1)}, u32[]{:S(2)}) copy-start(bf16[16,512,256]{2,1,0:T(8,128)(2,1)} %spec_ref.1) | copy-start | bytes 12582916
  1.2 5.3 %copy-start.5 = (bf16[16,512,192]{1,2,0:T(8,128)(2,1)S(1)}, bf16[16,512,192]{1,2,0:T(8,128)(2,1)}, u32[]{:S(2)}) copy-start(bf16[16,512,192]{1,2,0:T(8,128)(2,1)} %param.9) | copy-start | bytes 9437188
  14.3 14.4 %all-to-all-start.1 = ((f32[32,1,128]{2,1,0:T(1,128)}), f32[32,1,128]{2,1,0:T(1,128)S(1)}, u32[]{:S(2)}, u32[]{:S(2)}) async-start(f32[32,1,128]{2,1,0:T(1,128)} %broadcast_in_dim.92), calls=%async_computation.1 | async-start | bytes 32768 | tf_op jit(solution)/shard_map/all_to_all | solution.py:208
  28.7 40.5 %all-to-all-start.3 = ((bf16[32,6,16,256]{3,2,1,0:T(8,128)(2,1)}), bf16[32,6,16,256]{3,2,1,0:T(8,128)(2,1)S(1)}, u32[]{:S(2)}, u32[]{:S(2)}) async-start(bf16[32,6,16,256]{3,2,1,0:T(8,128)(2,1)} %bitcast.9), calls=%async_computation.3 | async-start | bytes 3145728 | tf_op jit(solution)/shard_map/all_to_all | solution.py:216
  69.2 54.0 %all-to-all-start = ((bf16[32,6,16,256]{3,2,1,0:T(8,128)(2,1)}), bf16[32,6,16,256]{3,2,1,0:T(8,128)(2,1)S(1)}, u32[]{:S(2)}, u32[]{:S(2)}) async-start(bf16[32,6,16,256]{3,2,1,0:T(8,128)(2,1)} %bitcast.25), calls=%async_computation | async-start | bytes 3145728 | tf_op jit(solution)/shard_map/all_to_all | solution.py:216
  87.7 1.9 copy-start.7
  87.7 1.9 copy-start
  87.7 1.9 copy-start.3
  89.6 1.0 copy-start.1
  121.8 7.6 %copy-start.2 = (bf16[1024,128]{1,0:T(8,128)(2,1)S(1)}, bf16[1024,128]{1,0:T(8,128)(2,1)}, u32[]{:S(2)}) copy-start(bf16[1024,128]{1,0:T(8,128)(2,1)} %out_w_ref.3) | copy-start | bytes 786436
  123.2 43.7 %all-to-all-start.4 = ((bf16[6,32,16,256]{3,2,0,1:T(8,128)(2,1)}), bf16[6,32,16,256]{3,2,0,1:T(8,128)(2,1)}, u32[]{:S(2)}, u32[]{:S(2)}) async-start(bf16[6,32,16,256]{3,2,0,1:T(8,128)(2,1)} %copy.32), calls=%async_computation.4 | async-start | bytes 3145728 | tf_op jit(solution)/shard_map/all_to_all | solution.py:221
  166.9 41.5 %all-to-all-start.2 = ((bf16[6,32,16,256]{3,2,0,1:T(8,128)(2,1)}), bf16[6,32,16,256]{3,2,0,1:T(8,128)(2,1)S(1)}, u32[]{:S(2)}, u32[]{:S(2)}) async-start(bf16[6,32,16,256]{3,2,0,1:T(8,128)(2,1)} %copy.30), calls=%async_computation.2 | async-start | bytes 3145728 | tf_op jit(solution)/shard_map/all_to_all | solution.py:221
  170.7 6.0 %copy-start.8 = (f32[128]{0:T(128)S(1)}, f32[128]{0:T(128)}, u32[]{:S(2)}) copy-start(f32[128]{0:T(128)} %param.15) | copy-start | bytes 1540

commit v8 on v7

--- a/solution.py
+++ b/solution.py
@@ -222,6 +222,7 @@
         return back.transpose(2, 1, 0, 3).reshape(row_count, half_lat, chan_width)
 
     north = round_trip(out_north, weight_north)
+    out_south, wave_table = lax.optimization_barrier((out_south, wave_table))
     south = round_trip(out_south, weight_south)
     factor = 2.0 * math.sqrt(degrees * wave_total / lat_total)
     damp_all = jnp.concatenate([damping, damping])

time: 221 us -> 220 us (level)
  waiting for transfers between devices: 73.9 us -> 71.3 us
    all_to_all x1, waiting for transfers between devices: 5.13 us -> 0.01 us  [on_device(): lax.all_to_all(jnp.broadcast_to(partial_value[None], (devices, chan_count...]
    all_to_all x2, starting transfers between devices: 6.24 us -> 9.61 us  [round_trip(): lax.all_to_all(outbound, 'lat', split_axis=0, concat_axis=0, tiled=True)]
    all_to_all x2, waiting for transfers between devices: 35.8 us -> 38.4 us  [round_trip(): lax.all_to_all(outbound, 'lat', split_axis=0, concat_axis=0, tiled=True)]
  transfers between devices with their start and end apart: 5 -> 5, of which waited for: 4 -> 4; matrix products, arithmetic and copies ran while one was open for 15% -> 15% of each run, Pallas kernels for 28% -> 29%
where the time goes in v8:
time: 220 us; the launch traced here: 219 us
  Pallas kernels  72.8 us (33%)
  waiting for transfers between devices  71.3 us (32%)
  starting transfers between devices  24.7 us (11%)
  local copies, waits for them, and re-layouts  19.9 us (9%)
  other arithmetic  18.7 us (8%)
  matrix products  10.9 us (5%)
    pallas_call x2, Pallas kernels, column_network(): pl.pallas_call(column_kernel, grid=(lat_local,), in_specs=[pl.BlockSpec(m...  62.6 us
    all_to_all x2, waiting for transfers between devices, round_trip(): lax.all_to_all(outbound, 'lat', split_axis=0, concat_axis=0, tiled=True)  38.4 us
    all_to_all x2, waiting for transfers between devices, round_trip(): lax.all_to_all(returning, 'lat', split_axis=1, concat_axis=1, tiled=True)  32.9 us
    another operation x1, other arithmetic  13.5 us
    dot_general x2, matrix products, hemisphere(): jnp.einsum('rnj,rnc->jrc', lat_basis, values, preferred_element_type=jnp....  10.9 us
    pallas_call x1, Pallas kernels, inverse_legendre(): pl.pallas_call(functools.partial(inverse_kernel, factor=factor), grid=(ro...  10.2 us
    all_to_all x2, starting transfers between devices, round_trip(): lax.all_to_all(outbound, 'lat', split_axis=0, concat_axis=0, tiled=True)  9.61 us
    all_to_all x2, starting transfers between devices, round_trip(): lax.all_to_all(returning, 'lat', split_axis=1, concat_axis=1, tiled=True)  7.81 us
  transfers between devices with their start and end apart: 5, of which 4 were waited for; matrix products, arithmetic and copies ran while one was open for 15% of the time, Pallas kernels for 29%

profile of v8, /device:TPU:0, one launch (start us, length us, event | category | flops | bytes accessed | tf_op | source)
XLA Modules:
  0.0 219.1 jit_solution(7413912737990498428)
XLA Ops:
  1.2 4.6 %fusion.38 = (f32[192,16,256]{2,0,1:T(8,128)S(1)}, bf16[192,16,256]{2,0,1:T(8,128)(2,1)S(1)}) fusion(bf16[16,512,192]{1,2,0:T(8,128)(2,1)} %param.9, bf16[16,512,256]{2,1,0:T(8,128)(2,1)} %spec_ref.1, pred[16,512]{1,0:T(8,128)(4,1)S(1)} %get-tuple-element.16), kind=kOutput, calls=%fused_computation.72 | convolution fusion | flops 808976384 | bytes 12066816 | tf_op jit(solution)/shard_map/rnj,rnc->jrc/dot_general | solution.py:193
  6.5 6.3 %fusion.37 = (f32[192,16,256]{2,0,1:T(8,128)S(1)}, bf16[192,16,256]{2,0,1:T(8,128)(2,1)S(1)}) fusion(bf16[16,512,192]{1,2,0:T(8,128)(2,1)S(1)} %copy-done.5, pred[16,512]{1,0:T(8,128)(4,1)S(1)} %get-tuple-element.15, bf16[16,512,256]{2,1,0:T(8,128)(2,1)S(1)} %copy-done.4, pred[16,512]{1,0:T(8,128)(4,1)S(1)} %get-tuple-element.16), kind=kOutput, calls=%fused_computation.71 | convolution fusion | flops 817364992 | bytes 12075008 | tf_op jit(solution)/shard_map/rnj,rnc->jrc/dot_general | solution.py:193
  14.3 7.3 %all-to-all-start.1 = ((f32[32,1,128]{2,1,0:T(1,128)}), f32[32,1,128]{2,1,0:T(1,128)S(1)}, u32[]{:S(2)}, u32[]{:S(2)}) async-start(f32[32,1,128]{2,1,0:T(1,128)} %broadcast_in_dim.92), calls=%async_computation.1 | async-start | bytes 32768 | tf_op jit(solution)/shard_map/all_to_all | solution.py:208
  21.6 13.5 %cosine_convert_fusion = (bf16[512,1536]{1,0:T(8,128)(2,1)S(1)}, bf16[512,1536]{1,0:T(8,128)(2,1)S(1)}) fusion(s32[512]{0:T(512)S(1)} %fusion.31), kind=kLoop, calls=%fused_computation.10 | loop fusion | flops 8650752 | bytes 3147776 | tf_op jit(solution)/shard_map/convert
  35.1 1.9 pad_maximum_fusion.table_ref
  36.9 2.0 copy.31
  39.0 5.8 %all-to-all-start.3 = ((bf16[32,6,16,256]{3,2,1,0:T(8,128)(2,1)}), bf16[32,6,16,256]{3,2,1,0:T(8,128)(2,1)S(1)}, u32[]{:S(2)}, u32[]{:S(2)}) async-start(bf16[32,6,16,256]{3,2,1,0:T(8,128)(2,1)} %bitcast.9), calls=%async_computation.3 | async-start | bytes 3145728 | tf_op jit(solution)/shard_map/all_to_all | solution.py:216
  44.9 2.0 copy.28
  46.9 35.7 %all-to-all-done.3.rows_ref = bf16[32,6,16,256]{3,2,1,0:T(8,128)(2,1)S(1)} async-done(((bf16[32,6,16,256]{3,2,1,0:T(8,128)(2,1)}), bf16[32,6,16,256]{3,2,1,0:T(8,128)(2,1)S(1)}, u32[]{:S(2)}, u32[]{:S(2)}) %all-to-all-start.3) | async-done | bytes 1572896 | tf_op jit(solution)/shard_map/all_to_all | solution.py:216
  82.6 3.8 %all-to-all-start = ((bf16[32,6,16,256]{3,2,1,0:T(8,128)(2,1)}), bf16[32,6,16,256]{3,2,1,0:T(8,128)(2,1)S(1)}, u32[]{:S(2)}, u32[]{:S(2)}) async-start(bf16[32,6,16,256]{3,2,1,0:T(8,128)(2,1)} %bitcast.25), calls=%async_computation | async-start | bytes 3145728 | tf_op jit(solution)/shard_map/all_to_all | solution.py:216
  87.8 0.9 copy-done.1
  88.7 31.2 %shard_map.83 = bf16[6,512,256]{2,1,0:T(8,128)(2,1)S(1)} custom-call(f32[6]{0:T(128)S(1)} %multiply_cosine_fusion.2.weight_ref, bf16[32,6,16,256]{3,2,1,0:T(8,128)(2,1)S(1)} %all-to-all-done.3.rows_ref, f32[1,128]{1,0:T(1,128)S(1)} %multiply_bitcast_fusion.scale_ref, bf16[128,1024]{1,0:T(8,128)(2,1)S(1)} %copy-done, f32[1,1024]{1,0:T(1,128)S(1)} %bitcast.23, ...), custom_call_target="tpu_custom_call" | custom-call | flops 9663676416 | bytes 6291456 | tf_op jit(solution)/shard_map/pallas_call | solution.py:90
  119.9 1.4 copy.32
  121.3 2.8 %all-to-all-done.rows_ref = bf16[32,6,16,256]{3,2,1,0:T(8,128)(2,1)S(1)} async-done(((bf16[32,6,16,256]{3,2,1,0:T(8,128)(2,1)}), bf16[32,6,16,256]{3,2,1,0:T(8,128)(2,1)S(1)}, u32[]{:S(2)}, u32[]{:S(2)}) %all-to-all-start) | async-done | bytes 1572896 | tf_op jit(solution)/shard_map/all_to_all | solution.py:216
  124.1 4.1 %all-to-all-start.4 = ((bf16[6,32,16,256]{3,2,0,1:T(8,128)(2,1)}), bf16[6,32,16,256]{3,2,0,1:T(8,128)(2,1)}, u32[]{:S(2)}, u32[]{:S(2)}) async-start(bf16[6,32,16,256]{3,2,0,1:T(8,128)(2,1)} %copy.32), calls=%async_computation.4 | async-start | bytes 3145728 | tf_op jit(solution)/shard_map/all_to_all | solution.py:221
  128.2 31.3 %shard_map.82 = bf16[6,512,256]{2,1,0:T(8,128)(2,1)S(1)} custom-call(f32[6]{0:T(128)S(1)} %multiply_cosine_fusion.3.weight_ref, bf16[32,6,16,256]{3,2,1,0:T(8,128)(2,1)S(1)} %all-to-all-done.rows_ref, f32[1,128]{1,0:T(1,128)S(1)} %multiply_bitcast_fusion.scale_ref, bf16[128,1024]{1,0:T(8,128)(2,1)S(1)} %copy-done, f32[1,1024]{1,0:T(1,128)S(1)} %bitcast.24, ...), custom_call_target="tpu_custom_call" | custom-call | flops 9663676416 | bytes 6291456 | tf_op jit(solution)/shard_map/pallas_call | solution.py:90
  159.6 1.4 copy.30
  160.9 4.8 %all-to-all-done.4 = bf16[6,32,16,256]{3,2,0,1:T(8,128)(2,1)} async-done(((bf16[6,32,16,256]{3,2,0,1:T(8,128)(2,1)}), bf16[6,32,16,256]{3,2,0,1:T(8,128)(2,1)}, u32[]{:S(2)}, u32[]{:S(2)}) %all-to-all-start.4) | async-done | bytes 1572896 | tf_op jit(solution)/shard_map/all_to_all | solution.py:221
  165.7 3.7 %all-to-all-start.2 = ((bf16[6,32,16,256]{3,2,0,1:T(8,128)(2,1)}), bf16[6,32,16,256]{3,2,0,1:T(8,128)(2,1)S(1)}, u32[]{:S(2)}, u32[]{:S(2)}) async-start(bf16[6,32,16,256]{3,2,0,1:T(8,128)(2,1)} %copy.30), calls=%async_computation.2 | async-start | bytes 3145728 | tf_op jit(solution)/shard_map/all_to_all | solution.py:221
  169.5 6.0 %copy.33.basis_ref = bf16[16,512,192]{2,1,0:T(8,128)(2,1)} copy(bf16[16,512,192]{1,2,0:T(8,128)(2,1)} %param.9) | data formatting | bytes 6291456 | tf_op args[1]
  176.0 3.1 %copy.35.south_ref = bf16[16,192,256]{2,1,0:T(8,128)(2,1)} copy(bf16[16,192,256]{2,0,1:T(8,128)(2,1)} %bitcast.12) | data formatting | bytes 3145728 | tf_op jit(solution)/shard_map/reshape | solution.py:222
  179.1 28.1 %all-to-all-done.2 = bf16[6,32,16,256]{3,2,0,1:T(8,128)(2,1)S(1)} async-done(((bf16[6,32,16,256]{3,2,0,1:T(8,128)(2,1)}), bf16[6,32,16,256]{3,2,0,1:T(8,128)(2,1)S(1)}, u32[]{:S(2)}, u32[]{:S(2)}) %all-to-all-start.2) | async-done | bytes 1572896 | tf_op jit(solution)/shard_map/all_to_all | solution.py:221
  207.2 1.7 copy.34.north_ref
  208.9 10.2 %shard_map.84 = f32[16,512,256]{2,1,0:T(8,128)} custom-call(s32[16]{0:T(128)} %copy-done.6, bf16[16,512,192]{2,1,0:T(8,128)(2,1)} %copy.33.basis_ref, bf16[16,192,256]{2,1,0:T(8,128)(2,1)} %copy.34.north_ref, bf16[16,192,256]{2,1,0:T(8,128)(2,1)} %copy.35.south_ref, bf16[16,512,256]{2,1,0:T(8,128)(2,1)} %spec_ref.1, f32[1,256]{1,0:T(1,128)} %bitcast.28), custom_call_target="tpu_custom_call" | custom-call | flops 1610612736 | bytes 18874368 | tf_op jit(solution)/shard_map/pallas_call | solution.py:142
  (36 shorter events, 4.7 us)
Async XLA Ops:
  1.0 4.8 %copy-start.6 = (s32[16]{0:T(128)}, s32[16]{0:T(128)S(1)}, u32[]{:S(2)}) copy-start(s32[16]{0:T(128)S(1)} %get-tuple-element.12.wave_ref) | copy-start | bytes 196
  1.2 4.6 %copy-start.4 = (bf16[16,512,256]{2,1,0:T(8,128)(2,1)S(1)}, bf16[16,512,256]{2,1,0:T(8,128)(2,1)}, u32[]{:S(2)}) copy-start(bf16[16,512,256]{2,1,0:T(8,128)(2,1)} %spec_ref.1) | copy-start | bytes 12582916
  1.2 5.3 %copy-start.5 = (bf16[16,512,192]{1,2,0:T(8,128)(2,1)S(1)}, bf16[16,512,192]{1,2,0:T(8,128)(2,1)}, u32[]{:S(2)}) copy-start(bf16[16,512,192]{1,2,0:T(8,128)(2,1)} %param.9) | copy-start | bytes 9437188
  14.3 24.7 %all-to-all-start.1 = ((f32[32,1,128]{2,1,0:T(1,128)}), f32[32,1,128]{2,1,0:T(1,128)S(1)}, u32[]{:S(2)}, u32[]{:S(2)}) async-start(f32[32,1,128]{2,1,0:T(1,128)} %broadcast_in_dim.92), calls=%async_computation.1 | async-start | bytes 32768 | tf_op jit(solution)/shard_map/all_to_all | solution.py:208
  39.0 43.6 %all-to-all-start.3 = ((bf16[32,6,16,256]{3,2,1,0:T(8,128)(2,1)}), bf16[32,6,16,256]{3,2,1,0:T(8,128)(2,1)S(1)}, u32[]{:S(2)}, u32[]{:S(2)}) async-start(bf16[32,6,16,256]{3,2,1,0:T(8,128)(2,1)} %bitcast.9), calls=%async_computation.3 | async-start | bytes 3145728 | tf_op jit(solution)/shard_map/all_to_all | solution.py:216
  44.8 42.9 %copy-start.7 = (f32[128]{0:T(128)S(1)}, f32[128]{0:T(128)}, u32[]{:S(2)}) copy-start(f32[128]{0:T(128)} %param.14) | copy-start | bytes 1540
  44.8 42.9 %copy-start = (bf16[128,1024]{1,0:T(8,128)(2,1)S(1)}, bf16[128,1024]{1,0:T(8,128)(2,1)}, u32[]{:S(2)}) copy-start(bf16[128,1024]{1,0:T(8,128)(2,1)} %in_w_ref.3) | copy-start | bytes 786436
  44.8 42.9 %copy-start.3 = (f32[1024]{0:T(1024)S(1)}, f32[1024]{0:T(1024)}, u32[]{:S(2)}) copy-start(f32[1024]{0:T(1024)} %param.12) | copy-start | bytes 12292
  82.6 41.5 %all-to-all-start = ((bf16[32,6,16,256]{3,2,1,0:T(8,128)(2,1)}), bf16[32,6,16,256]{3,2,1,0:T(8,128)(2,1)S(1)}, u32[]{:S(2)}, u32[]{:S(2)}) async-start(bf16[32,6,16,256]{3,2,1,0:T(8,128)(2,1)} %bitcast.25), calls=%async_computation | async-start | bytes 3145728 | tf_op jit(solution)/shard_map/all_to_all | solution.py:216
  87.8 1.0 copy-start.1
  119.9 8.3 %copy-start.2 = (bf16[1024,128]{1,0:T(8,128)(2,1)S(1)}, bf16[1024,128]{1,0:T(8,128)(2,1)}, u32[]{:S(2)}) copy-start(bf16[1024,128]{1,0:T(8,128)(2,1)} %out_w_ref.3) | copy-start | bytes 786436
  124.1 41.7 %all-to-all-start.4 = ((bf16[6,32,16,256]{3,2,0,1:T(8,128)(2,1)}), bf16[6,32,16,256]{3,2,0,1:T(8,128)(2,1)}, u32[]{:S(2)}, u32[]{:S(2)}) async-start(bf16[6,32,16,256]{3,2,0,1:T(8,128)(2,1)} %copy.32), calls=%async_computation.4 | async-start | bytes 3145728 | tf_op jit(solution)/shard_map/all_to_all | solution.py:221
  165.7 41.5 %all-to-all-start.2 = ((bf16[6,32,16,256]{3,2,0,1:T(8,128)(2,1)}), bf16[6,32,16,256]{3,2,0,1:T(8,128)(2,1)S(1)}, u32[]{:S(2)}, u32[]{:S(2)}) async-start(bf16[6,32,16,256]{3,2,0,1:T(8,128)(2,1)} %copy.30), calls=%async_computation.2 | async-start | bytes 3145728 | tf_op jit(solution)/shard_map/all_to_all | solution.py:221
  169.5 6.0 %copy-start.8 = (f32[128]{0:T(128)S(1)}, f32[128]{0:T(128)}, u32[]{:S(2)}) copy-start(f32[128]{0:T(128)} %param.15) | copy-start | bytes 1540

commit v9 on v7

--- a/solution.py
+++ b/solution.py
@@ -80,7 +80,8 @@
 def column_network(
     lat_w, rows_in, col_scale, in_weight, in_bias, out_weight, wave_table
 ):
-    sources, lat_local, rows_per, width = rows_in.shape
+    sources, _, rows_per, width = rows_in.shape
+    lat_local = lat_w.shape[0]
     chan = width // 2
     waves = sources * rows_per
     nlon = wave_table.shape[1]
@@ -205,15 +206,23 @@
     out_north, part_north = hemisphere(masked, lat_weights_of(j_all, lat_total))
     out_south, part_south = hemisphere(flipped, lat_weights_of(lat_total - 1 - j_all, lat_total))
     partial_value = part_north + part_south
-    gathered = lax.all_to_all(
-        jnp.broadcast_to(partial_value[None], (devices, chan_count)), "lat", 0, 0, tiled=True
-    )
-    global_sum = jnp.sum(gathered, axis=0)
+    hi = partial_value.astype(jnp.bfloat16)
+    rest = partial_value - hi.astype(jnp.float32)
+    mid = rest.astype(jnp.bfloat16)
+    lo = (rest - mid.astype(jnp.float32)).astype(jnp.bfloat16)
+    pieces = jnp.zeros((row_count, chan_width), jnp.bfloat16)
+    pieces = pieces.at[0, :chan_count].set(hi).at[0, chan_count:].set(mid)
+    pieces = pieces.at[1, :chan_count].set(lo)
+    slot = jnp.broadcast_to(pieces[None, None], (devices, 1, row_count, chan_width))
+    north_in = lax.all_to_all(
+        jnp.concatenate([out_north, slot], axis=1), "lat", split_axis=0, concat_axis=0, tiled=True
+    )
+    got = north_in[:, half_local, :2].astype(jnp.float32)
+    global_sum = jnp.sum(got[:, 0, :chan_count] + got[:, 0, chan_count:] + got[:, 1, :chan_count], axis=0)
     variance = global_sum / (NLON * jnp.sum(weight_all))
     col_scale = col_gain * lax.rsqrt(variance + 1e-05)
 
-    def round_trip(outbound, lat_weight):
-        rows_in = lax.all_to_all(outbound, "lat", split_axis=0, concat_axis=0, tiled=True)
+    def round_trip(rows_in, lat_weight):
         weighted_local = column_network(
             lat_weight, rows_in, col_scale, in_weight, in_bias, out_weight, wave_table
         )
@@ -221,8 +230,12 @@
         back = lax.all_to_all(returning, "lat", split_axis=1, concat_axis=1, tiled=True)
         return back.transpose(2, 1, 0, 3).reshape(row_count, half_lat, chan_width)
 
-    north = round_trip(out_north, weight_north)
-    south = round_trip(out_south, weight_south)
+    out_south, wave_table, col_scale, north_in = lax.optimization_barrier(
+        (out_south, wave_table, col_scale, north_in)
+    )
+    north = round_trip(north_in, weight_north)
+    south_in = lax.all_to_all(out_south, "lat", split_axis=0, concat_axis=0, tiled=True)
+    south = round_trip(south_in, weight_south)
     factor = 2.0 * math.sqrt(degrees * wave_total / lat_total)
     damp_all = jnp.concatenate([damping, damping])
     return inverse_legendre(wave_own, lat_basis, north, south, spectral, damp_all, factor)

time: 221 us -> 209 us (0.946)
  waiting for transfers between devices: 73.9 us -> 60.3 us
  other arithmetic: 18.7 us -> 22.8 us
  starting transfers between devices: 23.4 us -> 19.4 us
    all_to_all x3 -> x2, waiting for transfers between devices: 40.9 us -> 27.4 us  [the longest x1 24.5 us: on_device(): lax.all_to_all(jnp.concatenate([out_north, slot], axis=1), 'lat', split_a...]
    another operation x1 -> x4, other arithmetic: 13.5 us -> 16.1 us
    all_to_all x3 -> x2, starting transfers between devices: 13.5 us -> 11.5 us  [the longest x1 7.33 us: on_device(): lax.all_to_all(jnp.concatenate([out_north, slot], axis=1), 'lat', split_a...]
    unnamed x19 -> x23, local copies, waits for them, and re-layouts: 7.67 us -> 8.64 us
  transfers between devices with their start and end apart: 5 -> 4, of which waited for: 4 -> 4; matrix products, arithmetic and copies ran while one was open for 15% -> 15% of each run, Pallas kernels for 28% -> 30%
where the time goes in v9:
time: 209 us; the launch traced here: 208 us
  Pallas kernels  72.8 us (35%)
  waiting for transfers between devices  60.3 us (29%)
  other arithmetic  22.8 us (11%)
  local copies, waits for them, and re-layouts  21.3 us (10%)
  starting transfers between devices  19.4 us (9%)
  matrix products  10.9 us (5%)
    pallas_call x2, Pallas kernels, column_network(): pl.pallas_call(column_kernel, grid=(lat_local,), in_specs=[pl.BlockSpec(m...  62.6 us
    all_to_all x2, waiting for transfers between devices, round_trip(): lax.all_to_all(returning, 'lat', split_axis=1, concat_axis=1, tiled=True)  32.9 us
    all_to_all x1, waiting for transfers between devices, on_device(): lax.all_to_all(jnp.concatenate([out_north, slot], axis=1), 'lat', split_a...  24.5 us
    another operation x4, other arithmetic  16.1 us
    dot_general x2, matrix products, hemisphere(): jnp.einsum('rnj,rnc->jrc', lat_basis, values, preferred_element_type=jnp....  10.9 us
    pallas_call x1, Pallas kernels, inverse_legendre(): pl.pallas_call(functools.partial(inverse_kernel, factor=factor), grid=(ro...  10.2 us
    unnamed x23, local copies, waits for them, and re-layouts  8.64 us
    all_to_all x2, starting transfers between devices, round_trip(): lax.all_to_all(returning, 'lat', split_axis=1, concat_axis=1, tiled=True)  7.85 us
  transfers between devices with their start and end apart: 4, of which 4 were waited for; matrix products, arithmetic and copies ran while one was open for 15% of the time, Pallas kernels for 30%

profile of v9, /device:TPU:0, one launch (start us, length us, event | category | flops | bytes accessed | tf_op | source)
XLA Modules:
  0.0 208.3 jit_solution(6412962071647868335)
XLA Ops:
  1.2 4.6 %fusion.41 = (f32[192,16,256]{2,0,1:T(8,128)S(1)}, bf16[192,16,256]{2,0,1:T(8,128)(2,1)S(1)}) fusion(bf16[16,512,192]{1,2,0:T(8,128)(2,1)} %param.15, bf16[16,512,256]{2,1,0:T(8,128)(2,1)} %spec_ref.1, pred[16,512]{1,0:T(8,128)(4,1)S(1)} %get-tuple-element.57), kind=kOutput, calls=%fused_computation.86 | convolution fusion | flops 808976384 | bytes 12066816 | tf_op jit(solution)/shard_map/rnj,rnc->jrc/dot_general | solution.py:194
  6.5 6.3 %fusion.40 = (f32[192,16,256]{2,0,1:T(8,128)S(1)}, bf16[192,16,256]{2,0,1:T(8,128)(2,1)S(1)}) fusion(bf16[16,512,192]{1,2,0:T(8,128)(2,1)S(1)} %copy-done.6, pred[16,512]{1,0:T(8,128)(4,1)S(1)} %get-tuple-element.58, bf16[16,512,256]{2,1,0:T(8,128)(2,1)S(1)} %copy-done.5, pred[16,512]{1,0:T(8,128)(4,1)S(1)} %get-tuple-element.57), kind=kOutput, calls=%fused_computation.85 | convolution fusion | flops 817364992 | bytes 12075008 | tf_op jit(solution)/shard_map/rnj,rnc->jrc/dot_general | solution.py:194
  15.8 2.0 broadcast_select_fusion.7
  17.8 1.4 scatter.11
  19.4 1.4 pad_maximum_fusion.1
  20.8 7.3 %all-to-all-start = ((bf16[32,7,16,256]{3,2,1,0:T(8,128)(2,1)}), bf16[32,7,16,256]{3,2,1,0:T(8,128)(2,1)S(1)}, u32[]{:S(2)}, u32[]{:S(2)}) async-start(bf16[32,7,16,256]{3,2,1,0:T(8,128)(2,1)} %pad_maximum_fusion.1), calls=%async_computation | async-start | bytes 3670016 | tf_op jit(solution)/shard_map/all_to_all | solution.py:217
  28.1 2.0 copy.21
  31.4 13.5 %cosine_convert_fusion = (bf16[512,1536]{1,0:T(8,128)(2,1)S(1)}, bf16[512,1536]{1,0:T(8,128)(2,1)S(1)}) fusion(s32[512]{0:T(512)S(1)} %fusion.33), kind=kLoop, calls=%fused_computation.10 | loop fusion | flops 8650752 | bytes 3147776 | tf_op jit(solution)/shard_map/convert.1
  45.0 1.9 pad_maximum_fusion.table_ref
  46.8 24.5 %all-to-all-done.rows_ref = bf16[32,7,16,256]{3,2,1,0:T(8,128)(2,1)S(1)} async-done(((bf16[32,7,16,256]{3,2,1,0:T(8,128)(2,1)}), bf16[32,7,16,256]{3,2,1,0:T(8,128)(2,1)S(1)}, u32[]{:S(2)}, u32[]{:S(2)}) %all-to-all-start) | async-done | bytes 1835040 | tf_op jit(solution)/shard_map/all_to_all | solution.py:217
  71.4 4.2 %all-to-all-start.2 = ((bf16[32,6,16,256]{3,2,1,0:T(8,128)(2,1)}), bf16[32,6,16,256]{3,2,1,0:T(8,128)(2,1)S(1)}, u32[]{:S(2)}, u32[]{:S(2)}) async-start(bf16[32,6,16,256]{3,2,1,0:T(8,128)(2,1)} %bitcast.41), calls=%async_computation.2 | async-start | bytes 3145728 | tf_op jit(solution)/shard_map/all_to_all | solution.py:237
  77.6 31.3 %shard_map.82 = bf16[6,512,256]{2,1,0:T(8,128)(2,1)S(1)} custom-call(f32[6]{0:T(128)S(1)} %multiply_cosine_fusion.3.weight_ref, bf16[32,7,16,256]{3,2,1,0:T(8,128)(2,1)S(1)} %all-to-all-done.rows_ref, f32[1,128]{1,0:T(1,128)S(1)} %bitcast.37, bf16[128,1024]{1,0:T(8,128)(2,1)S(1)} %copy-done, f32[1,1024]{1,0:T(1,128)S(1)} %bitcast.39, ...), custom_call_target="tpu_custom_call" | custom-call | flops 9663676416 | bytes 6291456 | tf_op jit(solution)/shard_map/pallas_call | solution.py:91
  109.0 1.3 copy.23
  110.3 2.9 %all-to-all-done.2.rows_ref = bf16[32,6,16,256]{3,2,1,0:T(8,128)(2,1)S(1)} async-done(((bf16[32,6,16,256]{3,2,1,0:T(8,128)(2,1)}), bf16[32,6,16,256]{3,2,1,0:T(8,128)(2,1)S(1)}, u32[]{:S(2)}, u32[]{:S(2)}) %all-to-all-start.2) | async-done | bytes 1572896 | tf_op jit(solution)/shard_map/all_to_all | solution.py:237
  113.2 3.9 %all-to-all-start.1 = ((bf16[6,32,16,256]{3,2,0,1:T(8,128)(2,1)}), bf16[6,32,16,256]{3,2,0,1:T(8,128)(2,1)}, u32[]{:S(2)}, u32[]{:S(2)}) async-start(bf16[6,32,16,256]{3,2,0,1:T(8,128)(2,1)} %copy.23), calls=%async_computation.1 | async-start | bytes 3145728 | tf_op jit(solution)/shard_map/all_to_all | solution.py:230
  117.2 31.2 %shard_map.83 = bf16[6,512,256]{2,1,0:T(8,128)(2,1)S(1)} custom-call(f32[6]{0:T(128)S(1)} %multiply_cosine_fusion.2.weight_ref, bf16[32,6,16,256]{3,2,1,0:T(8,128)(2,1)S(1)} %all-to-all-done.2.rows_ref, f32[1,128]{1,0:T(1,128)S(1)} %bitcast.38, bf16[128,1024]{1,0:T(8,128)(2,1)S(1)} %copy-done.1, f32[1,1024]{1,0:T(1,128)S(1)} %bitcast.40, ...), custom_call_target="tpu_custom_call" | custom-call | flops 9663676416 | bytes 6291456 | tf_op jit(solution)/shard_map/pallas_call | solution.py:91
  148.4 1.4 copy.24
  149.8 5.1 %all-to-all-done.1 = bf16[6,32,16,256]{3,2,0,1:T(8,128)(2,1)} async-done(((bf16[6,32,16,256]{3,2,0,1:T(8,128)(2,1)}), bf16[6,32,16,256]{3,2,0,1:T(8,128)(2,1)}, u32[]{:S(2)}, u32[]{:S(2)}) %all-to-all-start.1) | async-done | bytes 1572896 | tf_op jit(solution)/shard_map/all_to_all | solution.py:230
  154.8 4.0 %all-to-all-start.3 = ((bf16[6,32,16,256]{3,2,0,1:T(8,128)(2,1)}), bf16[6,32,16,256]{3,2,0,1:T(8,128)(2,1)S(1)}, u32[]{:S(2)}, u32[]{:S(2)}) async-start(bf16[6,32,16,256]{3,2,0,1:T(8,128)(2,1)} %copy.24), calls=%async_computation.3 | async-start | bytes 3145728 | tf_op jit(solution)/shard_map/all_to_all | solution.py:230
  158.8 6.0 %copy.25.basis_ref = bf16[16,512,192]{2,1,0:T(8,128)(2,1)} copy(bf16[16,512,192]{1,2,0:T(8,128)(2,1)} %param.15) | data formatting | bytes 6291456 | tf_op args[1]
  165.4 3.1 %copy.26.north_ref = bf16[16,192,256]{2,1,0:T(8,128)(2,1)} copy(bf16[16,192,256]{2,0,1:T(8,128)(2,1)} %bitcast.13) | data formatting | bytes 3145728 | tf_op jit(solution)/shard_map/reshape | solution.py:231
  168.5 27.9 %all-to-all-done.3 = bf16[6,32,16,256]{3,2,0,1:T(8,128)(2,1)S(1)} async-done(((bf16[6,32,16,256]{3,2,0,1:T(8,128)(2,1)}), bf16[6,32,16,256]{3,2,0,1:T(8,128)(2,1)S(1)}, u32[]{:S(2)}, u32[]{:S(2)}) %all-to-all-start.3) | async-done | bytes 1572896 | tf_op jit(solution)/shard_map/all_to_all | solution.py:230
  196.4 1.7 copy.27.south_ref
  198.1 10.2 %shard_map.84 = f32[16,512,256]{2,1,0:T(8,128)} custom-call(s32[16]{0:T(128)} %copy-done.7, bf16[16,512,192]{2,1,0:T(8,128)(2,1)} %copy.25.basis_ref, bf16[16,192,256]{2,1,0:T(8,128)(2,1)} %copy.26.north_ref, bf16[16,192,256]{2,1,0:T(8,128)(2,1)} %copy.27.south_ref, bf16[16,512,256]{2,1,0:T(8,128)(2,1)} %spec_ref.1, f32[1,256]{1,0:T(1,128)} %bitcast.44), custom_call_target="tpu_custom_call" | custom-call | flops 1610612736 | bytes 18874368 | tf_op jit(solution)/shard_map/pallas_call | solution.py:143
  (48 shorter events, 8.4 us)
Async XLA Ops:
  1.0 4.8 %copy-start.7 = (s32[16]{0:T(128)}, s32[16]{0:T(128)S(1)}, u32[]{:S(2)}) copy-start(s32[16]{0:T(128)S(1)} %get-tuple-element.52.wave_ref) | copy-start | bytes 196
  1.2 4.6 %copy-start.5 = (bf16[16,512,256]{2,1,0:T(8,128)(2,1)S(1)}, bf16[16,512,256]{2,1,0:T(8,128)(2,1)}, u32[]{:S(2)}) copy-start(bf16[16,512,256]{2,1,0:T(8,128)(2,1)} %spec_ref.1) | copy-start | bytes 12582916
  1.2 5.3 %copy-start.6 = (bf16[16,512,192]{1,2,0:T(8,128)(2,1)S(1)}, bf16[16,512,192]{1,2,0:T(8,128)(2,1)}, u32[]{:S(2)}) copy-start(bf16[16,512,192]{1,2,0:T(8,128)(2,1)} %param.15) | copy-start | bytes 9437188
  12.8 1.5 copy-start.10
  20.8 50.5 %all-to-all-start = ((bf16[32,7,16,256]{3,2,1,0:T(8,128)(2,1)}), bf16[32,7,16,256]{3,2,1,0:T(8,128)(2,1)S(1)}, u32[]{:S(2)}, u32[]{:S(2)}) async-start(bf16[32,7,16,256]{3,2,1,0:T(8,128)(2,1)} %pad_maximum_fusion.1), calls=%async_computation | async-start | bytes 3670016 | tf_op jit(solution)/shard_map/all_to_all | solution.py:217
  45.0 26.5 %copy-start.8 = (f32[128]{0:T(128)S(1)}, f32[128]{0:T(128)}, u32[]{:S(2)}) copy-start(f32[128]{0:T(128)} %param.20) | copy-start | bytes 1540
  46.8 28.9 %copy-start.4 = (f32[1024]{0:T(1024)S(1)}, f32[1024]{0:T(1024)}, u32[]{:S(2)}) copy-start(f32[1024]{0:T(1024)} %param.18) | copy-start | bytes 12292
  71.4 41.8 %all-to-all-start.2 = ((bf16[32,6,16,256]{3,2,1,0:T(8,128)(2,1)}), bf16[32,6,16,256]{3,2,1,0:T(8,128)(2,1)S(1)}, u32[]{:S(2)}, u32[]{:S(2)}) async-start(bf16[32,6,16,256]{3,2,1,0:T(8,128)(2,1)} %bitcast.41), calls=%async_computation.2 | async-start | bytes 3145728 | tf_op jit(solution)/shard_map/all_to_all | solution.py:237
  75.7 1.0 copy-start
  76.7 0.9 copy-start.2
  109.0 8.2 %copy-start.1 = (bf16[128,1024]{1,0:T(8,128)(2,1)S(1)}, bf16[128,1024]{1,0:T(8,128)(2,1)}, u32[]{:S(2)}) copy-start(bf16[128,1024]{1,0:T(8,128)(2,1)} %in_w_ref.3) | copy-start | bytes 786436
  109.0 8.2 %copy-start.3 = (bf16[1024,128]{1,0:T(8,128)(2,1)S(1)}, bf16[1024,128]{1,0:T(8,128)(2,1)}, u32[]{:S(2)}) copy-start(bf16[1024,128]{1,0:T(8,128)(2,1)} %out_w_ref.3) | copy-start | bytes 786436
  113.2 41.6 %all-to-all-start.1 = ((bf16[6,32,16,256]{3,2,0,1:T(8,128)(2,1)}), bf16[6,32,16,256]{3,2,0,1:T(8,128)(2,1)}, u32[]{:S(2)}, u32[]{:S(2)}) async-start(bf16[6,32,16,256]{3,2,0,1:T(8,128)(2,1)} %copy.23), calls=%async_computation.1 | async-start | bytes 3145728 | tf_op jit(solution)/shard_map/all_to_all | solution.py:230
  154.8 41.6 %all-to-all-start.3 = ((bf16[6,32,16,256]{3,2,0,1:T(8,128)(2,1)}), bf16[6,32,16,256]{3,2,0,1:T(8,128)(2,1)S(1)}, u32[]{:S(2)}, u32[]{:S(2)}) async-start(bf16[6,32,16,256]{3,2,0,1:T(8,128)(2,1)} %copy.24), calls=%async_computation.3 | async-start | bytes 3145728 | tf_op jit(solution)/shard_map/all_to_all | solution.py:230
  158.8 6.0 %copy-start.9 = (f32[128]{0:T(128)S(1)}, f32[128]{0:T(128)}, u32[]{:S(2)}) copy-start(f32[128]{0:T(128)} %param.21) | copy-start | bytes 1540

commit v10 on v9

--- a/solution.py
+++ b/solution.py
@@ -210,9 +210,13 @@
     rest = partial_value - hi.astype(jnp.float32)
     mid = rest.astype(jnp.bfloat16)
     lo = (rest - mid.astype(jnp.float32)).astype(jnp.bfloat16)
-    pieces = jnp.zeros((row_count, chan_width), jnp.bfloat16)
-    pieces = pieces.at[0, :chan_count].set(hi).at[0, chan_count:].set(mid)
-    pieces = pieces.at[1, :chan_count].set(lo)
+    pieces = jnp.concatenate(
+        [
+            jnp.concatenate([hi, mid])[None],
+            jnp.concatenate([lo, jnp.zeros_like(lo)])[None],
+            jnp.zeros((row_count - 2, chan_width), jnp.bfloat16),
+        ]
+    )
     slot = jnp.broadcast_to(pieces[None, None], (devices, 1, row_count, chan_width))
     north_in = lax.all_to_all(
         jnp.concatenate([out_north, slot], axis=1), "lat", split_axis=0, concat_axis=0, tiled=True

time: 209 us -> 204 us (0.976)
  other arithmetic: 22.8 us -> 20.2 us
  local copies, waits for them, and re-layouts: 21.3 us -> 19.1 us
    another operation x4 -> x1, other arithmetic: 16.1 us -> 13.5 us
    unnamed x23 -> x21, local copies, waits for them, and re-layouts: 8.64 us -> 8.62 us
  transfers between devices with their start and end apart: 4 -> 4, of which waited for: 4 -> 4; matrix products, arithmetic and copies ran while one was open for 15% -> 15% of each run, Pallas kernels for 30% -> 31%
where the time goes in v10:
time: 204 us
  Pallas kernels  72.8 us (36%)
  waiting for transfers between devices  60.6 us (30%)
  other arithmetic  20.2 us (10%)
  starting transfers between devices  19.2 us (9%)
  local copies, waits for them, and re-layouts  19.1 us (9%)
  matrix products  10.9 us (5%)
    pallas_call x2, Pallas kernels, column_network(): pl.pallas_call(column_kernel, grid=(lat_local,), in_specs=[pl.BlockSpec(m...  62.6 us
    all_to_all x2, waiting for transfers between devices, round_trip(): lax.all_to_all(returning, 'lat', split_axis=1, concat_axis=1, tiled=True)  33 us
    all_to_all x1, waiting for transfers between devices, on_device(): lax.all_to_all(jnp.concatenate([out_north, slot], axis=1), 'lat', split_a...  24.5 us
    another operation x1, other arithmetic  13.5 us
    dot_general x2, matrix products, hemisphere(): jnp.einsum('rnj,rnc->jrc', lat_basis, values, preferred_element_type=jnp....  10.9 us
    pallas_call x1, Pallas kernels, inverse_legendre(): pl.pallas_call(functools.partial(inverse_kernel, factor=factor), grid=(ro...  10.2 us
    unnamed x21, local copies, waits for them, and re-layouts  8.62 us
    all_to_all x2, starting transfers between devices, round_trip(): lax.all_to_all(returning, 'lat', split_axis=1, concat_axis=1, tiled=True)  7.81 us
  transfers between devices with their start and end apart: 4, of which 4 were waited for; matrix products, arithmetic and copies ran while one was open for 15% of the time, Pallas kernels for 31%

profile of v10, /device:TPU:0, one launch (start us, length us, event | category | flops | bytes accessed | tf_op | source)
XLA Modules:
  0.0 203.7 jit_solution(13071857587404126336)
XLA Ops:
  1.2 4.6 %fusion.41 = (f32[192,16,256]{2,0,1:T(8,128)S(1)}, bf16[192,16,256]{2,0,1:T(8,128)(2,1)S(1)}) fusion(bf16[16,512,192]{1,2,0:T(8,128)(2,1)} %param.9, bf16[16,512,256]{2,1,0:T(8,128)(2,1)} %spec_ref.1, pred[16,512]{1,0:T(8,128)(4,1)S(1)} %get-tuple-element.22), kind=kOutput, calls=%fused_computation.84 | convolution fusion | flops 808976384 | bytes 12066816 | tf_op jit(solution)/shard_map/rnj,rnc->jrc/dot_general | solution.py:194
  6.5 6.3 %fusion.40 = (f32[192,16,256]{2,0,1:T(8,128)S(1)}, bf16[192,16,256]{2,0,1:T(8,128)(2,1)S(1)}) fusion(bf16[16,512,192]{1,2,0:T(8,128)(2,1)S(1)} %copy-done.6, pred[16,512]{1,0:T(8,128)(4,1)S(1)} %get-tuple-element.23, bf16[16,512,256]{2,1,0:T(8,128)(2,1)S(1)} %copy-done.5, pred[16,512]{1,0:T(8,128)(4,1)S(1)} %get-tuple-element.22), kind=kOutput, calls=%fused_computation.83 | convolution fusion | flops 817364992 | bytes 12075008 | tf_op jit(solution)/shard_map/rnj,rnc->jrc/dot_general | solution.py:194
  14.8 1.4 pad_maximum_fusion.1
  16.2 7.3 %all-to-all-start = ((bf16[32,7,16,256]{3,2,1,0:T(8,128)(2,1)}), bf16[32,7,16,256]{3,2,1,0:T(8,128)(2,1)S(1)}, u32[]{:S(2)}, u32[]{:S(2)}) async-start(bf16[32,7,16,256]{3,2,1,0:T(8,128)(2,1)} %pad_maximum_fusion.1), calls=%async_computation | async-start | bytes 3670016 | tf_op jit(solution)/shard_map/all_to_all | solution.py:221
  23.5 2.0 copy.21
  26.8 13.5 %cosine_convert_fusion = (bf16[512,1536]{1,0:T(8,128)(2,1)S(1)}, bf16[512,1536]{1,0:T(8,128)(2,1)S(1)}) fusion(s32[512]{0:T(512)S(1)} %fusion.33), kind=kLoop, calls=%fused_computation.10 | loop fusion | flops 8650752 | bytes 3147776 | tf_op jit(solution)/shard_map/convert.1
  40.4 1.9 pad_maximum_fusion.table_ref
  42.2 24.5 %all-to-all-done.rows_ref = bf16[32,7,16,256]{3,2,1,0:T(8,128)(2,1)S(1)} async-done(((bf16[32,7,16,256]{3,2,1,0:T(8,128)(2,1)}), bf16[32,7,16,256]{3,2,1,0:T(8,128)(2,1)S(1)}, u32[]{:S(2)}, u32[]{:S(2)}) %all-to-all-start) | async-done | bytes 1835040 | tf_op jit(solution)/shard_map/all_to_all | solution.py:221
  66.8 4.0 %all-to-all-start.2 = ((bf16[32,6,16,256]{3,2,1,0:T(8,128)(2,1)}), bf16[32,6,16,256]{3,2,1,0:T(8,128)(2,1)S(1)}, u32[]{:S(2)}, u32[]{:S(2)}) async-start(bf16[32,6,16,256]{3,2,1,0:T(8,128)(2,1)} %bitcast.30), calls=%async_computation.2 | async-start | bytes 3145728 | tf_op jit(solution)/shard_map/all_to_all | solution.py:241
  70.9 0.9 copy-done
  71.9 0.9 copy-done.2
  72.8 31.3 %shard_map.82 = bf16[6,512,256]{2,1,0:T(8,128)(2,1)S(1)} custom-call(f32[6]{0:T(128)S(1)} %multiply_cosine_fusion.3.weight_ref, bf16[32,7,16,256]{3,2,1,0:T(8,128)(2,1)S(1)} %all-to-all-done.rows_ref, f32[1,128]{1,0:T(1,128)S(1)} %bitcast.26, bf16[128,1024]{1,0:T(8,128)(2,1)S(1)} %copy-done, f32[1,1024]{1,0:T(1,128)S(1)} %bitcast.28, ...), custom_call_target="tpu_custom_call" | custom-call | flops 9663676416 | bytes 6291456 | tf_op jit(solution)/shard_map/pallas_call | solution.py:91
  104.2 1.3 copy.23
  105.5 3.1 %all-to-all-done.2.rows_ref = bf16[32,6,16,256]{3,2,1,0:T(8,128)(2,1)S(1)} async-done(((bf16[32,6,16,256]{3,2,1,0:T(8,128)(2,1)}), bf16[32,6,16,256]{3,2,1,0:T(8,128)(2,1)S(1)}, u32[]{:S(2)}, u32[]{:S(2)}) %all-to-all-start.2) | async-done | bytes 1572896 | tf_op jit(solution)/shard_map/all_to_all | solution.py:241
  108.6 4.1 %all-to-all-start.1 = ((bf16[6,32,16,256]{3,2,0,1:T(8,128)(2,1)}), bf16[6,32,16,256]{3,2,0,1:T(8,128)(2,1)}, u32[]{:S(2)}, u32[]{:S(2)}) async-start(bf16[6,32,16,256]{3,2,0,1:T(8,128)(2,1)} %copy.23), calls=%async_computation.1 | async-start | bytes 3145728 | tf_op jit(solution)/shard_map/all_to_all | solution.py:234
  112.7 31.2 %shard_map.83 = bf16[6,512,256]{2,1,0:T(8,128)(2,1)S(1)} custom-call(f32[6]{0:T(128)S(1)} %multiply_cosine_fusion.2.weight_ref, bf16[32,6,16,256]{3,2,1,0:T(8,128)(2,1)S(1)} %all-to-all-done.2.rows_ref, f32[1,128]{1,0:T(1,128)S(1)} %bitcast.27, bf16[128,1024]{1,0:T(8,128)(2,1)S(1)} %copy-done.1, f32[1,1024]{1,0:T(1,128)S(1)} %bitcast.29, ...), custom_call_target="tpu_custom_call" | custom-call | flops 9663676416 | bytes 6291456 | tf_op jit(solution)/shard_map/pallas_call | solution.py:91
  144.0 1.4 copy.24
  145.3 4.9 %all-to-all-done.1 = bf16[6,32,16,256]{3,2,0,1:T(8,128)(2,1)} async-done(((bf16[6,32,16,256]{3,2,0,1:T(8,128)(2,1)}), bf16[6,32,16,256]{3,2,0,1:T(8,128)(2,1)}, u32[]{:S(2)}, u32[]{:S(2)}) %all-to-all-start.1) | async-done | bytes 1572896 | tf_op jit(solution)/shard_map/all_to_all | solution.py:234
  150.2 3.7 %all-to-all-start.3 = ((bf16[6,32,16,256]{3,2,0,1:T(8,128)(2,1)}), bf16[6,32,16,256]{3,2,0,1:T(8,128)(2,1)S(1)}, u32[]{:S(2)}, u32[]{:S(2)}) async-start(bf16[6,32,16,256]{3,2,0,1:T(8,128)(2,1)} %copy.24), calls=%async_computation.3 | async-start | bytes 3145728 | tf_op jit(solution)/shard_map/all_to_all | solution.py:234
  154.0 6.0 %copy.25.basis_ref = bf16[16,512,192]{2,1,0:T(8,128)(2,1)} copy(bf16[16,512,192]{1,2,0:T(8,128)(2,1)} %param.9) | data formatting | bytes 6291456 | tf_op args[1]
  160.5 3.1 %copy.26.north_ref = bf16[16,192,256]{2,1,0:T(8,128)(2,1)} copy(bf16[16,192,256]{2,0,1:T(8,128)(2,1)} %bitcast.10) | data formatting | bytes 3145728 | tf_op jit(solution)/shard_map/reshape | solution.py:235
  163.7 28.1 %all-to-all-done.3 = bf16[6,32,16,256]{3,2,0,1:T(8,128)(2,1)S(1)} async-done(((bf16[6,32,16,256]{3,2,0,1:T(8,128)(2,1)}), bf16[6,32,16,256]{3,2,0,1:T(8,128)(2,1)S(1)}, u32[]{:S(2)}, u32[]{:S(2)}) %all-to-all-start.3) | async-done | bytes 1572896 | tf_op jit(solution)/shard_map/all_to_all | solution.py:234
  191.7 1.7 copy.27.south_ref
  193.4 10.2 %shard_map.84 = f32[16,512,256]{2,1,0:T(8,128)} custom-call(s32[16]{0:T(128)} %copy-done.7, bf16[16,512,192]{2,1,0:T(8,128)(2,1)} %copy.25.basis_ref, bf16[16,192,256]{2,1,0:T(8,128)(2,1)} %copy.26.north_ref, bf16[16,192,256]{2,1,0:T(8,128)(2,1)} %copy.27.south_ref, bf16[16,512,256]{2,1,0:T(8,128)(2,1)} %spec_ref.1, f32[1,256]{1,0:T(1,128)} %bitcast.33), custom_call_target="tpu_custom_call" | custom-call | flops 1610612736 | bytes 18874368 | tf_op jit(solution)/shard_map/pallas_call | solution.py:143
  (45 shorter events, 5.2 us)
Async XLA Ops:
  1.0 4.8 %copy-start.7 = (s32[16]{0:T(128)}, s32[16]{0:T(128)S(1)}, u32[]{:S(2)}) copy-start(s32[16]{0:T(128)S(1)} %get-tuple-element.16.wave_ref) | copy-start | bytes 196
  1.2 4.6 %copy-start.5 = (bf16[16,512,256]{2,1,0:T(8,128)(2,1)S(1)}, bf16[16,512,256]{2,1,0:T(8,128)(2,1)}, u32[]{:S(2)}) copy-start(bf16[16,512,256]{2,1,0:T(8,128)(2,1)} %spec_ref.1) | copy-start | bytes 12582916
  1.2 5.3 %copy-start.6 = (bf16[16,512,192]{1,2,0:T(8,128)(2,1)S(1)}, bf16[16,512,192]{1,2,0:T(8,128)(2,1)}, u32[]{:S(2)}) copy-start(bf16[16,512,192]{1,2,0:T(8,128)(2,1)} %param.9) | copy-start | bytes 9437188
  16.2 50.5 %all-to-all-start = ((bf16[32,7,16,256]{3,2,1,0:T(8,128)(2,1)}), bf16[32,7,16,256]{3,2,1,0:T(8,128)(2,1)S(1)}, u32[]{:S(2)}, u32[]{:S(2)}) async-start(bf16[32,7,16,256]{3,2,1,0:T(8,128)(2,1)} %pad_maximum_fusion.1), calls=%async_computation | async-start | bytes 3670016 | tf_op jit(solution)/shard_map/all_to_all | solution.py:221
  40.3 26.5 %copy-start.8 = (f32[128]{0:T(128)S(1)}, f32[128]{0:T(128)}, u32[]{:S(2)}) copy-start(f32[128]{0:T(128)} %param.14) | copy-start | bytes 1540
  42.2 28.7 %copy-start.4 = (f32[1024]{0:T(1024)S(1)}, f32[1024]{0:T(1024)}, u32[]{:S(2)}) copy-start(f32[1024]{0:T(1024)} %param.12) | copy-start | bytes 12292
  66.8 41.8 %all-to-all-start.2 = ((bf16[32,6,16,256]{3,2,1,0:T(8,128)(2,1)}), bf16[32,6,16,256]{3,2,1,0:T(8,128)(2,1)S(1)}, u32[]{:S(2)}, u32[]{:S(2)}) async-start(bf16[32,6,16,256]{3,2,1,0:T(8,128)(2,1)} %bitcast.30), calls=%async_computation.2 | async-start | bytes 3145728 | tf_op jit(solution)/shard_map/all_to_all | solution.py:241
  70.9 1.0 copy-start
  71.9 0.9 copy-start.2
  104.2 8.6 %copy-start.1 = (bf16[128,1024]{1,0:T(8,128)(2,1)S(1)}, bf16[128,1024]{1,0:T(8,128)(2,1)}, u32[]{:S(2)}) copy-start(bf16[128,1024]{1,0:T(8,128)(2,1)} %in_w_ref.3) | copy-start | bytes 786436
  104.2 8.6 %copy-start.3 = (bf16[1024,128]{1,0:T(8,128)(2,1)S(1)}, bf16[1024,128]{1,0:T(8,128)(2,1)}, u32[]{:S(2)}) copy-start(bf16[1024,128]{1,0:T(8,128)(2,1)} %out_w_ref.3) | copy-start | bytes 786436
  108.6 41.7 %all-to-all-start.1 = ((bf16[6,32,16,256]{3,2,0,1:T(8,128)(2,1)}), bf16[6,32,16,256]{3,2,0,1:T(8,128)(2,1)}, u32[]{:S(2)}, u32[]{:S(2)}) async-start(bf16[6,32,16,256]{3,2,0,1:T(8,128)(2,1)} %copy.23), calls=%async_computation.1 | async-start | bytes 3145728 | tf_op jit(solution)/shard_map/all_to_all | solution.py:234
  150.2 41.5 %all-to-all-start.3 = ((bf16[6,32,16,256]{3,2,0,1:T(8,128)(2,1)}), bf16[6,32,16,256]{3,2,0,1:T(8,128)(2,1)S(1)}, u32[]{:S(2)}, u32[]{:S(2)}) async-start(bf16[6,32,16,256]{3,2,0,1:T(8,128)(2,1)} %copy.24), calls=%async_computation.3 | async-start | bytes 3145728 | tf_op jit(solution)/shard_map/all_to_all | solution.py:234
  154.0 6.0 %copy-start.9 = (f32[128]{0:T(128)S(1)}, f32[128]{0:T(128)}, u32[]{:S(2)}) copy-start(f32[128]{0:T(128)} %param.15) | copy-start | bytes 1540

commit v11 on v10

--- a/solution.py
+++ b/solution.py
@@ -210,19 +210,21 @@
     rest = partial_value - hi.astype(jnp.float32)
     mid = rest.astype(jnp.bfloat16)
     lo = (rest - mid.astype(jnp.float32)).astype(jnp.bfloat16)
-    pieces = jnp.concatenate(
+    pieces = jnp.concatenate([hi, mid, lo])
+    flat = half_local * row_count * chan_width
+    send = jnp.concatenate(
         [
-            jnp.concatenate([hi, mid])[None],
-            jnp.concatenate([lo, jnp.zeros_like(lo)])[None],
-            jnp.zeros((row_count - 2, chan_width), jnp.bfloat16),
-        ]
-    )
-    slot = jnp.broadcast_to(pieces[None, None], (devices, 1, row_count, chan_width))
-    north_in = lax.all_to_all(
-        jnp.concatenate([out_north, slot], axis=1), "lat", split_axis=0, concat_axis=0, tiled=True
-    )
-    got = north_in[:, half_local, :2].astype(jnp.float32)
-    global_sum = jnp.sum(got[:, 0, :chan_count] + got[:, 0, chan_count:] + got[:, 1, :chan_count], axis=0)
+            out_north.reshape(devices, flat),
+            jnp.broadcast_to(pieces[None], (devices, 3 * chan_count)),
+        ],
+        axis=1,
+    )
+    got = lax.all_to_all(send, "lat", split_axis=0, concat_axis=0, tiled=True)
+    north_in = got[:, :flat].reshape(devices, half_local, row_count, chan_width)
+    got = got[:, flat:].astype(jnp.float32)
+    global_sum = jnp.sum(
+        got[:, :chan_count] + got[:, chan_count:2 * chan_count] + got[:, 2 * chan_count:], axis=0
+    )
     variance = global_sum / (NLON * jnp.sum(weight_all))
     col_scale = col_gain * lax.rsqrt(variance + 1e-05)
 
@@ -234,8 +236,8 @@
         back = lax.all_to_all(returning, "lat", split_axis=1, concat_axis=1, tiled=True)
         return back.transpose(2, 1, 0, 3).reshape(row_count, half_lat, chan_width)
 
-    out_south, wave_table, col_scale, north_in = lax.optimization_barrier(
-        (out_south, wave_table, col_scale, north_in)
+    out_south, wave_table, col_scale = lax.optimization_barrier(
+        (out_south, wave_table, col_scale)
     )
     north = round_trip(north_in, weight_north)
     south_in = lax.all_to_all(out_south, "lat", split_axis=0, concat_axis=0, tiled=True)

time: 204 us -> 218 us (1.069)
  local copies, waits for them, and re-layouts: 19.1 us -> 33.2 us
  waiting for transfers between devices: 60.6 us -> 55.2 us
  other arithmetic: 20.2 us -> 23.9 us
    unnamed x21 -> x25, local copies, waits for them, and re-layouts: 8.62 us -> 19.9 us
    all_to_all x1, waiting for transfers between devices: 24.5 us -> 19.6 us  [on_device(): got = lax.all_to_all(send, 'lat', split_axis=0, concat_axis=0, tiled=True)]
    reduce_sum x1, other arithmetic: 0.65 us -> 3.64 us  [hemisphere(): jnp.sum(real_coef[None, :, None] * wide[:, :, :chan_count] ** 2 + imag_co...]
    all_to_all x0 -> x2, other arithmetic: none -> 2.19 us  [on_device(): got = lax.all_to_all(send, 'lat', split_axis=0, concat_axis=0, tiled=True)]
  transfers between devices with their start and end apart: 4 -> 4, of which waited for: 4 -> 4; matrix products, arithmetic and copies ran while one was open for 15% -> 15% of each run, Pallas kernels for 31% -> 29%
where the time goes in v11:
time: 218 us; the launch traced here: 217 us
  Pallas kernels  73 us (33%)
  waiting for transfers between devices  55.2 us (25%)
  local copies, waits for them, and re-layouts  33.2 us (15%)
  other arithmetic  23.9 us (11%)
  starting transfers between devices  19.3 us (9%)
  matrix products  11.7 us (5%)
    pallas_call x2, Pallas kernels, column_network(): pl.pallas_call(column_kernel, grid=(lat_local,), in_specs=[pl.BlockSpec(m...  62.8 us
    all_to_all x2, waiting for transfers between devices, round_trip(): lax.all_to_all(returning, 'lat', split_axis=1, concat_axis=1, tiled=True)  32.8 us
    unnamed x25, local copies, waits for them, and re-layouts  19.9 us
    all_to_all x1, waiting for transfers between devices, on_device(): got = lax.all_to_all(send, 'lat', split_axis=0, concat_axis=0, tiled=True)  19.6 us
    another operation x1, other arithmetic  13.5 us
    dot_general x2, matrix products, hemisphere(): jnp.einsum('rnj,rnc->jrc', lat_basis, values, preferred_element_type=jnp....  11.7 us
    pallas_call x1, Pallas kernels, inverse_legendre(): pl.pallas_call(functools.partial(inverse_kernel, factor=factor), grid=(ro...  10.2 us
    all_to_all x2, starting transfers between devices, round_trip(): lax.all_to_all(returning, 'lat', split_axis=1, concat_axis=1, tiled=True)  7.85 us
  transfers between devices with their start and end apart: 4, of which 4 were waited for; matrix products, arithmetic and copies ran while one was open for 15% of the time, Pallas kernels for 29%

profile of v11, /device:TPU:0, one launch (start us, length us, event | category | flops | bytes accessed | tf_op | source)
XLA Modules:
  0.0 217.2 jit_solution(16823353989996653469)
XLA Ops:
  1.2 5.7 %fusion.40 = (f32[192,16,256]{2,0,1:T(8,128)}, bf16[192,16,256]{2,0,1:T(8,128)(2,1)S(1)}) fusion(bf16[16,512,192]{1,2,0:T(8,128)(2,1)} %param.9, bf16[16,512,256]{2,1,0:T(8,128)(2,1)} %spec_ref.1, pred[16,512]{1,0:T(8,128)(4,1)S(1)} %get-tuple-element.21), kind=kOutput, calls=%fused_computation.84 | convolution fusion | flops 808976384 | bytes 12066816 | tf_op jit(solution)/shard_map/rnj,rnc->jrc/dot_general | solution.py:194
  7.7 6.0 %fusion.39 = (f32[192,16,256]{2,0,1:T(8,128)}, bf16[192,16,256]{2,0,1:T(8,128)(2,1)}) fusion(bf16[16,512,192]{1,2,0:T(8,128)(2,1)S(1)} %copy-done.5, pred[16,512]{1,0:T(8,128)(4,1)S(1)} %get-tuple-element.20, bf16[16,512,256]{2,1,0:T(8,128)(2,1)S(1)} %copy-done.4, pred[16,512]{1,0:T(8,128)(4,1)S(1)} %get-tuple-element.21), kind=kOutput, calls=%fused_computation.83 | convolution fusion | flops 817364992 | bytes 12075008 | tf_op jit(solution)/shard_map/rnj,rnc->jrc/dot_general | solution.py:194
  15.3 3.6 %fusion.14 = (f32[192,128]{1,0:T(8,128)S(1)}, f32[192,128]{1,0:T(8,128)S(1)}) fusion(f32[192,16,256]{2,0,1:T(8,128)} %get-tuple-element.22, f32[16]{0:T(128)S(1)} %compare_select_fusion, f32[16]{0:T(128)S(1)} %get-tuple-element.13, f32[192,16,256]{2,0,1:T(8,128)} %get-tuple-element.24), kind=kLoop, calls=%fused_computation.24 | loop fusion | flops 4669440 | bytes 6488192 | tf_op jit(solution)/shard_map/reduce_sum | solution.py:198
  19.9 1.9 reduce
  21.8 2.5 %reshape.131 = bf16[32,2,12480]{2,1,0:T(2,128)(2,1)} reshape(bf16[32,24960]{1,0:T(8,128)(2,1)S(1)} %reduce) | data formatting | bytes 3194880
  24.4 7.4 %all-to-all-start = ((bf16[32,2,12480]{2,1,0:T(2,128)(2,1)}), bf16[32,2,12480]{2,1,0:T(2,128)(2,1)}, u32[]{:S(2)}, u32[]{:S(2)}) async-start(bf16[32,2,12480]{2,1,0:T(2,128)(2,1)} %reshape.131), calls=%async_computation | async-start | bytes 3211264 | tf_op jit(solution)/shard_map/all_to_all | solution.py:222
  31.8 2.0 copy.38
  35.1 13.5 %cosine_convert_fusion = (bf16[512,1536]{1,0:T(8,128)(2,1)S(1)}, bf16[512,1536]{1,0:T(8,128)(2,1)S(1)}) fusion(s32[512]{0:T(512)S(1)} %fusion.32), kind=kLoop, calls=%fused_computation.10 | loop fusion | flops 8650752 | bytes 3147776 | tf_op jit(solution)/shard_map/convert
  48.7 1.9 pad_maximum_fusion.table_ref
  50.5 19.6 %all-to-all-done = bf16[32,2,12480]{2,1,0:T(2,128)(2,1)} async-done(((bf16[32,2,12480]{2,1,0:T(2,128)(2,1)}), bf16[32,2,12480]{2,1,0:T(2,128)(2,1)}, u32[]{:S(2)}, u32[]{:S(2)}) %all-to-all-start) | async-done | bytes 1597472 | tf_op jit(solution)/shard_map/all_to_all | solution.py:222
  70.1 8.9 %reshape.132 = bf16[32,1,24960]{2,1,0:T(2,128)(2,1)S(1)} reshape(bf16[32,2,12480]{2,1,0:T(2,128)(2,1)} %all-to-all-done) | data formatting | bytes 3194880
  80.4 4.1 %all-to-all-start.2 = ((bf16[32,6,16,256]{3,2,1,0:T(8,128)(2,1)}), bf16[32,6,16,256]{3,2,1,0:T(8,128)(2,1)S(1)}, u32[]{:S(2)}, u32[]{:S(2)}) async-start(bf16[32,6,16,256]{3,2,1,0:T(8,128)(2,1)} %bitcast.35), calls=%async_computation.2 | async-start | bytes 3145728 | tf_op jit(solution)/shard_map/all_to_all | solution.py:243
  84.6 1.6 slice.40
  86.6 31.4 %shard_map.82 = bf16[6,512,256]{2,1,0:T(8,128)(2,1)S(1)} custom-call(f32[6]{0:T(128)S(1)} %multiply_cosine_fusion.3.weight_ref, bf16[32,6,16,256]{3,2,1,0:T(8,128)(2,1)S(1)} %bitcast.27, f32[1,128]{1,0:T(1,128)S(1)} %bitcast.29, bf16[128,1024]{1,0:T(8,128)(2,1)S(1)} %copy-done, f32[1,1024]{1,0:T(1,128)S(1)} %bitcast.31, bf16[1024,128]{1,0:T(8,128)(2,1)S(1)} %copy-done.1, ...), custom_call_target="tpu_custom_call" | custom-call | flops 9663676416 | bytes 6291456 | tf_op jit(solution)/shard_map/pallas_call | solution.py:91
  119.3 2.8 %all-to-all-done.2.rows_ref = bf16[32,6,16,256]{3,2,1,0:T(8,128)(2,1)S(1)} async-done(((bf16[32,6,16,256]{3,2,1,0:T(8,128)(2,1)}), bf16[32,6,16,256]{3,2,1,0:T(8,128)(2,1)S(1)}, u32[]{:S(2)}, u32[]{:S(2)}) %all-to-all-start.2) | async-done | bytes 1572896 | tf_op jit(solution)/shard_map/all_to_all | solution.py:243
  122.1 3.9 %all-to-all-start.1 = ((bf16[6,32,16,256]{3,2,0,1:T(8,128)(2,1)}), bf16[6,32,16,256]{3,2,0,1:T(8,128)(2,1)}, u32[]{:S(2)}, u32[]{:S(2)}) async-start(bf16[6,32,16,256]{3,2,0,1:T(8,128)(2,1)} %copy.39), calls=%async_computation.1 | async-start | bytes 3145728 | tf_op jit(solution)/shard_map/all_to_all | solution.py:236
  126.0 31.4 %shard_map.83 = bf16[6,512,256]{2,1,0:T(8,128)(2,1)S(1)} custom-call(f32[6]{0:T(128)S(1)} %multiply_cosine_fusion.2.weight_ref, bf16[32,6,16,256]{3,2,1,0:T(8,128)(2,1)S(1)} %all-to-all-done.2.rows_ref, f32[1,128]{1,0:T(1,128)S(1)} %bitcast.30, bf16[128,1024]{1,0:T(8,128)(2,1)S(1)} %copy-done, f32[1,1024]{1,0:T(1,128)S(1)} %bitcast.32, ...), custom_call_target="tpu_custom_call" | custom-call | flops 9663676416 | bytes 6291456 | tf_op jit(solution)/shard_map/pallas_call | solution.py:91
  158.8 4.9 %all-to-all-done.1 = bf16[6,32,16,256]{3,2,0,1:T(8,128)(2,1)} async-done(((bf16[6,32,16,256]{3,2,0,1:T(8,128)(2,1)}), bf16[6,32,16,256]{3,2,0,1:T(8,128)(2,1)}, u32[]{:S(2)}, u32[]{:S(2)}) %all-to-all-start.1) | async-done | bytes 1572896 | tf_op jit(solution)/shard_map/all_to_all | solution.py:236
  163.7 4.0 %all-to-all-start.3 = ((bf16[6,32,16,256]{3,2,0,1:T(8,128)(2,1)}), bf16[6,32,16,256]{3,2,0,1:T(8,128)(2,1)S(1)}, u32[]{:S(2)}, u32[]{:S(2)}) async-start(bf16[6,32,16,256]{3,2,0,1:T(8,128)(2,1)} %copy.40), calls=%async_computation.3 | async-start | bytes 3145728 | tf_op jit(solution)/shard_map/all_to_all | solution.py:236
  167.7 6.0 %copy.41.basis_ref = bf16[16,512,192]{2,1,0:T(8,128)(2,1)} copy(bf16[16,512,192]{1,2,0:T(8,128)(2,1)} %param.9) | data formatting | bytes 6291456 | tf_op args[1]
  174.3 3.1 %copy.42.north_ref = bf16[16,192,256]{2,1,0:T(8,128)(2,1)} copy(bf16[16,192,256]{2,0,1:T(8,128)(2,1)} %bitcast.8) | data formatting | bytes 3145728 | tf_op jit(solution)/shard_map/reshape | solution.py:237
  177.4 27.9 %all-to-all-done.3 = bf16[6,32,16,256]{3,2,0,1:T(8,128)(2,1)S(1)} async-done(((bf16[6,32,16,256]{3,2,0,1:T(8,128)(2,1)}), bf16[6,32,16,256]{3,2,0,1:T(8,128)(2,1)S(1)}, u32[]{:S(2)}, u32[]{:S(2)}) %all-to-all-start.3) | async-done | bytes 1572896 | tf_op jit(solution)/shard_map/all_to_all | solution.py:236
  205.3 1.7 copy.43.south_ref
  207.0 10.2 %shard_map.84 = f32[16,512,256]{2,1,0:T(8,128)} custom-call(s32[16]{0:T(128)} %copy-done.7, bf16[16,512,192]{2,1,0:T(8,128)(2,1)} %copy.41.basis_ref, bf16[16,192,256]{2,1,0:T(8,128)(2,1)} %copy.42.north_ref, bf16[16,192,256]{2,1,0:T(8,128)(2,1)} %copy.43.south_ref, bf16[16,512,256]{2,1,0:T(8,128)(2,1)} %spec_ref.1, f32[1,256]{1,0:T(1,128)} %bitcast.38), custom_call_target="tpu_custom_call" | custom-call | flops 1610612736 | bytes 18874368 | tf_op jit(solution)/shard_map/pallas_call | solution.py:143
  (46 shorter events, 10.3 us)
Async XLA Ops:
  1.0 5.9 %copy-start.7 = (s32[16]{0:T(128)}, s32[16]{0:T(128)S(1)}, u32[]{:S(2)}) copy-start(s32[16]{0:T(128)S(1)} %get-tuple-element.14.wave_ref) | copy-start | bytes 196
  1.2 5.7 %copy-start.4 = (bf16[16,512,256]{2,1,0:T(8,128)(2,1)S(1)}, bf16[16,512,256]{2,1,0:T(8,128)(2,1)}, u32[]{:S(2)}) copy-start(bf16[16,512,256]{2,1,0:T(8,128)(2,1)} %spec_ref.1) | copy-start | bytes 12582916
  1.2 6.5 %copy-start.5 = (bf16[16,512,192]{1,2,0:T(8,128)(2,1)S(1)}, bf16[16,512,192]{1,2,0:T(8,128)(2,1)}, u32[]{:S(2)}) copy-start(bf16[16,512,192]{1,2,0:T(8,128)(2,1)} %param.9) | copy-start | bytes 9437188
  21.8 10.0 %copy-start.6 = (bf16[192,16,256]{2,0,1:T(8,128)(2,1)S(1)}, bf16[192,16,256]{2,0,1:T(8,128)(2,1)}, u32[]{:S(2)}) copy-start(bf16[192,16,256]{2,0,1:T(8,128)(2,1)} %get-tuple-element.23) | copy-start | bytes 4718596
  24.4 45.8 %all-to-all-start = ((bf16[32,2,12480]{2,1,0:T(2,128)(2,1)}), bf16[32,2,12480]{2,1,0:T(2,128)(2,1)}, u32[]{:S(2)}, u32[]{:S(2)}) async-start(bf16[32,2,12480]{2,1,0:T(2,128)(2,1)} %reshape.131), calls=%async_computation | async-start | bytes 3211264 | tf_op jit(solution)/shard_map/all_to_all | solution.py:222
  79.0 1.4 copy-start.8
  79.2 1.2 copy-start.3
  80.4 41.7 %all-to-all-start.2 = ((bf16[32,6,16,256]{3,2,1,0:T(8,128)(2,1)}), bf16[32,6,16,256]{3,2,1,0:T(8,128)(2,1)S(1)}, u32[]{:S(2)}, u32[]{:S(2)}) async-start(bf16[32,6,16,256]{3,2,1,0:T(8,128)(2,1)} %bitcast.35), calls=%async_computation.2 | async-start | bytes 3145728 | tf_op jit(solution)/shard_map/all_to_all | solution.py:243
  84.6 2.0 copy-start
  84.6 2.0 copy-start.1
  84.6 2.0 copy-start.2
  122.1 41.6 %all-to-all-start.1 = ((bf16[6,32,16,256]{3,2,0,1:T(8,128)(2,1)}), bf16[6,32,16,256]{3,2,0,1:T(8,128)(2,1)}, u32[]{:S(2)}, u32[]{:S(2)}) async-start(bf16[6,32,16,256]{3,2,0,1:T(8,128)(2,1)} %copy.39), calls=%async_computation.1 | async-start | bytes 3145728 | tf_op jit(solution)/shard_map/all_to_all | solution.py:236
  163.7 41.6 %all-to-all-start.3 = ((bf16[6,32,16,256]{3,2,0,1:T(8,128)(2,1)}), bf16[6,32,16,256]{3,2,0,1:T(8,128)(2,1)S(1)}, u32[]{:S(2)}, u32[]{:S(2)}) async-start(bf16[6,32,16,256]{3,2,0,1:T(8,128)(2,1)} %copy.40), calls=%async_computation.3 | async-start | bytes 3145728 | tf_op jit(solution)/shard_map/all_to_all | solution.py:236
  167.7 6.0 %copy-start.9 = (f32[128]{0:T(128)S(1)}, f32[128]{0:T(128)}, u32[]{:S(2)}) copy-start(f32[128]{0:T(128)} %param.15) | copy-start | bytes 1540

commit v12 on v10

--- a/solution.py
+++ b/solution.py
@@ -138,7 +138,7 @@
 def inverse_legendre(wave_own, lat_basis, north, south, spectral, damp_all, factor):
     rows, degrees, half_lat = lat_basis.shape
     width = spectral.shape[2]
-    block = 4 if rows % 4 == 0 else 1
+    block = 8 if rows % 8 == 0 else 1
     three = lambda shape: pl.BlockSpec(shape, lambda r: (r, 0, 0))
     return pl.pallas_call(
         functools.partial(inverse_kernel, factor=factor),

time: 204 us -> 204 us (level)
  no operation moved by 1% of the time
where the time goes in v12:
time: 204 us; the launch traced here: 203 us
  Pallas kernels  72.1 us (35%)
  waiting for transfers between devices  60.6 us (30%)
  other arithmetic  20.2 us (10%)
  starting transfers between devices  19.2 us (9%)
  local copies, waits for them, and re-layouts  19.1 us (9%)
  matrix products  10.9 us (5%)
    pallas_call x2, Pallas kernels, column_network(): pl.pallas_call(column_kernel, grid=(lat_local,), in_specs=[pl.BlockSpec(m...  62.6 us
    all_to_all x2, waiting for transfers between devices, round_trip(): lax.all_to_all(returning, 'lat', split_axis=1, concat_axis=1, tiled=True)  33 us
    all_to_all x1, waiting for transfers between devices, on_device(): lax.all_to_all(jnp.concatenate([out_north, slot], axis=1), 'lat', split_a...  24.5 us
    another operation x1, other arithmetic  13.5 us
    dot_general x2, matrix products, hemisphere(): jnp.einsum('rnj,rnc->jrc', lat_basis, values, preferred_element_type=jnp....  10.9 us
    pallas_call x1, Pallas kernels, inverse_legendre(): pl.pallas_call(functools.partial(inverse_kernel, factor=factor), grid=(ro...  9.54 us
    unnamed x21, local copies, waits for them, and re-layouts  8.62 us
    all_to_all x2, starting transfers between devices, round_trip(): lax.all_to_all(returning, 'lat', split_axis=1, concat_axis=1, tiled=True)  7.81 us
  transfers between devices with their start and end apart: 4, of which 4 were waited for; matrix products, arithmetic and copies ran while one was open for 15% of the time, Pallas kernels for 31%

profile of v12, /device:TPU:0, one launch (start us, length us, event | category | flops | bytes accessed | tf_op | source)
XLA Modules:
  0.0 203.0 jit_solution(7675559236138672109)
XLA Ops:
  1.2 4.6 %fusion.41 = (f32[192,16,256]{2,0,1:T(8,128)S(1)}, bf16[192,16,256]{2,0,1:T(8,128)(2,1)S(1)}) fusion(bf16[16,512,192]{1,2,0:T(8,128)(2,1)} %param.9, bf16[16,512,256]{2,1,0:T(8,128)(2,1)} %spec_ref.1, pred[16,512]{1,0:T(8,128)(4,1)S(1)} %get-tuple-element.22), kind=kOutput, calls=%fused_computation.84 | convolution fusion | flops 808976384 | bytes 12066816 | tf_op jit(solution)/shard_map/rnj,rnc->jrc/dot_general | solution.py:194
  6.5 6.3 %fusion.40 = (f32[192,16,256]{2,0,1:T(8,128)S(1)}, bf16[192,16,256]{2,0,1:T(8,128)(2,1)S(1)}) fusion(bf16[16,512,192]{1,2,0:T(8,128)(2,1)S(1)} %copy-done.6, pred[16,512]{1,0:T(8,128)(4,1)S(1)} %get-tuple-element.23, bf16[16,512,256]{2,1,0:T(8,128)(2,1)S(1)} %copy-done.5, pred[16,512]{1,0:T(8,128)(4,1)S(1)} %get-tuple-element.22), kind=kOutput, calls=%fused_computation.83 | convolution fusion | flops 817364992 | bytes 12075008 | tf_op jit(solution)/shard_map/rnj,rnc->jrc/dot_general | solution.py:194
  14.8 1.4 pad_maximum_fusion.1
  16.2 7.3 %all-to-all-start = ((bf16[32,7,16,256]{3,2,1,0:T(8,128)(2,1)}), bf16[32,7,16,256]{3,2,1,0:T(8,128)(2,1)S(1)}, u32[]{:S(2)}, u32[]{:S(2)}) async-start(bf16[32,7,16,256]{3,2,1,0:T(8,128)(2,1)} %pad_maximum_fusion.1), calls=%async_computation | async-start | bytes 3670016 | tf_op jit(solution)/shard_map/all_to_all | solution.py:221
  23.5 2.0 copy.21
  26.8 13.5 %cosine_convert_fusion = (bf16[512,1536]{1,0:T(8,128)(2,1)S(1)}, bf16[512,1536]{1,0:T(8,128)(2,1)S(1)}) fusion(s32[512]{0:T(512)S(1)} %fusion.33), kind=kLoop, calls=%fused_computation.10 | loop fusion | flops 8650752 | bytes 3147776 | tf_op jit(solution)/shard_map/convert.1
  40.4 1.9 pad_maximum_fusion.table_ref
  42.2 24.5 %all-to-all-done.rows_ref = bf16[32,7,16,256]{3,2,1,0:T(8,128)(2,1)S(1)} async-done(((bf16[32,7,16,256]{3,2,1,0:T(8,128)(2,1)}), bf16[32,7,16,256]{3,2,1,0:T(8,128)(2,1)S(1)}, u32[]{:S(2)}, u32[]{:S(2)}) %all-to-all-start) | async-done | bytes 1835040 | tf_op jit(solution)/shard_map/all_to_all | solution.py:221
  66.8 4.0 %all-to-all-start.2 = ((bf16[32,6,16,256]{3,2,1,0:T(8,128)(2,1)}), bf16[32,6,16,256]{3,2,1,0:T(8,128)(2,1)S(1)}, u32[]{:S(2)}, u32[]{:S(2)}) async-start(bf16[32,6,16,256]{3,2,1,0:T(8,128)(2,1)} %bitcast.30), calls=%async_computation.2 | async-start | bytes 3145728 | tf_op jit(solution)/shard_map/all_to_all | solution.py:241
  70.9 0.9 copy-done
  71.9 0.9 copy-done.2
  72.8 31.3 %shard_map.82 = bf16[6,512,256]{2,1,0:T(8,128)(2,1)S(1)} custom-call(f32[6]{0:T(128)S(1)} %multiply_cosine_fusion.3.weight_ref, bf16[32,7,16,256]{3,2,1,0:T(8,128)(2,1)S(1)} %all-to-all-done.rows_ref, f32[1,128]{1,0:T(1,128)S(1)} %bitcast.26, bf16[128,1024]{1,0:T(8,128)(2,1)S(1)} %copy-done, f32[1,1024]{1,0:T(1,128)S(1)} %bitcast.28, ...), custom_call_target="tpu_custom_call" | custom-call | flops 9663676416 | bytes 6291456 | tf_op jit(solution)/shard_map/pallas_call | solution.py:91
  104.2 1.3 copy.23
  105.5 3.1 %all-to-all-done.2.rows_ref = bf16[32,6,16,256]{3,2,1,0:T(8,128)(2,1)S(1)} async-done(((bf16[32,6,16,256]{3,2,1,0:T(8,128)(2,1)}), bf16[32,6,16,256]{3,2,1,0:T(8,128)(2,1)S(1)}, u32[]{:S(2)}, u32[]{:S(2)}) %all-to-all-start.2) | async-done | bytes 1572896 | tf_op jit(solution)/shard_map/all_to_all | solution.py:241
  108.6 4.1 %all-to-all-start.1 = ((bf16[6,32,16,256]{3,2,0,1:T(8,128)(2,1)}), bf16[6,32,16,256]{3,2,0,1:T(8,128)(2,1)}, u32[]{:S(2)}, u32[]{:S(2)}) async-start(bf16[6,32,16,256]{3,2,0,1:T(8,128)(2,1)} %copy.23), calls=%async_computation.1 | async-start | bytes 3145728 | tf_op jit(solution)/shard_map/all_to_all | solution.py:234
  112.7 31.2 %shard_map.83 = bf16[6,512,256]{2,1,0:T(8,128)(2,1)S(1)} custom-call(f32[6]{0:T(128)S(1)} %multiply_cosine_fusion.2.weight_ref, bf16[32,6,16,256]{3,2,1,0:T(8,128)(2,1)S(1)} %all-to-all-done.2.rows_ref, f32[1,128]{1,0:T(1,128)S(1)} %bitcast.27, bf16[128,1024]{1,0:T(8,128)(2,1)S(1)} %copy-done.1, f32[1,1024]{1,0:T(1,128)S(1)} %bitcast.29, ...), custom_call_target="tpu_custom_call" | custom-call | flops 9663676416 | bytes 6291456 | tf_op jit(solution)/shard_map/pallas_call | solution.py:91
  144.0 1.4 copy.24
  145.3 4.9 %all-to-all-done.1 = bf16[6,32,16,256]{3,2,0,1:T(8,128)(2,1)} async-done(((bf16[6,32,16,256]{3,2,0,1:T(8,128)(2,1)}), bf16[6,32,16,256]{3,2,0,1:T(8,128)(2,1)}, u32[]{:S(2)}, u32[]{:S(2)}) %all-to-all-start.1) | async-done | bytes 1572896 | tf_op jit(solution)/shard_map/all_to_all | solution.py:234
  150.2 3.7 %all-to-all-start.3 = ((bf16[6,32,16,256]{3,2,0,1:T(8,128)(2,1)}), bf16[6,32,16,256]{3,2,0,1:T(8,128)(2,1)S(1)}, u32[]{:S(2)}, u32[]{:S(2)}) async-start(bf16[6,32,16,256]{3,2,0,1:T(8,128)(2,1)} %copy.24), calls=%async_computation.3 | async-start | bytes 3145728 | tf_op jit(solution)/shard_map/all_to_all | solution.py:234
  154.0 6.0 %copy.25.basis_ref = bf16[16,512,192]{2,1,0:T(8,128)(2,1)} copy(bf16[16,512,192]{1,2,0:T(8,128)(2,1)} %param.9) | data formatting | bytes 6291456 | tf_op args[1]
  160.5 3.1 %copy.26.north_ref = bf16[16,192,256]{2,1,0:T(8,128)(2,1)} copy(bf16[16,192,256]{2,0,1:T(8,128)(2,1)} %bitcast.10) | data formatting | bytes 3145728 | tf_op jit(solution)/shard_map/reshape | solution.py:235
  163.7 28.1 %all-to-all-done.3 = bf16[6,32,16,256]{3,2,0,1:T(8,128)(2,1)S(1)} async-done(((bf16[6,32,16,256]{3,2,0,1:T(8,128)(2,1)}), bf16[6,32,16,256]{3,2,0,1:T(8,128)(2,1)S(1)}, u32[]{:S(2)}, u32[]{:S(2)}) %all-to-all-start.3) | async-done | bytes 1572896 | tf_op jit(solution)/shard_map/all_to_all | solution.py:234
  191.7 1.7 copy.27.south_ref
  193.4 9.5 %shard_map.84 = f32[16,512,256]{2,1,0:T(8,128)} custom-call(s32[16]{0:T(128)} %copy-done.7, bf16[16,512,192]{2,1,0:T(8,128)(2,1)} %copy.25.basis_ref, bf16[16,192,256]{2,1,0:T(8,128)(2,1)} %copy.26.north_ref, bf16[16,192,256]{2,1,0:T(8,128)(2,1)} %copy.27.south_ref, bf16[16,512,256]{2,1,0:T(8,128)(2,1)} %spec_ref.1, f32[1,256]{1,0:T(1,128)} %bitcast.33), custom_call_target="tpu_custom_call" | custom-call | flops 1610612736 | bytes 18874368 | tf_op jit(solution)/shard_map/pallas_call | solution.py:143
  (45 shorter events, 5.2 us)
Async XLA Ops:
  1.0 4.8 %copy-start.7 = (s32[16]{0:T(128)}, s32[16]{0:T(128)S(1)}, u32[]{:S(2)}) copy-start(s32[16]{0:T(128)S(1)} %get-tuple-element.16.wave_ref) | copy-start | bytes 196
  1.2 4.6 %copy-start.5 = (bf16[16,512,256]{2,1,0:T(8,128)(2,1)S(1)}, bf16[16,512,256]{2,1,0:T(8,128)(2,1)}, u32[]{:S(2)}) copy-start(bf16[16,512,256]{2,1,0:T(8,128)(2,1)} %spec_ref.1) | copy-start | bytes 12582916
  1.2 5.3 %copy-start.6 = (bf16[16,512,192]{1,2,0:T(8,128)(2,1)S(1)}, bf16[16,512,192]{1,2,0:T(8,128)(2,1)}, u32[]{:S(2)}) copy-start(bf16[16,512,192]{1,2,0:T(8,128)(2,1)} %param.9) | copy-start | bytes 9437188
  16.2 50.5 %all-to-all-start = ((bf16[32,7,16,256]{3,2,1,0:T(8,128)(2,1)}), bf16[32,7,16,256]{3,2,1,0:T(8,128)(2,1)S(1)}, u32[]{:S(2)}, u32[]{:S(2)}) async-start(bf16[32,7,16,256]{3,2,1,0:T(8,128)(2,1)} %pad_maximum_fusion.1), calls=%async_computation | async-start | bytes 3670016 | tf_op jit(solution)/shard_map/all_to_all | solution.py:221
  40.3 26.5 %copy-start.8 = (f32[128]{0:T(128)S(1)}, f32[128]{0:T(128)}, u32[]{:S(2)}) copy-start(f32[128]{0:T(128)} %param.14) | copy-start | bytes 1540
  42.2 28.7 %copy-start.4 = (f32[1024]{0:T(1024)S(1)}, f32[1024]{0:T(1024)}, u32[]{:S(2)}) copy-start(f32[1024]{0:T(1024)} %param.12) | copy-start | bytes 12292
  66.8 41.8 %all-to-all-start.2 = ((bf16[32,6,16,256]{3,2,1,0:T(8,128)(2,1)}), bf16[32,6,16,256]{3,2,1,0:T(8,128)(2,1)S(1)}, u32[]{:S(2)}, u32[]{:S(2)}) async-start(bf16[32,6,16,256]{3,2,1,0:T(8,128)(2,1)} %bitcast.30), calls=%async_computation.2 | async-start | bytes 3145728 | tf_op jit(solution)/shard_map/all_to_all | solution.py:241
  70.9 1.0 copy-start
  71.9 0.9 copy-start.2
  104.2 8.6 %copy-start.1 = (bf16[128,1024]{1,0:T(8,128)(2,1)S(1)}, bf16[128,1024]{1,0:T(8,128)(2,1)}, u32[]{:S(2)}) copy-start(bf16[128,1024]{1,0:T(8,128)(2,1)} %in_w_ref.3) | copy-start | bytes 786436
  104.2 8.6 %copy-start.3 = (bf16[1024,128]{1,0:T(8,128)(2,1)S(1)}, bf16[1024,128]{1,0:T(8,128)(2,1)}, u32[]{:S(2)}) copy-start(bf16[1024,128]{1,0:T(8,128)(2,1)} %out_w_ref.3) | copy-start | bytes 786436
  108.6 41.7 %all-to-all-start.1 = ((bf16[6,32,16,256]{3,2,0,1:T(8,128)(2,1)}), bf16[6,32,16,256]{3,2,0,1:T(8,128)(2,1)}, u32[]{:S(2)}, u32[]{:S(2)}) async-start(bf16[6,32,16,256]{3,2,0,1:T(8,128)(2,1)} %copy.23), calls=%async_computation.1 | async-start | bytes 3145728 | tf_op jit(solution)/shard_map/all_to_all | solution.py:234
  150.2 41.5 %all-to-all-start.3 = ((bf16[6,32,16,256]{3,2,0,1:T(8,128)(2,1)}), bf16[6,32,16,256]{3,2,0,1:T(8,128)(2,1)S(1)}, u32[]{:S(2)}, u32[]{:S(2)}) async-start(bf16[6,32,16,256]{3,2,0,1:T(8,128)(2,1)} %copy.24), calls=%async_computation.3 | async-start | bytes 3145728 | tf_op jit(solution)/shard_map/all_to_all | solution.py:234
  154.0 6.0 %copy-start.9 = (f32[128]{0:T(128)S(1)}, f32[128]{0:T(128)}, u32[]{:S(2)}) copy-start(f32[128]{0:T(128)} %param.15) | copy-start | bytes 1540

commit v13 on v12

--- a/solution.py
+++ b/solution.py
@@ -194,6 +194,7 @@
         fourier = jnp.einsum(
             "rnj,rnc->jrc", lat_basis, values, preferred_element_type=jnp.float32
         ).astype(jnp.bfloat16)
+        fourier = lax.optimization_barrier(fourier)
         wide = fourier.astype(jnp.float32)
         per_lat = jnp.sum(
             real_coef[None, :, None] * wide[:, :, :chan_count] ** 2

time: 204 us -> 203 us (level)
  matrix products: 10.9 us -> 8.48 us
    optimization_barrier x0 -> x2, local copies, waits for them, and re-layouts: none -> 2.9 us  [hemisphere(): fourier = lax.optimization_barrier(fourier)]
    convert_element_type x2 -> x0, local copies, waits for them, and re-layouts: 2.89 us -> none  [hemisphere(): fourier = jnp.einsum('rnj,rnc->jrc', lat_basis, values, preferred_element...]
    dot_general x2, matrix products: 10.9 us -> 8.48 us  [hemisphere(): jnp.einsum('rnj,rnc->jrc', lat_basis, values, preferred_element_type=jnp....]
where the time goes in v13:
time: 203 us
  Pallas kernels  72.1 us (36%)
  waiting for transfers between devices  60.3 us (30%)
  other arithmetic  20.9 us (10%)
  local copies, waits for them, and re-layouts  20.6 us (10%)
  starting transfers between devices  19.4 us (10%)
  matrix products  8.48 us (4%)
    pallas_call x2, Pallas kernels, column_network(): pl.pallas_call(column_kernel, grid=(lat_local,), in_specs=[pl.BlockSpec(m...  62.6 us
    all_to_all x2, waiting for transfers between devices, round_trip(): lax.all_to_all(returning, 'lat', split_axis=1, concat_axis=1, tiled=True)  32.9 us
    all_to_all x1, waiting for transfers between devices, on_device(): lax.all_to_all(jnp.concatenate([out_north, slot], axis=1), 'lat', split_a...  24.5 us
    another operation x1, other arithmetic  13.5 us
    unnamed x21, local copies, waits for them, and re-layouts  10 us
    pallas_call x1, Pallas kernels, inverse_legendre(): pl.pallas_call(functools.partial(inverse_kernel, factor=factor), grid=(ro...  9.54 us
    dot_general x2, matrix products, hemisphere(): jnp.einsum('rnj,rnc->jrc', lat_basis, values, preferred_element_type=jnp....  8.48 us
    all_to_all x2, starting transfers between devices, round_trip(): lax.all_to_all(returning, 'lat', split_axis=1, concat_axis=1, tiled=True)  7.85 us
  transfers between devices with their start and end apart: 4, of which 4 were waited for; matrix products, arithmetic and copies ran while one was open for 15% of the time, Pallas kernels for 31%

profile of v13, /device:TPU:0, one launch (start us, length us, event | category | flops | bytes accessed | tf_op | source)
XLA Modules:
  0.0 202.7 jit_solution(1564541801358907911)
XLA Ops:
  1.2 4.1 %fusion.21 = bf16[192,16,256]{2,0,1:T(8,128)(2,1)S(1)} fusion(bf16[16,512,192]{1,2,0:T(8,128)(2,1)} %param.9, bf16[16,512,256]{2,1,0:T(8,128)(2,1)} %spec_ref.1, pred[16,512]{1,0:T(8,128)(4,1)S(1)} %get-tuple-element.22), kind=kOutput, calls=%fused_computation.33 | convolution fusion | flops 808189952 | bytes 8921088 | tf_op jit(solution)/shard_map/rnj,rnc->jrc/dot_general | solution.py:194
  7.2 1.5 copy-done.5
  8.7 4.4 %fusion.20 = bf16[192,16,256]{2,0,1:T(8,128)(2,1)S(1)} fusion(bf16[16,512,192]{1,2,0:T(8,128)(2,1)S(1)} %copy-done.6, pred[16,512]{1,0:T(8,128)(4,1)S(1)} %get-tuple-element.23, bf16[16,512,256]{2,1,0:T(8,128)(2,1)S(1)} %copy-done.5, pred[16,512]{1,0:T(8,128)(4,1)S(1)} %get-tuple-element.22), kind=kOutput, calls=%fused_computation.32 | convolution fusion | flops 816578560 | bytes 8929280 | tf_op jit(solution)/shard_map/rnj,rnc->jrc/dot_general | solution.py:194
  14.4 1.4 pad_maximum_fusion.1
  15.9 7.3 %all-to-all-start = ((bf16[32,7,16,256]{3,2,1,0:T(8,128)(2,1)}), bf16[32,7,16,256]{3,2,1,0:T(8,128)(2,1)S(1)}, u32[]{:S(2)}, u32[]{:S(2)}) async-start(bf16[32,7,16,256]{3,2,1,0:T(8,128)(2,1)} %pad_maximum_fusion.1), calls=%async_computation | async-start | bytes 3670016 | tf_op jit(solution)/shard_map/all_to_all | solution.py:222
  23.2 2.0 copy.21
  26.5 13.5 %cosine_convert_fusion = (bf16[512,1536]{1,0:T(8,128)(2,1)S(1)}, bf16[512,1536]{1,0:T(8,128)(2,1)S(1)}) fusion(s32[512]{0:T(512)S(1)} %fusion.33), kind=kLoop, calls=%fused_computation.10 | loop fusion | flops 8650752 | bytes 3147776 | tf_op jit(solution)/shard_map/convert.1
  40.0 1.9 pad_maximum_fusion.table_ref
  41.9 24.5 %all-to-all-done.rows_ref = bf16[32,7,16,256]{3,2,1,0:T(8,128)(2,1)S(1)} async-done(((bf16[32,7,16,256]{3,2,1,0:T(8,128)(2,1)}), bf16[32,7,16,256]{3,2,1,0:T(8,128)(2,1)S(1)}, u32[]{:S(2)}, u32[]{:S(2)}) %all-to-all-start) | async-done | bytes 1835040 | tf_op jit(solution)/shard_map/all_to_all | solution.py:222
  66.5 4.2 %all-to-all-start.2 = ((bf16[32,6,16,256]{3,2,1,0:T(8,128)(2,1)}), bf16[32,6,16,256]{3,2,1,0:T(8,128)(2,1)S(1)}, u32[]{:S(2)}, u32[]{:S(2)}) async-start(bf16[32,6,16,256]{3,2,1,0:T(8,128)(2,1)} %bitcast.31), calls=%async_computation.2 | async-start | bytes 3145728 | tf_op jit(solution)/shard_map/all_to_all | solution.py:242
  71.7 0.9 copy-done.2
  72.7 31.3 %shard_map.82 = bf16[6,512,256]{2,1,0:T(8,128)(2,1)S(1)} custom-call(f32[6]{0:T(128)S(1)} %multiply_cosine_fusion.3.weight_ref, bf16[32,7,16,256]{3,2,1,0:T(8,128)(2,1)S(1)} %all-to-all-done.rows_ref, f32[1,128]{1,0:T(1,128)S(1)} %bitcast.26, bf16[128,1024]{1,0:T(8,128)(2,1)S(1)} %copy-done, f32[1,1024]{1,0:T(1,128)S(1)} %bitcast.28, ...), custom_call_target="tpu_custom_call" | custom-call | flops 9663676416 | bytes 6291456 | tf_op jit(solution)/shard_map/pallas_call | solution.py:91
  104.0 1.3 copy.23
  105.4 2.9 %all-to-all-done.2.rows_ref = bf16[32,6,16,256]{3,2,1,0:T(8,128)(2,1)S(1)} async-done(((bf16[32,6,16,256]{3,2,1,0:T(8,128)(2,1)}), bf16[32,6,16,256]{3,2,1,0:T(8,128)(2,1)S(1)}, u32[]{:S(2)}, u32[]{:S(2)}) %all-to-all-start.2) | async-done | bytes 1572896 | tf_op jit(solution)/shard_map/all_to_all | solution.py:242
  108.3 3.9 %all-to-all-start.1 = ((bf16[6,32,16,256]{3,2,0,1:T(8,128)(2,1)}), bf16[6,32,16,256]{3,2,0,1:T(8,128)(2,1)}, u32[]{:S(2)}, u32[]{:S(2)}) async-start(bf16[6,32,16,256]{3,2,0,1:T(8,128)(2,1)} %copy.23), calls=%async_computation.1 | async-start | bytes 3145728 | tf_op jit(solution)/shard_map/all_to_all | solution.py:235
  112.2 31.2 %shard_map.83 = bf16[6,512,256]{2,1,0:T(8,128)(2,1)S(1)} custom-call(f32[6]{0:T(128)S(1)} %multiply_cosine_fusion.2.weight_ref, bf16[32,6,16,256]{3,2,1,0:T(8,128)(2,1)S(1)} %all-to-all-done.2.rows_ref, f32[1,128]{1,0:T(1,128)S(1)} %bitcast.27, bf16[128,1024]{1,0:T(8,128)(2,1)S(1)} %copy-done.1, f32[1,1024]{1,0:T(1,128)S(1)} %bitcast.29, ...), custom_call_target="tpu_custom_call" | custom-call | flops 9663676416 | bytes 6291456 | tf_op jit(solution)/shard_map/pallas_call | solution.py:91
  143.5 1.4 copy.24
  144.8 5.1 %all-to-all-done.1 = bf16[6,32,16,256]{3,2,0,1:T(8,128)(2,1)} async-done(((bf16[6,32,16,256]{3,2,0,1:T(8,128)(2,1)}), bf16[6,32,16,256]{3,2,0,1:T(8,128)(2,1)}, u32[]{:S(2)}, u32[]{:S(2)}) %all-to-all-start.1) | async-done | bytes 1572896 | tf_op jit(solution)/shard_map/all_to_all | solution.py:235
  149.9 4.0 %all-to-all-start.3 = ((bf16[6,32,16,256]{3,2,0,1:T(8,128)(2,1)}), bf16[6,32,16,256]{3,2,0,1:T(8,128)(2,1)S(1)}, u32[]{:S(2)}, u32[]{:S(2)}) async-start(bf16[6,32,16,256]{3,2,0,1:T(8,128)(2,1)} %copy.24), calls=%async_computation.3 | async-start | bytes 3145728 | tf_op jit(solution)/shard_map/all_to_all | solution.py:235
  153.9 6.0 %copy.25.basis_ref = bf16[16,512,192]{2,1,0:T(8,128)(2,1)} copy(bf16[16,512,192]{1,2,0:T(8,128)(2,1)} %param.9) | data formatting | bytes 6291456 | tf_op args[1]
  160.5 3.1 %copy.26.north_ref = bf16[16,192,256]{2,1,0:T(8,128)(2,1)} copy(bf16[16,192,256]{2,0,1:T(8,128)(2,1)} %bitcast.10) | data formatting | bytes 3145728 | tf_op jit(solution)/shard_map/reshape | solution.py:236
  163.6 27.9 %all-to-all-done.3 = bf16[6,32,16,256]{3,2,0,1:T(8,128)(2,1)S(1)} async-done(((bf16[6,32,16,256]{3,2,0,1:T(8,128)(2,1)}), bf16[6,32,16,256]{3,2,0,1:T(8,128)(2,1)S(1)}, u32[]{:S(2)}, u32[]{:S(2)}) %all-to-all-start.3) | async-done | bytes 1572896 | tf_op jit(solution)/shard_map/all_to_all | solution.py:235
  191.4 1.7 copy.27.south_ref
  193.2 9.5 %shard_map.84 = f32[16,512,256]{2,1,0:T(8,128)} custom-call(s32[16]{0:T(128)} %copy-done.7, bf16[16,512,192]{2,1,0:T(8,128)(2,1)} %copy.25.basis_ref, bf16[16,192,256]{2,1,0:T(8,128)(2,1)} %copy.26.north_ref, bf16[16,192,256]{2,1,0:T(8,128)(2,1)} %copy.27.south_ref, bf16[16,512,256]{2,1,0:T(8,128)(2,1)} %spec_ref.1, f32[1,256]{1,0:T(1,128)} %bitcast.33), custom_call_target="tpu_custom_call" | custom-call | flops 1610612736 | bytes 18874368 | tf_op jit(solution)/shard_map/pallas_call | solution.py:143
  (47 shorter events, 6.7 us)
Async XLA Ops:
  1.1 4.2 %copy-start.7 = (s32[16]{0:T(128)}, s32[16]{0:T(128)S(1)}, u32[]{:S(2)}) copy-start(s32[16]{0:T(128)S(1)} %get-tuple-element.16.wave_ref) | copy-start | bytes 196
  5.3 1.9 copy-start.6
  6.2 2.5 %copy-start.5 = (bf16[16,512,256]{2,1,0:T(8,128)(2,1)S(1)}, bf16[16,512,256]{2,1,0:T(8,128)(2,1)}, u32[]{:S(2)}) copy-start(bf16[16,512,256]{2,1,0:T(8,128)(2,1)} %spec_ref.1) | copy-start | bytes 12582916
  15.9 50.5 %all-to-all-start = ((bf16[32,7,16,256]{3,2,1,0:T(8,128)(2,1)}), bf16[32,7,16,256]{3,2,1,0:T(8,128)(2,1)S(1)}, u32[]{:S(2)}, u32[]{:S(2)}) async-start(bf16[32,7,16,256]{3,2,1,0:T(8,128)(2,1)} %pad_maximum_fusion.1), calls=%async_computation | async-start | bytes 3670016 | tf_op jit(solution)/shard_map/all_to_all | solution.py:222
  40.0 26.5 %copy-start.8 = (f32[128]{0:T(128)S(1)}, f32[128]{0:T(128)}, u32[]{:S(2)}) copy-start(f32[128]{0:T(128)} %param.14) | copy-start | bytes 1540
  41.9 28.9 %copy-start.4 = (f32[1024]{0:T(1024)S(1)}, f32[1024]{0:T(1024)}, u32[]{:S(2)}) copy-start(f32[1024]{0:T(1024)} %param.12) | copy-start | bytes 12292
  66.5 41.8 %all-to-all-start.2 = ((bf16[32,6,16,256]{3,2,1,0:T(8,128)(2,1)}), bf16[32,6,16,256]{3,2,1,0:T(8,128)(2,1)S(1)}, u32[]{:S(2)}, u32[]{:S(2)}) async-start(bf16[32,6,16,256]{3,2,1,0:T(8,128)(2,1)} %bitcast.31), calls=%async_computation.2 | async-start | bytes 3145728 | tf_op jit(solution)/shard_map/all_to_all | solution.py:242
  70.8 1.0 copy-start
  71.7 0.9 copy-start.2
  104.0 8.2 %copy-start.1 = (bf16[128,1024]{1,0:T(8,128)(2,1)S(1)}, bf16[128,1024]{1,0:T(8,128)(2,1)}, u32[]{:S(2)}) copy-start(bf16[128,1024]{1,0:T(8,128)(2,1)} %in_w_ref.3) | copy-start | bytes 786436
  104.0 8.2 %copy-start.3 = (bf16[1024,128]{1,0:T(8,128)(2,1)S(1)}, bf16[1024,128]{1,0:T(8,128)(2,1)}, u32[]{:S(2)}) copy-start(bf16[1024,128]{1,0:T(8,128)(2,1)} %out_w_ref.3) | copy-start | bytes 786436
  108.3 41.6 %all-to-all-start.1 = ((bf16[6,32,16,256]{3,2,0,1:T(8,128)(2,1)}), bf16[6,32,16,256]{3,2,0,1:T(8,128)(2,1)}, u32[]{:S(2)}, u32[]{:S(2)}) async-start(bf16[6,32,16,256]{3,2,0,1:T(8,128)(2,1)} %copy.23), calls=%async_computation.1 | async-start | bytes 3145728 | tf_op jit(solution)/shard_map/all_to_all | solution.py:235
  149.9 41.6 %all-to-all-start.3 = ((bf16[6,32,16,256]{3,2,0,1:T(8,128)(2,1)}), bf16[6,32,16,256]{3,2,0,1:T(8,128)(2,1)S(1)}, u32[]{:S(2)}, u32[]{:S(2)}) async-start(bf16[6,32,16,256]{3,2,0,1:T(8,128)(2,1)} %copy.24), calls=%async_computation.3 | async-start | bytes 3145728 | tf_op jit(solution)/shard_map/all_to_all | solution.py:235
  153.9 6.0 %copy-start.9 = (f32[128]{0:T(128)S(1)}, f32[128]{0:T(128)}, u32[]{:S(2)}) copy-start(f32[128]{0:T(128)} %param.15) | copy-start | bytes 1540

commit v14 on v7

--- a/solution.py
+++ b/solution.py
@@ -80,7 +80,8 @@
 def column_network(
     lat_w, rows_in, col_scale, in_weight, in_bias, out_weight, wave_table
 ):
-    sources, lat_local, rows_per, width = rows_in.shape
+    sources, _, rows_per, width = rows_in.shape
+    lat_local = lat_w.shape[0]
     chan = width // 2
     waves = sources * rows_per
     nlon = wave_table.shape[1]
@@ -137,7 +138,7 @@
 def inverse_legendre(wave_own, lat_basis, north, south, spectral, damp_all, factor):
     rows, degrees, half_lat = lat_basis.shape
     width = spectral.shape[2]
-    block = 4 if rows % 4 == 0 else 1
+    block = 8 if rows % 8 == 0 else 1
     three = lambda shape: pl.BlockSpec(shape, lambda r: (r, 0, 0))
     return pl.pallas_call(
         functools.partial(inverse_kernel, factor=factor),
@@ -203,8 +204,9 @@
         return fourier.reshape(devices, half_local, row_count, chan_width), part
 
     out_north, part_north = hemisphere(masked, lat_weights_of(j_all, lat_total))
+    north_in = lax.all_to_all(out_north, "lat", split_axis=0, concat_axis=0, tiled=True)
     out_south, part_south = hemisphere(flipped, lat_weights_of(lat_total - 1 - j_all, lat_total))
-    partial_value = part_north + part_south
+    partial_value, north_in = lax.optimization_barrier((part_north + part_south, north_in))
     gathered = lax.all_to_all(
         jnp.broadcast_to(partial_value[None], (devices, chan_count)), "lat", 0, 0, tiled=True
     )
@@ -212,8 +214,7 @@
     variance = global_sum / (NLON * jnp.sum(weight_all))
     col_scale = col_gain * lax.rsqrt(variance + 1e-05)
 
-    def round_trip(outbound, lat_weight):
-        rows_in = lax.all_to_all(outbound, "lat", split_axis=0, concat_axis=0, tiled=True)
+    def round_trip(rows_in, lat_weight):
         weighted_local = column_network(
             lat_weight, rows_in, col_scale, in_weight, in_bias, out_weight, wave_table
         )
@@ -221,8 +222,12 @@
         back = lax.all_to_all(returning, "lat", split_axis=1, concat_axis=1, tiled=True)
         return back.transpose(2, 1, 0, 3).reshape(row_count, half_lat, chan_width)
 
-    north = round_trip(out_north, weight_north)
-    south = round_trip(out_south, weight_south)
+    out_south, wave_table, col_scale, north_in = lax.optimization_barrier(
+        (out_south, wave_table, col_scale, north_in)
+    )
+    north = round_trip(north_in, weight_north)
+    south_in = lax.all_to_all(out_south, "lat", split_axis=0, concat_axis=0, tiled=True)
+    south = round_trip(south_in, weight_south)
     factor = 2.0 * math.sqrt(degrees * wave_total / lat_total)
     damp_all = jnp.concatenate([damping, damping])
     return inverse_legendre(wave_own, lat_basis, north, south, spectral, damp_all, factor)

time: 221 us -> 203 us (0.919)
  waiting for transfers between devices: 73.9 us -> 52.6 us
  other arithmetic: 18.7 us -> 21.7 us
    all_to_all x2, waiting for transfers between devices: 35.8 us -> 19.3 us  [the longest x1 15.2 us: on_device(): lax.all_to_all(out_north, 'lat', split_axis=0, concat_axis=0, tiled=True)]
    all_to_all x2, starting transfers between devices: 6.24 us -> 12.8 us  [the longest x1 7.3 us: on_device(): lax.all_to_all(out_north, 'lat', split_axis=0, concat_axis=0, tiled=True)]
    all_to_all x1, waiting for transfers between devices: 5.13 us -> 0.34 us  [on_device(): lax.all_to_all(jnp.broadcast_to(partial_value[None], (devices, chan_count...]
    all_to_all x1, starting transfers between devices: 7.28 us -> 3.77 us  [on_device(): lax.all_to_all(jnp.broadcast_to(partial_value[None], (devices, chan_count...]
  transfers between devices with their start and end apart: 5 -> 5, of which waited for: 4 -> 5; matrix products, arithmetic and copies ran while one was open for 15% -> 20% of each run, Pallas kernels for 28% -> 31%
where the time goes in v14:
time: 203 us
  Pallas kernels  72.1 us (36%)
  waiting for transfers between devices  52.6 us (26%)
  starting transfers between devices  24.4 us (12%)
  other arithmetic  21.7 us (11%)
  local copies, waits for them, and re-layouts  19.1 us (9%)
  matrix products  11.9 us (6%)
    pallas_call x2, Pallas kernels, column_network(): pl.pallas_call(column_kernel, grid=(lat_local,), in_specs=[pl.BlockSpec(m...  62.6 us
    all_to_all x2, waiting for transfers between devices, round_trip(): lax.all_to_all(returning, 'lat', split_axis=1, concat_axis=1, tiled=True)  33 us
    all_to_all x1, waiting for transfers between devices, on_device(): lax.all_to_all(out_north, 'lat', split_axis=0, concat_axis=0, tiled=True)  15.2 us
    another operation x1, other arithmetic  15 us
    dot_general x2, matrix products, hemisphere(): jnp.einsum('rnj,rnc->jrc', lat_basis, values, preferred_element_type=jnp....  11.9 us
    pallas_call x1, Pallas kernels, inverse_legendre(): pl.pallas_call(functools.partial(inverse_kernel, factor=factor), grid=(ro...  9.54 us
    all_to_all x2, starting transfers between devices, round_trip(): lax.all_to_all(returning, 'lat', split_axis=1, concat_axis=1, tiled=True)  7.81 us
    all_to_all x1, starting transfers between devices, on_device(): lax.all_to_all(out_north, 'lat', split_axis=0, concat_axis=0, tiled=True)  7.3 us
  transfers between devices with their start and end apart: 5, of which 5 were waited for; matrix products, arithmetic and copies ran while one was open for 20% of the time, Pallas kernels for 31%

profile of v14, /device:TPU:0, one launch (start us, length us, event | category | flops | bytes accessed | tf_op | source)
XLA Modules:
  0.0 202.6 jit_solution(7128228182609816564)
XLA Ops:
  1.1 5.2 %fusion.38 = (f32[192,16,256]{2,0,1:T(8,128)}, bf16[192,16,256]{2,0,1:T(8,128)(2,1)S(1)}) fusion(bf16[16,512,192]{1,2,0:T(8,128)(2,1)} %param.9, bf16[16,512,256]{2,1,0:T(8,128)(2,1)} %spec_ref.1, pred[16,512]{1,0:T(8,128)(4,1)S(1)} %get-tuple-element.23), kind=kOutput, calls=%fused_computation.72 | convolution fusion | flops 808976384 | bytes 12066816 | tf_op jit(solution)/shard_map/rnj,rnc->jrc/dot_general | solution.py:194
  6.3 2.0 copy.29
  8.4 7.3 %all-to-all-start = ((bf16[32,6,16,256]{3,2,1,0:T(8,128)(2,1)}), bf16[32,6,16,256]{3,2,1,0:T(8,128)(2,1)S(1)}, u32[]{:S(2)}, u32[]{:S(2)}) async-start(bf16[32,6,16,256]{3,2,1,0:T(8,128)(2,1)} %bitcast.3), calls=%async_computation | async-start | bytes 3145728 | tf_op jit(solution)/shard_map/all_to_all | solution.py:207
  15.8 6.6 %fusion.37 = (f32[192,16,256]{2,0,1:T(8,128)S(1)}, bf16[192,16,256]{2,0,1:T(8,128)(2,1)}) fusion(bf16[16,512,192]{1,2,0:T(8,128)(2,1)} %param.9, pred[16,512]{1,0:T(8,128)(4,1)S(1)} %get-tuple-element.24, bf16[16,512,256]{2,1,0:T(8,128)(2,1)} %spec_ref.1, pred[16,512]{1,0:T(8,128)(4,1)S(1)} %get-tuple-element.23), kind=kOutput, calls=%fused_computation.71 | convolution fusion | flops 817364992 | bytes 12075008 | tf_op jit(solution)/shard_map/rnj,rnc->jrc/dot_general | solution.py:194
  23.2 15.0 %cosine_convert_fusion = (bf16[512,1536]{1,0:T(8,128)(2,1)S(1)}, bf16[512,1536]{1,0:T(8,128)(2,1)}) fusion(s32[512]{0:T(512)S(1)} %fusion.31), kind=kLoop, calls=%fused_computation.10 | loop fusion | flops 8650752 | bytes 3147776 | tf_op jit(solution)/shard_map/convert
  38.1 15.2 %all-to-all-done.rows_ref = bf16[32,6,16,256]{3,2,1,0:T(8,128)(2,1)S(1)} async-done(((bf16[32,6,16,256]{3,2,1,0:T(8,128)(2,1)}), bf16[32,6,16,256]{3,2,1,0:T(8,128)(2,1)S(1)}, u32[]{:S(2)}, u32[]{:S(2)}) %all-to-all-start) | async-done | bytes 1572896 | tf_op jit(solution)/shard_map/all_to_all | solution.py:207
  54.0 3.8 %all-to-all-start.1 = ((f32[32,1,128]{2,1,0:T(1,128)}), f32[32,1,128]{2,1,0:T(1,128)S(1)}, u32[]{:S(2)}, u32[]{:S(2)}) async-start(f32[32,1,128]{2,1,0:T(1,128)} %broadcast_in_dim.92), calls=%async_computation.1 | async-start | bytes 32768 | tf_op jit(solution)/shard_map/all_to_all | solution.py:210
  57.8 3.4 %pad_maximum_fusion.table_ref = bf16[1024,1536]{1,0:T(8,128)(2,1)} fusion(bf16[512,1536]{1,0:T(8,128)(2,1)} %get-tuple-element.22, bf16[512,1536]{1,0:T(8,128)(2,1)S(1)} %get-tuple-element.21), kind=kLoop, calls=%fused_computation.8 | loop fusion | flops 6291456 | bytes 6291456 | tf_op jit(solution)/shard_map/concatenate | solution.py:29
  61.2 2.0 %copy.28 = bf16[192,16,256]{2,1,0:T(8,128)(2,1)} copy(bf16[192,16,256]{2,0,1:T(8,128)(2,1)S(1)} %copy-done.5) | data formatting | bytes 3145728 | tf_op jit(solution)/shard_map/convert_element_type | solution.py:196
  65.0 5.5 %all-to-all-start.3 = ((bf16[32,6,16,256]{3,2,1,0:T(8,128)(2,1)}), bf16[32,6,16,256]{3,2,1,0:T(8,128)(2,1)S(1)}, u32[]{:S(2)}, u32[]{:S(2)}) async-start(bf16[32,6,16,256]{3,2,1,0:T(8,128)(2,1)} %bitcast.26), calls=%async_computation.3 | async-start | bytes 3145728 | tf_op jit(solution)/shard_map/all_to_all | solution.py:229
  70.6 0.9 copy-done.1
  71.5 31.3 %shard_map.82 = bf16[6,512,256]{2,1,0:T(8,128)(2,1)S(1)} custom-call(f32[6]{0:T(128)S(1)} %multiply_cosine_fusion.3.weight_ref, bf16[32,6,16,256]{3,2,1,0:T(8,128)(2,1)S(1)} %all-to-all-done.rows_ref, f32[1,128]{1,0:T(1,128)S(1)} %bitcast.22, bf16[128,1024]{1,0:T(8,128)(2,1)S(1)} %copy-done, f32[1,1024]{1,0:T(1,128)S(1)} %bitcast.24, ...), custom_call_target="tpu_custom_call" | custom-call | flops 9663676416 | bytes 6291456 | tf_op jit(solution)/shard_map/pallas_call | solution.py:91
  102.9 1.3 copy.31
  104.2 4.0 %all-to-all-done.3.rows_ref = bf16[32,6,16,256]{3,2,1,0:T(8,128)(2,1)S(1)} async-done(((bf16[32,6,16,256]{3,2,1,0:T(8,128)(2,1)}), bf16[32,6,16,256]{3,2,1,0:T(8,128)(2,1)S(1)}, u32[]{:S(2)}, u32[]{:S(2)}) %all-to-all-start.3) | async-done | bytes 1572896 | tf_op jit(solution)/shard_map/all_to_all | solution.py:229
  108.2 4.1 %all-to-all-start.2 = ((bf16[6,32,16,256]{3,2,0,1:T(8,128)(2,1)}), bf16[6,32,16,256]{3,2,0,1:T(8,128)(2,1)}, u32[]{:S(2)}, u32[]{:S(2)}) async-start(bf16[6,32,16,256]{3,2,0,1:T(8,128)(2,1)} %copy.31), calls=%async_computation.2 | async-start | bytes 3145728 | tf_op jit(solution)/shard_map/all_to_all | solution.py:222
  112.4 31.2 %shard_map.83 = bf16[6,512,256]{2,1,0:T(8,128)(2,1)S(1)} custom-call(f32[6]{0:T(128)S(1)} %multiply_cosine_fusion.2.weight_ref, bf16[32,6,16,256]{3,2,1,0:T(8,128)(2,1)S(1)} %all-to-all-done.3.rows_ref, f32[1,128]{1,0:T(1,128)S(1)} %bitcast.23, bf16[128,1024]{1,0:T(8,128)(2,1)S(1)} %copy-done, f32[1,1024]{1,0:T(1,128)S(1)} %bitcast.25, ...), custom_call_target="tpu_custom_call" | custom-call | flops 9663676416 | bytes 6291456 | tf_op jit(solution)/shard_map/pallas_call | solution.py:91
  143.6 1.4 copy.32
  145.0 4.9 %all-to-all-done.2 = bf16[6,32,16,256]{3,2,0,1:T(8,128)(2,1)} async-done(((bf16[6,32,16,256]{3,2,0,1:T(8,128)(2,1)}), bf16[6,32,16,256]{3,2,0,1:T(8,128)(2,1)}, u32[]{:S(2)}, u32[]{:S(2)}) %all-to-all-start.2) | async-done | bytes 1572896 | tf_op jit(solution)/shard_map/all_to_all | solution.py:222
  149.9 3.7 %all-to-all-start.4 = ((bf16[6,32,16,256]{3,2,0,1:T(8,128)(2,1)}), bf16[6,32,16,256]{3,2,0,1:T(8,128)(2,1)S(1)}, u32[]{:S(2)}, u32[]{:S(2)}) async-start(bf16[6,32,16,256]{3,2,0,1:T(8,128)(2,1)} %copy.32), calls=%async_computation.4 | async-start | bytes 3145728 | tf_op jit(solution)/shard_map/all_to_all | solution.py:222
  153.7 6.0 %copy.33.basis_ref = bf16[16,512,192]{2,1,0:T(8,128)(2,1)} copy(bf16[16,512,192]{1,2,0:T(8,128)(2,1)} %param.9) | data formatting | bytes 6291456 | tf_op args[1]
  160.2 3.1 %copy.34.north_ref = bf16[16,192,256]{2,1,0:T(8,128)(2,1)} copy(bf16[16,192,256]{2,0,1:T(8,128)(2,1)} %bitcast.9) | data formatting | bytes 3145728 | tf_op jit(solution)/shard_map/reshape | solution.py:223
  163.3 28.1 %all-to-all-done.4 = bf16[6,32,16,256]{3,2,0,1:T(8,128)(2,1)S(1)} async-done(((bf16[6,32,16,256]{3,2,0,1:T(8,128)(2,1)}), bf16[6,32,16,256]{3,2,0,1:T(8,128)(2,1)S(1)}, u32[]{:S(2)}, u32[]{:S(2)}) %all-to-all-start.4) | async-done | bytes 1572896 | tf_op jit(solution)/shard_map/all_to_all | solution.py:222
  191.4 1.7 copy.35.south_ref
  193.1 9.5 %shard_map.84 = f32[16,512,256]{2,1,0:T(8,128)} custom-call(s32[16]{0:T(128)} %copy-done.6, bf16[16,512,192]{2,1,0:T(8,128)(2,1)} %copy.33.basis_ref, bf16[16,192,256]{2,1,0:T(8,128)(2,1)} %copy.34.north_ref, bf16[16,192,256]{2,1,0:T(8,128)(2,1)} %copy.35.south_ref, bf16[16,512,256]{2,1,0:T(8,128)(2,1)} %spec_ref.1, f32[1,256]{1,0:T(1,128)} %bitcast.29), custom_call_target="tpu_custom_call" | custom-call | flops 1610612736 | bytes 18874368 | tf_op jit(solution)/shard_map/pallas_call | solution.py:143
  (36 shorter events, 4.4 us)
Async XLA Ops:
  1.0 14.8 %copy-start.6 = (s32[16]{0:T(128)}, s32[16]{0:T(128)S(1)}, u32[]{:S(2)}) copy-start(s32[16]{0:T(128)S(1)} %get-tuple-element.20.wave_ref) | copy-start | bytes 196
  8.4 45.0 %all-to-all-start = ((bf16[32,6,16,256]{3,2,1,0:T(8,128)(2,1)}), bf16[32,6,16,256]{3,2,1,0:T(8,128)(2,1)S(1)}, u32[]{:S(2)}, u32[]{:S(2)}) async-start(bf16[32,6,16,256]{3,2,1,0:T(8,128)(2,1)} %bitcast.3), calls=%async_computation | async-start | bytes 3145728 | tf_op jit(solution)/shard_map/all_to_all | solution.py:207
  15.8 6.6 %copy-start.4 = (f32[192,16,256]{2,0,1:T(8,128)S(1)}, f32[192,16,256]{2,0,1:T(8,128)}, u32[]{:S(2)}) copy-start(f32[192,16,256]{2,0,1:T(8,128)} %get-tuple-element.27) | copy-start | bytes 9437188
  54.0 10.9 %all-to-all-start.1 = ((f32[32,1,128]{2,1,0:T(1,128)}), f32[32,1,128]{2,1,0:T(1,128)S(1)}, u32[]{:S(2)}, u32[]{:S(2)}) async-start(f32[32,1,128]{2,1,0:T(1,128)} %broadcast_in_dim.92), calls=%async_computation.1 | async-start | bytes 32768 | tf_op jit(solution)/shard_map/all_to_all | solution.py:210
  57.8 3.4 %copy-start.5 = (bf16[192,16,256]{2,0,1:T(8,128)(2,1)S(1)}, bf16[192,16,256]{2,0,1:T(8,128)(2,1)}, u32[]{:S(2)}) copy-start(bf16[192,16,256]{2,0,1:T(8,128)(2,1)} %get-tuple-element.26) | copy-start | bytes 4718596
  61.2 3.8 %copy-start.7 = (f32[128]{0:T(128)S(1)}, f32[128]{0:T(128)}, u32[]{:S(2)}) copy-start(f32[128]{0:T(128)} %param.14) | copy-start | bytes 1540
  61.2 9.4 %copy-start = (bf16[128,1024]{1,0:T(8,128)(2,1)S(1)}, bf16[128,1024]{1,0:T(8,128)(2,1)}, u32[]{:S(2)}) copy-start(bf16[128,1024]{1,0:T(8,128)(2,1)} %in_w_ref.3) | copy-start | bytes 786436
  61.2 9.4 %copy-start.3 = (f32[1024]{0:T(1024)S(1)}, f32[1024]{0:T(1024)}, u32[]{:S(2)}) copy-start(f32[1024]{0:T(1024)} %param.12) | copy-start | bytes 12292
  65.0 43.3 %all-to-all-start.3 = ((bf16[32,6,16,256]{3,2,1,0:T(8,128)(2,1)}), bf16[32,6,16,256]{3,2,1,0:T(8,128)(2,1)S(1)}, u32[]{:S(2)}, u32[]{:S(2)}) async-start(bf16[32,6,16,256]{3,2,1,0:T(8,128)(2,1)} %bitcast.26), calls=%async_computation.3 | async-start | bytes 3145728 | tf_op jit(solution)/shard_map/all_to_all | solution.py:229
  70.6 1.0 copy-start.1
  102.9 9.5 %copy-start.2 = (bf16[1024,128]{1,0:T(8,128)(2,1)S(1)}, bf16[1024,128]{1,0:T(8,128)(2,1)}, u32[]{:S(2)}) copy-start(bf16[1024,128]{1,0:T(8,128)(2,1)} %out_w_ref.3) | copy-start | bytes 786436
  108.2 41.7 %all-to-all-start.2 = ((bf16[6,32,16,256]{3,2,0,1:T(8,128)(2,1)}), bf16[6,32,16,256]{3,2,0,1:T(8,128)(2,1)}, u32[]{:S(2)}, u32[]{:S(2)}) async-start(bf16[6,32,16,256]{3,2,0,1:T(8,128)(2,1)} %copy.31), calls=%async_computation.2 | async-start | bytes 3145728 | tf_op jit(solution)/shard_map/all_to_all | solution.py:222
  149.9 41.5 %all-to-all-start.4 = ((bf16[6,32,16,256]{3,2,0,1:T(8,128)(2,1)}), bf16[6,32,16,256]{3,2,0,1:T(8,128)(2,1)S(1)}, u32[]{:S(2)}, u32[]{:S(2)}) async-start(bf16[6,32,16,256]{3,2,0,1:T(8,128)(2,1)} %copy.32), calls=%async_computation.4 | async-start | bytes 3145728 | tf_op jit(solution)/shard_map/all_to_all | solution.py:222
  153.6 6.0 %copy-start.8 = (f32[128]{0:T(128)S(1)}, f32[128]{0:T(128)}, u32[]{:S(2)}) copy-start(f32[128]{0:T(128)} %param.15) | copy-start | bytes 1540

commit v15 on v12

--- a/solution.py
+++ b/solution.py
@@ -190,21 +190,23 @@
     real_coef = jnp.where(wave_own == 0, float(NLON), NLON / 2.0)
     imag_coef = jnp.where(wave_own == 0, 0.0, NLON / 2.0)
 
-    def hemisphere(values, lat_weight):
-        fourier = jnp.einsum(
-            "rnj,rnc->jrc", lat_basis, values, preferred_element_type=jnp.float32
-        ).astype(jnp.bfloat16)
+    def squares(fourier, lat_weight):
         wide = fourier.astype(jnp.float32)
         per_lat = jnp.sum(
             real_coef[None, :, None] * wide[:, :, :chan_count] ** 2
             + imag_coef[None, :, None] * wide[:, :, chan_count:] ** 2,
             axis=1,
         )
-        part = jnp.sum(lat_weight[:, None] * per_lat, axis=0)
-        return fourier.reshape(devices, half_local, row_count, chan_width), part
-
-    out_north, part_north = hemisphere(masked, lat_weights_of(j_all, lat_total))
-    out_south, part_south = hemisphere(flipped, lat_weights_of(lat_total - 1 - j_all, lat_total))
+        return jnp.sum(lat_weight[:, None] * per_lat, axis=0)
+
+    both = jnp.stack([masked, flipped], axis=0)
+    fourier = jnp.einsum(
+        "rnj,srnc->sjrc", lat_basis, both, preferred_element_type=jnp.float32
+    ).astype(jnp.bfloat16)
+    part_north = squares(fourier[0], lat_weights_of(j_all, lat_total))
+    part_south = squares(fourier[1], lat_weights_of(lat_total - 1 - j_all, lat_total))
+    out_north = fourier[0].reshape(devices, half_local, row_count, chan_width)
+    out_south = fourier[1].reshape(devices, half_local, row_count, chan_width)
     partial_value = part_north + part_south
     hi = partial_value.astype(jnp.bfloat16)
     rest = partial_value - hi.astype(jnp.float32)

time: 204 us -> 201 us (0.985)
  matrix products: 10.9 us -> 2.1 us
  other arithmetic: 20.2 us -> 27.3 us
    dot_general x2 -> x1, matrix products: 10.9 us -> 2.1 us  [on_device(): jnp.einsum('rnj,srnc->sjrc', lat_basis, both, preferred_element_type=jnp....]
    another operation x1 -> x2, other arithmetic: 13.5 us -> 19.7 us
    slice x0 -> x2, local copies, waits for them, and re-layouts: none -> 2.9 us  [the longest x1 2.02 us: on_device(): out_south = fourier[1].reshape(devices, half_local, row_count, chan_width)]
    convert_element_type x2 -> x0, local copies, waits for them, and re-layouts: 2.89 us -> none  [hemisphere(): fourier = jnp.einsum('rnj,rnc->jrc', lat_basis, values, preferred_element...]
    unnamed x21 -> x19, local copies, waits for them, and re-layouts: 8.62 us -> 7.9 us
where the time goes in v15:
time: 201 us
  Pallas kernels  72.1 us (36%)
  waiting for transfers between devices  60.4 us (30%)
  other arithmetic  27.3 us (14%)
  starting transfers between devices  19.4 us (10%)
  local copies, waits for them, and re-layouts  18.4 us (9%)
  matrix products  2.1 us (1%)
    pallas_call x2, Pallas kernels, column_network(): pl.pallas_call(column_kernel, grid=(lat_local,), in_specs=[pl.BlockSpec(m...  62.6 us
    all_to_all x2, waiting for transfers between devices, round_trip(): lax.all_to_all(returning, 'lat', split_axis=1, concat_axis=1, tiled=True)  33 us
    all_to_all x1, waiting for transfers between devices, on_device(): lax.all_to_all(jnp.concatenate([out_north, slot], axis=1), 'lat', split_a...  24.5 us
    another operation x1, other arithmetic  13.5 us
    pallas_call x1, Pallas kernels, inverse_legendre(): pl.pallas_call(functools.partial(inverse_kernel, factor=factor), grid=(ro...  9.54 us
    unnamed x19, local copies, waits for them, and re-layouts  7.9 us
    all_to_all x2, starting transfers between devices, round_trip(): lax.all_to_all(returning, 'lat', split_axis=1, concat_axis=1, tiled=True)  7.85 us
    all_to_all x1, starting transfers between devices, on_device(): lax.all_to_all(jnp.concatenate([out_north, slot], axis=1), 'lat', split_a...  7.3 us
  transfers between devices with their start and end apart: 4, of which 4 were waited for; matrix products, arithmetic and copies ran while one was open for 15% of the time, Pallas kernels for 31%

profile of v15, /device:TPU:0, one launch (start us, length us, event | category | flops | bytes accessed | tf_op | source)
XLA Modules:
  0.0 200.6 jit_solution(10191284325621405544)
XLA Ops:
  1.2 6.2 %fusion.5 = (bf16[1,16,512,256]{3,2,0,1:T(8,128)(2,1)S(1)}, bf16[1,16,512,256]{3,2,0,1:T(8,128)(2,1)S(1)}) fusion(bf16[16,512,256]{2,1,0:T(8,128)(2,1)} %spec_ref.1, pred[16,512]{1,0:T(8,128)(4,1)S(1)} %get-tuple-element.28, pred[16,512]{1,0:T(8,128)(4,1)S(1)} %get-tuple-element.29), kind=kLoop, calls=%fused_computation.8 | loop fusion | flops 6291456 | bytes 12599296 | tf_op jit(solution)/shard_map/stack | solution.py:202
  7.5 2.1 %convert_bitcast_fusion = bf16[2,192,16,256]{3,1,0,2:T(8,128)(2,1)S(1)} fusion(bf16[1,16,512,256]{3,2,0,1:T(8,128)(2,1)S(1)} %get-tuple-element.18, bf16[1,16,512,256]{3,2,0,1:T(8,128)(2,1)S(1)} %get-tuple-element.17, bf16[16,512,192]{1,2,0:T(8,128)(2,1)S(1)} %copy-done.5), kind=kOutput, calls=%fused_computation.18 | convolution fusion | flops 1628962816 | bytes 14680064 | tf_op jit(solution)/shard_map/rnj,srnc->sjrc/dot_general | solution.py:203
  12.4 1.4 pad_maximum_fusion.1
  13.8 7.3 %all-to-all-start = ((bf16[32,7,16,256]{3,2,1,0:T(8,128)(2,1)}), bf16[32,7,16,256]{3,2,1,0:T(8,128)(2,1)S(1)}, u32[]{:S(2)}, u32[]{:S(2)}) async-start(bf16[32,7,16,256]{3,2,1,0:T(8,128)(2,1)} %pad_maximum_fusion.1), calls=%async_computation | async-start | bytes 3670016 | tf_op jit(solution)/shard_map/all_to_all | solution.py:223
  21.1 2.0 %copy.27 = bf16[1,192,16,256]{3,2,1,0:T(8,128)(2,1)} copy(bf16[1,192,16,256]{3,1,2,0:T(8,128)(2,1)S(1)} %get-tuple-element.22) | data formatting | bytes 3145728 | tf_op jit(solution)/shard_map/slice | solution.py:209
  24.4 13.5 %cosine_convert_fusion = (bf16[512,1536]{1,0:T(8,128)(2,1)S(1)}, bf16[512,1536]{1,0:T(8,128)(2,1)S(1)}) fusion(s32[512]{0:T(512)S(1)} %fusion.35), kind=kLoop, calls=%fused_computation.14 | loop fusion | flops 8650752 | bytes 3147776 | tf_op jit(solution)/shard_map/convert.3
  37.9 1.9 pad_maximum_fusion.table_ref
  39.8 24.5 %all-to-all-done.rows_ref = bf16[32,7,16,256]{3,2,1,0:T(8,128)(2,1)S(1)} async-done(((bf16[32,7,16,256]{3,2,1,0:T(8,128)(2,1)}), bf16[32,7,16,256]{3,2,1,0:T(8,128)(2,1)S(1)}, u32[]{:S(2)}, u32[]{:S(2)}) %all-to-all-start) | async-done | bytes 1835040 | tf_op jit(solution)/shard_map/all_to_all | solution.py:223
  64.4 4.2 %all-to-all-start.2 = ((bf16[32,6,16,256]{3,2,1,0:T(8,128)(2,1)}), bf16[32,6,16,256]{3,2,1,0:T(8,128)(2,1)S(1)}, u32[]{:S(2)}, u32[]{:S(2)}) async-start(bf16[32,6,16,256]{3,2,1,0:T(8,128)(2,1)} %bitcast.48), calls=%async_computation.2 | async-start | bytes 3145728 | tf_op jit(solution)/shard_map/all_to_all | solution.py:243
  68.7 0.9 copy-done
  69.6 0.9 copy-done.2
  70.6 31.3 %shard_map.82 = bf16[6,512,256]{2,1,0:T(8,128)(2,1)S(1)} custom-call(f32[6]{0:T(128)S(1)} %multiply_cosine_fusion.3.weight_ref, bf16[32,7,16,256]{3,2,1,0:T(8,128)(2,1)S(1)} %all-to-all-done.rows_ref, f32[1,128]{1,0:T(1,128)S(1)} %bitcast.44, bf16[128,1024]{1,0:T(8,128)(2,1)S(1)} %copy-done, f32[1,1024]{1,0:T(1,128)S(1)} %bitcast.46, ...), custom_call_target="tpu_custom_call" | custom-call | flops 9663676416 | bytes 6291456 | tf_op jit(solution)/shard_map/pallas_call | solution.py:91
  101.9 1.3 copy.29
  103.3 2.9 %all-to-all-done.2.rows_ref = bf16[32,6,16,256]{3,2,1,0:T(8,128)(2,1)S(1)} async-done(((bf16[32,6,16,256]{3,2,1,0:T(8,128)(2,1)}), bf16[32,6,16,256]{3,2,1,0:T(8,128)(2,1)S(1)}, u32[]{:S(2)}, u32[]{:S(2)}) %all-to-all-start.2) | async-done | bytes 1572896 | tf_op jit(solution)/shard_map/all_to_all | solution.py:243
  106.2 3.9 %all-to-all-start.1 = ((bf16[6,32,16,256]{3,2,0,1:T(8,128)(2,1)}), bf16[6,32,16,256]{3,2,0,1:T(8,128)(2,1)}, u32[]{:S(2)}, u32[]{:S(2)}) async-start(bf16[6,32,16,256]{3,2,0,1:T(8,128)(2,1)} %copy.29), calls=%async_computation.1 | async-start | bytes 3145728 | tf_op jit(solution)/shard_map/all_to_all | solution.py:236
  110.1 31.2 %shard_map.83 = bf16[6,512,256]{2,1,0:T(8,128)(2,1)S(1)} custom-call(f32[6]{0:T(128)S(1)} %multiply_cosine_fusion.2.weight_ref, bf16[32,6,16,256]{3,2,1,0:T(8,128)(2,1)S(1)} %all-to-all-done.2.rows_ref, f32[1,128]{1,0:T(1,128)S(1)} %bitcast.45, bf16[128,1024]{1,0:T(8,128)(2,1)S(1)} %copy-done.1, f32[1,1024]{1,0:T(1,128)S(1)} %bitcast.47, ...), custom_call_target="tpu_custom_call" | custom-call | flops 9663676416 | bytes 6291456 | tf_op jit(solution)/shard_map/pallas_call | solution.py:91
  141.4 1.4 copy.30
  142.7 5.1 %all-to-all-done.1 = bf16[6,32,16,256]{3,2,0,1:T(8,128)(2,1)} async-done(((bf16[6,32,16,256]{3,2,0,1:T(8,128)(2,1)}), bf16[6,32,16,256]{3,2,0,1:T(8,128)(2,1)}, u32[]{:S(2)}, u32[]{:S(2)}) %all-to-all-start.1) | async-done | bytes 1572896 | tf_op jit(solution)/shard_map/all_to_all | solution.py:236
  147.8 4.0 %all-to-all-start.3 = ((bf16[6,32,16,256]{3,2,0,1:T(8,128)(2,1)}), bf16[6,32,16,256]{3,2,0,1:T(8,128)(2,1)S(1)}, u32[]{:S(2)}, u32[]{:S(2)}) async-start(bf16[6,32,16,256]{3,2,0,1:T(8,128)(2,1)} %copy.30), calls=%async_computation.3 | async-start | bytes 3145728 | tf_op jit(solution)/shard_map/all_to_all | solution.py:236
  151.8 6.0 %copy.31.basis_ref = bf16[16,512,192]{2,1,0:T(8,128)(2,1)} copy(bf16[16,512,192]{1,2,0:T(8,128)(2,1)} %param.9) | data formatting | bytes 6291456 | tf_op args[1]
  158.3 3.1 %copy.32.north_ref = bf16[16,192,256]{2,1,0:T(8,128)(2,1)} copy(bf16[16,192,256]{2,0,1:T(8,128)(2,1)} %bitcast.18) | data formatting | bytes 3145728 | tf_op jit(solution)/shard_map/reshape | solution.py:237
  161.4 27.9 %all-to-all-done.3 = bf16[6,32,16,256]{3,2,0,1:T(8,128)(2,1)S(1)} async-done(((bf16[6,32,16,256]{3,2,0,1:T(8,128)(2,1)}), bf16[6,32,16,256]{3,2,0,1:T(8,128)(2,1)S(1)}, u32[]{:S(2)}, u32[]{:S(2)}) %all-to-all-start.3) | async-done | bytes 1572896 | tf_op jit(solution)/shard_map/all_to_all | solution.py:236
  189.3 1.7 copy.33.south_ref
  191.1 9.5 %shard_map.84 = f32[16,512,256]{2,1,0:T(8,128)} custom-call(s32[16]{0:T(128)} %copy-done.6, bf16[16,512,192]{2,1,0:T(8,128)(2,1)} %copy.31.basis_ref, bf16[16,192,256]{2,1,0:T(8,128)(2,1)} %copy.32.north_ref, bf16[16,192,256]{2,1,0:T(8,128)(2,1)} %copy.33.south_ref, bf16[16,512,256]{2,1,0:T(8,128)(2,1)} %spec_ref.1, f32[1,256]{1,0:T(1,128)} %bitcast.51), custom_call_target="tpu_custom_call" | custom-call | flops 1610612736 | bytes 18874368 | tf_op jit(solution)/shard_map/pallas_call | solution.py:143
  (44 shorter events, 5.3 us)
Async XLA Ops:
  1.0 6.5 %copy-start.6 = (s32[16]{0:T(128)}, s32[16]{0:T(128)S(1)}, u32[]{:S(2)}) copy-start(s32[16]{0:T(128)S(1)} %get-tuple-element.16.wave_ref) | copy-start | bytes 196
  1.2 6.3 %copy-start.5 = (bf16[16,512,192]{1,2,0:T(8,128)(2,1)S(1)}, bf16[16,512,192]{1,2,0:T(8,128)(2,1)}, u32[]{:S(2)}) copy-start(bf16[16,512,192]{1,2,0:T(8,128)(2,1)} %param.9) | copy-start | bytes 9437188
  13.8 50.5 %all-to-all-start = ((bf16[32,7,16,256]{3,2,1,0:T(8,128)(2,1)}), bf16[32,7,16,256]{3,2,1,0:T(8,128)(2,1)S(1)}, u32[]{:S(2)}, u32[]{:S(2)}) async-start(bf16[32,7,16,256]{3,2,1,0:T(8,128)(2,1)} %pad_maximum_fusion.1), calls=%async_computation | async-start | bytes 3670016 | tf_op jit(solution)/shard_map/all_to_all | solution.py:223
  37.9 26.4 %copy-start.7 = (f32[128]{0:T(128)S(1)}, f32[128]{0:T(128)}, u32[]{:S(2)}) copy-start(f32[128]{0:T(128)} %param.14) | copy-start | bytes 1540
  39.8 28.9 %copy-start.4 = (f32[1024]{0:T(1024)S(1)}, f32[1024]{0:T(1024)}, u32[]{:S(2)}) copy-start(f32[1024]{0:T(1024)} %param.12) | copy-start | bytes 12292
  64.4 41.8 %all-to-all-start.2 = ((bf16[32,6,16,256]{3,2,1,0:T(8,128)(2,1)}), bf16[32,6,16,256]{3,2,1,0:T(8,128)(2,1)S(1)}, u32[]{:S(2)}, u32[]{:S(2)}) async-start(bf16[32,6,16,256]{3,2,1,0:T(8,128)(2,1)} %bitcast.48), calls=%async_computation.2 | async-start | bytes 3145728 | tf_op jit(solution)/shard_map/all_to_all | solution.py:243
  68.7 1.0 copy-start
  69.6 0.9 copy-start.2
  101.9 8.2 %copy-start.1 = (bf16[128,1024]{1,0:T(8,128)(2,1)S(1)}, bf16[128,1024]{1,0:T(8,128)(2,1)}, u32[]{:S(2)}) copy-start(bf16[128,1024]{1,0:T(8,128)(2,1)} %in_w_ref.3) | copy-start | bytes 786436
  101.9 8.2 %copy-start.3 = (bf16[1024,128]{1,0:T(8,128)(2,1)S(1)}, bf16[1024,128]{1,0:T(8,128)(2,1)}, u32[]{:S(2)}) copy-start(bf16[1024,128]{1,0:T(8,128)(2,1)} %out_w_ref.3) | copy-start | bytes 786436
  106.2 41.6 %all-to-all-start.1 = ((bf16[6,32,16,256]{3,2,0,1:T(8,128)(2,1)}), bf16[6,32,16,256]{3,2,0,1:T(8,128)(2,1)}, u32[]{:S(2)}, u32[]{:S(2)}) async-start(bf16[6,32,16,256]{3,2,0,1:T(8,128)(2,1)} %copy.29), calls=%async_computation.1 | async-start | bytes 3145728 | tf_op jit(solution)/shard_map/all_to_all | solution.py:236
  147.8 41.6 %all-to-all-start.3 = ((bf16[6,32,16,256]{3,2,0,1:T(8,128)(2,1)}), bf16[6,32,16,256]{3,2,0,1:T(8,128)(2,1)S(1)}, u32[]{:S(2)}, u32[]{:S(2)}) async-start(bf16[6,32,16,256]{3,2,0,1:T(8,128)(2,1)} %copy.30), calls=%async_computation.3 | async-start | bytes 3145728 | tf_op jit(solution)/shard_map/all_to_all | solution.py:236
  151.8 6.0 %copy-start.8 = (f32[128]{0:T(128)S(1)}, f32[128]{0:T(128)}, u32[]{:S(2)}) copy-start(f32[128]{0:T(128)} %param.15) | copy-start | bytes 1540

commit v16 on v15

--- a/solution.py
+++ b/solution.py
@@ -120,15 +120,19 @@
 
 
 def inverse_kernel(wave_ref, basis_ref, north_ref, south_ref, spec_ref, damp_ref, o_ref, *, factor):
-    block = basis_ref.shape[0]
-    degrees = basis_ref.shape[1]
+    block, degrees, half_lat = basis_ref.shape
+    width = spec_ref.shape[2]
     n = lax.broadcasted_iota(jnp.int32, (degrees, 1), 0)
     wave_factor = (n * (n + 1)).astype(jnp.float32) / (NN * NN)
+    north_all = north_ref[...].astype(jnp.float32)
+    south_all = south_ref[...].astype(jnp.float32)
     for b in range(block):
         m = wave_ref[pl.program_id(0) * block + b]
         basis = basis_ref[b]
-        east = jnp.dot(basis, north_ref[b], preferred_element_type=jnp.float32)
-        west = jnp.dot(basis, south_ref[b], preferred_element_type=jnp.float32)
+        north = north_all[:, :, b, :].reshape(half_lat, width).astype(jnp.bfloat16)
+        south = south_all[:, :, b, :].reshape(half_lat, width).astype(jnp.bfloat16)
+        east = jnp.dot(basis, north, preferred_element_type=jnp.float32)
+        west = jnp.dot(basis, south, preferred_element_type=jnp.float32)
         parity = jnp.where((n + m) % 2 == 0, 1.0, -1.0).astype(jnp.float32)
         legendre = factor * (east + parity * west)
         damped = legendre - damp_ref[...] * wave_factor * spec_ref[b].astype(jnp.float32)
@@ -146,8 +150,8 @@
         in_specs=[
             pl.BlockSpec(memory_space=pltpu.SMEM),
             three((block, degrees, half_lat)),
-            three((block, half_lat, width)),
-            three((block, half_lat, width)),
+            pl.BlockSpec(north.shape[:2] + (block, width), lambda r: (0, 0, r, 0)),
+            pl.BlockSpec(south.shape[:2] + (block, width), lambda r: (0, 0, r, 0)),
             three((block, degrees, width)),
             pl.BlockSpec((1, width), lambda r: (0, 0)),
         ],
@@ -234,7 +238,7 @@
         )
         returning = weighted_local.reshape(half_local, devices, row_count, chan_width)
         back = lax.all_to_all(returning, "lat", split_axis=1, concat_axis=1, tiled=True)
-        return back.transpose(2, 1, 0, 3).reshape(row_count, half_lat, chan_width)
+        return back
 
     out_south, wave_table, col_scale, north_in = lax.optimization_barrier(
         (out_south, wave_table, col_scale, north_in)
@@ -244,7 +248,9 @@
     south = round_trip(south_in, weight_south)
     factor = 2.0 * math.sqrt(degrees * wave_total / lat_total)
     damp_all = jnp.concatenate([damping, damping])
-    return inverse_legendre(wave_own, lat_basis, north, south, spectral, damp_all, factor)
+    basis_perm = lat_basis.reshape(row_count, degrees, devices, half_local).transpose(0, 1, 3, 2)
+    basis_perm = basis_perm.reshape(row_count, degrees, half_lat)
+    return inverse_legendre(wave_own, basis_perm, north, south, spectral, damp_all, factor)
 
 
 def solution(mesh):

time: 201 us -> 206 us (1.025)
  Pallas kernels: 72.1 us -> 76.2 us
  local copies, waits for them, and re-layouts: 18.4 us -> 20.6 us
    all_to_all x0 -> x2, local copies, waits for them, and re-layouts: none -> 5.48 us  [round_trip(): lax.all_to_all(returning, 'lat', split_axis=1, concat_axis=1, tiled=True)]
    unnamed x19 -> x21, local copies, waits for them, and re-layouts: 7.9 us -> 3.69 us
    pallas_call x1, Pallas kernels: 9.54 us -> 13.6 us  [inverse_legendre(): pl.pallas_call(functools.partial(inverse_kernel, factor=factor), grid=(ro...]
    reshape x2 -> x1, local copies, waits for them, and re-layouts: 4.83 us -> 3.97 us  [on_device(): basis_perm = basis_perm.reshape(row_count, degrees, half_lat)]
  transfers between devices with their start and end apart: 4 -> 4, of which waited for: 4 -> 4; matrix products, arithmetic and copies ran while one was open for 15% -> 15% of each run, Pallas kernels for 31% -> 30%
where the time goes in v16:
time: 206 us
  Pallas kernels  76.2 us (37%)
  waiting for transfers between devices  59.2 us (29%)
  other arithmetic  27.3 us (13%)
  local copies, waits for them, and re-layouts  20.6 us (10%)
  starting transfers between devices  19.5 us (9%)
  matrix products  2.1 us (1%)
    pallas_call x2, Pallas kernels, column_network(): pl.pallas_call(column_kernel, grid=(lat_local,), in_specs=[pl.BlockSpec(m...  62.6 us
    all_to_all x2, waiting for transfers between devices, round_trip(): lax.all_to_all(returning, 'lat', split_axis=1, concat_axis=1, tiled=True)  31.8 us
    all_to_all x1, waiting for transfers between devices, on_device(): lax.all_to_all(jnp.concatenate([out_north, slot], axis=1), 'lat', split_a...  24.5 us
    pallas_call x1, Pallas kernels, inverse_legendre(): pl.pallas_call(functools.partial(inverse_kernel, factor=factor), grid=(ro...  13.6 us
    another operation x1, other arithmetic  13.5 us
    all_to_all x2, starting transfers between devices, round_trip(): lax.all_to_all(returning, 'lat', split_axis=1, concat_axis=1, tiled=True)  7.97 us
    all_to_all x1, starting transfers between devices, on_device(): lax.all_to_all(jnp.concatenate([out_north, slot], axis=1), 'lat', split_a...  7.3 us
    another operation x1, other arithmetic, on_device(): both = jnp.stack([masked, flipped], axis=0)  6.23 us
  transfers between devices with their start and end apart: 4, of which 4 were waited for; matrix products, arithmetic and copies ran while one was open for 15% of the time, Pallas kernels for 30%

profile of v16, /device:TPU:0, one launch (start us, length us, event | category | flops | bytes accessed | tf_op | source)
XLA Modules:
  0.0 205.8 jit_solution(12763499646613458539)
XLA Ops:
  1.2 6.2 %fusion.5 = (bf16[1,16,512,256]{3,2,0,1:T(8,128)(2,1)S(1)}, bf16[1,16,512,256]{3,2,0,1:T(8,128)(2,1)S(1)}) fusion(bf16[16,512,256]{2,1,0:T(8,128)(2,1)} %spec_ref.1, pred[16,512]{1,0:T(8,128)(4,1)S(1)} %get-tuple-element.28, pred[16,512]{1,0:T(8,128)(4,1)S(1)} %get-tuple-element.29), kind=kLoop, calls=%fused_computation.8 | loop fusion | flops 6291456 | bytes 12599296 | tf_op jit(solution)/shard_map/stack | solution.py:206
  7.5 2.1 %convert_bitcast_fusion = bf16[2,192,16,256]{3,1,0,2:T(8,128)(2,1)S(1)} fusion(bf16[1,16,512,256]{3,2,0,1:T(8,128)(2,1)S(1)} %get-tuple-element.18, bf16[1,16,512,256]{3,2,0,1:T(8,128)(2,1)S(1)} %get-tuple-element.17, bf16[16,512,192]{1,2,0:T(8,128)(2,1)S(1)} %copy-done.5), kind=kOutput, calls=%fused_computation.18 | convolution fusion | flops 1628962816 | bytes 14680064 | tf_op jit(solution)/shard_map/rnj,srnc->sjrc/dot_general | solution.py:207
  12.4 1.4 pad_maximum_fusion.1
  13.8 7.3 %all-to-all-start = ((bf16[32,7,16,256]{3,2,1,0:T(8,128)(2,1)}), bf16[32,7,16,256]{3,2,1,0:T(8,128)(2,1)S(1)}, u32[]{:S(2)}, u32[]{:S(2)}) async-start(bf16[32,7,16,256]{3,2,1,0:T(8,128)(2,1)} %pad_maximum_fusion.1), calls=%async_computation | async-start | bytes 3670016 | tf_op jit(solution)/shard_map/all_to_all | solution.py:227
  21.1 2.0 copy.36
  24.4 13.5 %cosine_convert_fusion = (bf16[512,1536]{1,0:T(8,128)(2,1)S(1)}, bf16[512,1536]{1,0:T(8,128)(2,1)S(1)}) fusion(s32[512]{0:T(512)S(1)} %fusion.35), kind=kLoop, calls=%fused_computation.14 | loop fusion | flops 8650752 | bytes 3147776 | tf_op jit(solution)/shard_map/convert.3
  37.9 1.9 pad_maximum_fusion.table_ref
  39.8 24.5 %all-to-all-done.rows_ref = bf16[32,7,16,256]{3,2,1,0:T(8,128)(2,1)S(1)} async-done(((bf16[32,7,16,256]{3,2,1,0:T(8,128)(2,1)}), bf16[32,7,16,256]{3,2,1,0:T(8,128)(2,1)S(1)}, u32[]{:S(2)}, u32[]{:S(2)}) %all-to-all-start) | async-done | bytes 1835040 | tf_op jit(solution)/shard_map/all_to_all | solution.py:227
  64.4 4.2 %all-to-all-start.2 = ((bf16[32,6,16,256]{3,2,1,0:T(8,128)(2,1)}), bf16[32,6,16,256]{3,2,1,0:T(8,128)(2,1)S(1)}, u32[]{:S(2)}, u32[]{:S(2)}) async-start(bf16[32,6,16,256]{3,2,1,0:T(8,128)(2,1)} %bitcast.48), calls=%async_computation.2 | async-start | bytes 3145728 | tf_op jit(solution)/shard_map/all_to_all | solution.py:247
  70.6 31.3 %shard_map.82 = bf16[6,512,256]{2,1,0:T(8,128)(2,1)S(1)} custom-call(f32[6]{0:T(128)S(1)} %multiply_cosine_fusion.3.weight_ref, bf16[32,7,16,256]{3,2,1,0:T(8,128)(2,1)S(1)} %all-to-all-done.rows_ref, f32[1,128]{1,0:T(1,128)S(1)} %bitcast.42, bf16[128,1024]{1,0:T(8,128)(2,1)S(1)} %copy-done, f32[1,1024]{1,0:T(1,128)S(1)} %bitcast.44, ...), custom_call_target="tpu_custom_call" | custom-call | flops 9663676416 | bytes 6291456 | tf_op jit(solution)/shard_map/pallas_call | solution.py:91
  101.9 1.3 copy.38
  103.3 2.9 %all-to-all-done.2.rows_ref = bf16[32,6,16,256]{3,2,1,0:T(8,128)(2,1)S(1)} async-done(((bf16[32,6,16,256]{3,2,1,0:T(8,128)(2,1)}), bf16[32,6,16,256]{3,2,1,0:T(8,128)(2,1)S(1)}, u32[]{:S(2)}, u32[]{:S(2)}) %all-to-all-start.2) | async-done | bytes 1572896 | tf_op jit(solution)/shard_map/all_to_all | solution.py:247
  106.2 3.9 %all-to-all-start.1 = ((bf16[6,32,16,256]{3,2,0,1:T(8,128)(2,1)}), bf16[6,32,16,256]{3,2,0,1:T(8,128)(2,1)}, u32[]{:S(2)}, u32[]{:S(2)}) async-start(bf16[6,32,16,256]{3,2,0,1:T(8,128)(2,1)} %copy.38), calls=%async_computation.1 | async-start | bytes 3145728 | tf_op jit(solution)/shard_map/all_to_all | solution.py:240
  110.1 31.2 %shard_map.83 = bf16[6,512,256]{2,1,0:T(8,128)(2,1)S(1)} custom-call(f32[6]{0:T(128)S(1)} %multiply_cosine_fusion.2.weight_ref, bf16[32,6,16,256]{3,2,1,0:T(8,128)(2,1)S(1)} %all-to-all-done.2.rows_ref, f32[1,128]{1,0:T(1,128)S(1)} %bitcast.43, bf16[128,1024]{1,0:T(8,128)(2,1)S(1)} %copy-done.1, f32[1,1024]{1,0:T(1,128)S(1)} %bitcast.45, ...), custom_call_target="tpu_custom_call" | custom-call | flops 9663676416 | bytes 6291456 | tf_op jit(solution)/shard_map/pallas_call | solution.py:91
  141.4 1.4 copy.39
  142.7 5.1 %all-to-all-done.1 = bf16[6,32,16,256]{3,2,0,1:T(8,128)(2,1)} async-done(((bf16[6,32,16,256]{3,2,0,1:T(8,128)(2,1)}), bf16[6,32,16,256]{3,2,0,1:T(8,128)(2,1)}, u32[]{:S(2)}, u32[]{:S(2)}) %all-to-all-start.1) | async-done | bytes 1572896 | tf_op jit(solution)/shard_map/all_to_all | solution.py:240
  147.8 4.1 %all-to-all-start.3 = ((bf16[6,32,16,256]{3,2,0,1:T(8,128)(2,1)}), bf16[6,32,16,256]{3,2,0,1:T(8,128)(2,1)}, u32[]{:S(2)}, u32[]{:S(2)}) async-start(bf16[6,32,16,256]{3,2,0,1:T(8,128)(2,1)} %copy.39), calls=%async_computation.3 | async-start | bytes 3145728 | tf_op jit(solution)/shard_map/all_to_all | solution.py:240
  151.9 1.8 copy.32
  153.7 1.8 copy.33
  155.4 4.0 %copy.40.basis_ref = bf16[16,512,192]{2,1,0:T(8,128)(2,1)} copy(bf16[16,512,192]{1,2,0:T(8,128)(2,1)S(1)} %bitcast.46) | data formatting | bytes 6291456 | tf_op jit(solution)/shard_map/reshape | solution.py:252
  159.9 2.7 %copy.41.north_ref = bf16[6,32,16,256]{3,2,1,0:T(8,128)(2,1)} copy(bf16[6,32,16,256]{3,2,0,1:T(8,128)(2,1)} %all-to-all-done.1) | data formatting | bytes 3145728 | tf_op jit(solution)/shard_map/all_to_all | solution.py:240
  162.7 26.8 %all-to-all-done.3 = bf16[6,32,16,256]{3,2,0,1:T(8,128)(2,1)} async-done(((bf16[6,32,16,256]{3,2,0,1:T(8,128)(2,1)}), bf16[6,32,16,256]{3,2,0,1:T(8,128)(2,1)}, u32[]{:S(2)}, u32[]{:S(2)}) %all-to-all-start.3) | async-done | bytes 1572896 | tf_op jit(solution)/shard_map/all_to_all | solution.py:240
  189.4 2.7 %copy.42.south_ref = bf16[6,32,16,256]{3,2,1,0:T(8,128)(2,1)} copy(bf16[6,32,16,256]{3,2,0,1:T(8,128)(2,1)} %all-to-all-done.3) | data formatting | bytes 3145728 | tf_op jit(solution)/shard_map/all_to_all | solution.py:240
  192.2 13.6 %shard_map.84 = f32[16,512,256]{2,1,0:T(8,128)} custom-call(s32[16]{0:T(128)} %copy-done.7, bf16[16,512,192]{2,1,0:T(8,128)(2,1)} %copy.40.basis_ref, bf16[6,32,16,256]{3,2,1,0:T(8,128)(2,1)} %copy.41.north_ref, bf16[6,32,16,256]{3,2,1,0:T(8,128)(2,1)} %copy.42.south_ref, bf16[16,512,256]{2,1,0:T(8,128)(2,1)} %spec_ref.1, f32[1,256]{1,0:T(1,128)} %bitcast.50), custom_call_target="tpu_custom_call" | custom-call | flops 1610612736 | bytes 18874368 | tf_op jit(solution)/shard_map/pallas_call | solution.py:147
  (48 shorter events, 7.2 us)
Async XLA Ops:
  1.0 6.5 %copy-start.7 = (s32[16]{0:T(128)}, s32[16]{0:T(128)S(1)}, u32[]{:S(2)}) copy-start(s32[16]{0:T(128)S(1)} %get-tuple-element.16.wave_ref) | copy-start | bytes 196
  1.2 6.3 %copy-start.5 = (bf16[16,512,192]{1,2,0:T(8,128)(2,1)S(1)}, bf16[16,512,192]{1,2,0:T(8,128)(2,1)}, u32[]{:S(2)}) copy-start(bf16[16,512,192]{1,2,0:T(8,128)(2,1)} %param.9) | copy-start | bytes 9437188
  13.8 50.5 %all-to-all-start = ((bf16[32,7,16,256]{3,2,1,0:T(8,128)(2,1)}), bf16[32,7,16,256]{3,2,1,0:T(8,128)(2,1)S(1)}, u32[]{:S(2)}, u32[]{:S(2)}) async-start(bf16[32,7,16,256]{3,2,1,0:T(8,128)(2,1)} %pad_maximum_fusion.1), calls=%async_computation | async-start | bytes 3670016 | tf_op jit(solution)/shard_map/all_to_all | solution.py:227
  37.9 26.5 %copy-start.8 = (f32[128]{0:T(128)S(1)}, f32[128]{0:T(128)}, u32[]{:S(2)}) copy-start(f32[128]{0:T(128)} %param.14) | copy-start | bytes 1540
  39.8 28.9 %copy-start.4 = (f32[1024]{0:T(1024)S(1)}, f32[1024]{0:T(1024)}, u32[]{:S(2)}) copy-start(f32[1024]{0:T(1024)} %param.12) | copy-start | bytes 12292
  64.4 41.8 %all-to-all-start.2 = ((bf16[32,6,16,256]{3,2,1,0:T(8,128)(2,1)}), bf16[32,6,16,256]{3,2,1,0:T(8,128)(2,1)S(1)}, u32[]{:S(2)}, u32[]{:S(2)}) async-start(bf16[32,6,16,256]{3,2,1,0:T(8,128)(2,1)} %bitcast.48), calls=%async_computation.2 | async-start | bytes 3145728 | tf_op jit(solution)/shard_map/all_to_all | solution.py:247
  68.7 1.0 copy-start
  69.6 0.9 copy-start.2
  101.9 8.2 %copy-start.1 = (bf16[128,1024]{1,0:T(8,128)(2,1)S(1)}, bf16[128,1024]{1,0:T(8,128)(2,1)}, u32[]{:S(2)}) copy-start(bf16[128,1024]{1,0:T(8,128)(2,1)} %in_w_ref.3) | copy-start | bytes 786436
  101.9 8.2 %copy-start.3 = (bf16[1024,128]{1,0:T(8,128)(2,1)S(1)}, bf16[1024,128]{1,0:T(8,128)(2,1)}, u32[]{:S(2)}) copy-start(bf16[1024,128]{1,0:T(8,128)(2,1)} %out_w_ref.3) | copy-start | bytes 786436
  106.2 41.6 %all-to-all-start.1 = ((bf16[6,32,16,256]{3,2,0,1:T(8,128)(2,1)}), bf16[6,32,16,256]{3,2,0,1:T(8,128)(2,1)}, u32[]{:S(2)}, u32[]{:S(2)}) async-start(bf16[6,32,16,256]{3,2,0,1:T(8,128)(2,1)} %copy.38), calls=%async_computation.1 | async-start | bytes 3145728 | tf_op jit(solution)/shard_map/all_to_all | solution.py:240
  141.4 10.5 %copy-start.6 = (bf16[16,512,192]{1,2,0:T(8,128)(2,1)S(1)}, bf16[16,512,192]{1,2,0:T(8,128)(2,1)}, u32[]{:S(2)}) copy-start(bf16[16,512,192]{1,2,0:T(8,128)(2,1)} %param.9) | copy-start | bytes 9437188
  147.8 41.7 %all-to-all-start.3 = ((bf16[6,32,16,256]{3,2,0,1:T(8,128)(2,1)}), bf16[6,32,16,256]{3,2,0,1:T(8,128)(2,1)}, u32[]{:S(2)}, u32[]{:S(2)}) async-start(bf16[6,32,16,256]{3,2,0,1:T(8,128)(2,1)} %copy.39), calls=%async_computation.3 | async-start | bytes 3145728 | tf_op jit(solution)/shard_map/all_to_all | solution.py:240
  155.4 4.0 %copy-start.9 = (f32[128]{0:T(128)S(1)}, f32[128]{0:T(128)}, u32[]{:S(2)}) copy-start(f32[128]{0:T(128)} %param.15) | copy-start | bytes 1540

commit v17 on v15

--- a/solution.py
+++ b/solution.py
@@ -17,6 +17,8 @@
 def wavenumbers(block_order, slot_count):
     slot_ids = jnp.arange(slot_count, dtype=jnp.int32)
     blocks = block_order.shape[0]
+    if slot_count == blocks * MB:
+        return jnp.repeat(block_order, MB) * MB + slot_ids % MB
     matches = (slot_ids // MB)[:, None] == jnp.arange(blocks, dtype=jnp.int32)[None, :]
     chosen = jnp.sum(jnp.where(matches, block_order[None, :], 0), axis=1)
     return chosen * MB + slot_ids % MB

time: 201 us -> 201 us (level)
  no operation moved by 1% of the time
where the time goes in v17:
time: 201 us
  Pallas kernels  72.1 us (36%)
  waiting for transfers between devices  60.4 us (30%)
  other arithmetic  27.1 us (13%)
  starting transfers between devices  19.4 us (10%)
  local copies, waits for them, and re-layouts  18.5 us (9%)
  matrix products  2.1 us (1%)
    pallas_call x2, Pallas kernels, column_network(): pl.pallas_call(column_kernel, grid=(lat_local,), in_specs=[pl.BlockSpec(m...  62.6 us
    all_to_all x2, waiting for transfers between devices, round_trip(): lax.all_to_all(returning, 'lat', split_axis=1, concat_axis=1, tiled=True)  33 us
    all_to_all x1, waiting for transfers between devices, on_device(): lax.all_to_all(jnp.concatenate([out_north, slot], axis=1), 'lat', split_a...  24.5 us
    another operation x1, other arithmetic  13.5 us
    pallas_call x1, Pallas kernels, inverse_legendre(): pl.pallas_call(functools.partial(inverse_kernel, factor=factor), grid=(ro...  9.54 us
    unnamed x19, local copies, waits for them, and re-layouts  7.87 us
    all_to_all x2, starting transfers between devices, round_trip(): lax.all_to_all(returning, 'lat', split_axis=1, concat_axis=1, tiled=True)  7.85 us
    all_to_all x1, starting transfers between devices, on_device(): lax.all_to_all(jnp.concatenate([out_north, slot], axis=1), 'lat', split_a...  7.3 us
  transfers between devices with their start and end apart: 4, of which 4 were waited for; matrix products, arithmetic and copies ran while one was open for 15% of the time, Pallas kernels for 31%

profile of v17, /device:TPU:0, one launch (start us, length us, event | category | flops | bytes accessed | tf_op | source)
XLA Modules:
  0.0 200.5 jit_solution(475469918458440695)
XLA Ops:
  1.2 6.2 %fusion.5 = (bf16[1,16,512,256]{3,2,0,1:T(8,128)(2,1)S(1)}, bf16[1,16,512,256]{3,2,0,1:T(8,128)(2,1)S(1)}) fusion(bf16[16,512,256]{2,1,0:T(8,128)(2,1)} %spec_ref.1, pred[16,512]{1,0:T(8,128)(4,1)S(1)} %get-tuple-element.28, pred[16,512]{1,0:T(8,128)(4,1)S(1)} %get-tuple-element.29), kind=kLoop, calls=%fused_computation.8 | loop fusion | flops 6291456 | bytes 12599296 | tf_op jit(solution)/shard_map/stack | solution.py:204
  7.4 2.1 %convert_bitcast_fusion = bf16[2,192,16,256]{3,1,0,2:T(8,128)(2,1)S(1)} fusion(bf16[1,16,512,256]{3,2,0,1:T(8,128)(2,1)S(1)} %get-tuple-element.18, bf16[1,16,512,256]{3,2,0,1:T(8,128)(2,1)S(1)} %get-tuple-element.17, bf16[16,512,192]{1,2,0:T(8,128)(2,1)S(1)} %copy-done.5), kind=kOutput, calls=%fused_computation.18 | convolution fusion | flops 1628962816 | bytes 14680064 | tf_op jit(solution)/shard_map/rnj,srnc->sjrc/dot_general | solution.py:205
  12.3 1.4 pad_maximum_fusion.1
  13.7 7.3 %all-to-all-start = ((bf16[32,7,16,256]{3,2,1,0:T(8,128)(2,1)}), bf16[32,7,16,256]{3,2,1,0:T(8,128)(2,1)S(1)}, u32[]{:S(2)}, u32[]{:S(2)}) async-start(bf16[32,7,16,256]{3,2,1,0:T(8,128)(2,1)} %pad_maximum_fusion.1), calls=%async_computation | async-start | bytes 3670016 | tf_op jit(solution)/shard_map/all_to_all | solution.py:225
  21.0 2.0 %copy.27 = bf16[1,192,16,256]{3,2,1,0:T(8,128)(2,1)} copy(bf16[1,192,16,256]{3,1,2,0:T(8,128)(2,1)S(1)} %get-tuple-element.22) | data formatting | bytes 3145728 | tf_op jit(solution)/shard_map/slice | solution.py:211
  24.3 13.5 %cosine_convert_fusion = (bf16[512,1536]{1,0:T(8,128)(2,1)S(1)}, bf16[512,1536]{1,0:T(8,128)(2,1)S(1)}) fusion(s32[512]{0:T(512)S(1)} %fusion.31), kind=kLoop, calls=%fused_computation.14 | loop fusion | flops 8650752 | bytes 3147776 | tf_op jit(solution)/shard_map/convert.3
  37.9 1.9 pad_maximum_fusion.table_ref
  39.8 24.5 %all-to-all-done.rows_ref = bf16[32,7,16,256]{3,2,1,0:T(8,128)(2,1)S(1)} async-done(((bf16[32,7,16,256]{3,2,1,0:T(8,128)(2,1)}), bf16[32,7,16,256]{3,2,1,0:T(8,128)(2,1)S(1)}, u32[]{:S(2)}, u32[]{:S(2)}) %all-to-all-start) | async-done | bytes 1835040 | tf_op jit(solution)/shard_map/all_to_all | solution.py:225
  64.3 4.2 %all-to-all-start.2 = ((bf16[32,6,16,256]{3,2,1,0:T(8,128)(2,1)}), bf16[32,6,16,256]{3,2,1,0:T(8,128)(2,1)S(1)}, u32[]{:S(2)}, u32[]{:S(2)}) async-start(bf16[32,6,16,256]{3,2,1,0:T(8,128)(2,1)} %bitcast.48), calls=%async_computation.2 | async-start | bytes 3145728 | tf_op jit(solution)/shard_map/all_to_all | solution.py:245
  68.6 0.9 copy-done
  69.6 0.9 copy-done.2
  70.5 31.3 %shard_map.82 = bf16[6,512,256]{2,1,0:T(8,128)(2,1)S(1)} custom-call(f32[6]{0:T(128)S(1)} %multiply_cosine_fusion.3.weight_ref, bf16[32,7,16,256]{3,2,1,0:T(8,128)(2,1)S(1)} %all-to-all-done.rows_ref, f32[1,128]{1,0:T(1,128)S(1)} %bitcast.44, bf16[128,1024]{1,0:T(8,128)(2,1)S(1)} %copy-done, f32[1,1024]{1,0:T(1,128)S(1)} %bitcast.46, ...), custom_call_target="tpu_custom_call" | custom-call | flops 9663676416 | bytes 6291456 | tf_op jit(solution)/shard_map/pallas_call | solution.py:93
  101.9 1.3 copy.29
  103.2 2.9 %all-to-all-done.2.rows_ref = bf16[32,6,16,256]{3,2,1,0:T(8,128)(2,1)S(1)} async-done(((bf16[32,6,16,256]{3,2,1,0:T(8,128)(2,1)}), bf16[32,6,16,256]{3,2,1,0:T(8,128)(2,1)S(1)}, u32[]{:S(2)}, u32[]{:S(2)}) %all-to-all-start.2) | async-done | bytes 1572896 | tf_op jit(solution)/shard_map/all_to_all | solution.py:245
  106.1 3.9 %all-to-all-start.1 = ((bf16[6,32,16,256]{3,2,0,1:T(8,128)(2,1)}), bf16[6,32,16,256]{3,2,0,1:T(8,128)(2,1)}, u32[]{:S(2)}, u32[]{:S(2)}) async-start(bf16[6,32,16,256]{3,2,0,1:T(8,128)(2,1)} %copy.29), calls=%async_computation.1 | async-start | bytes 3145728 | tf_op jit(solution)/shard_map/all_to_all | solution.py:238
  110.1 31.2 %shard_map.83 = bf16[6,512,256]{2,1,0:T(8,128)(2,1)S(1)} custom-call(f32[6]{0:T(128)S(1)} %multiply_cosine_fusion.2.weight_ref, bf16[32,6,16,256]{3,2,1,0:T(8,128)(2,1)S(1)} %all-to-all-done.2.rows_ref, f32[1,128]{1,0:T(1,128)S(1)} %bitcast.45, bf16[128,1024]{1,0:T(8,128)(2,1)S(1)} %copy-done.1, f32[1,1024]{1,0:T(1,128)S(1)} %bitcast.47, ...), custom_call_target="tpu_custom_call" | custom-call | flops 9663676416 | bytes 6291456 | tf_op jit(solution)/shard_map/pallas_call | solution.py:93
  141.3 1.4 copy.30
  142.7 5.1 %all-to-all-done.1 = bf16[6,32,16,256]{3,2,0,1:T(8,128)(2,1)} async-done(((bf16[6,32,16,256]{3,2,0,1:T(8,128)(2,1)}), bf16[6,32,16,256]{3,2,0,1:T(8,128)(2,1)}, u32[]{:S(2)}, u32[]{:S(2)}) %all-to-all-start.1) | async-done | bytes 1572896 | tf_op jit(solution)/shard_map/all_to_all | solution.py:238
  147.7 4.0 %all-to-all-start.3 = ((bf16[6,32,16,256]{3,2,0,1:T(8,128)(2,1)}), bf16[6,32,16,256]{3,2,0,1:T(8,128)(2,1)S(1)}, u32[]{:S(2)}, u32[]{:S(2)}) async-start(bf16[6,32,16,256]{3,2,0,1:T(8,128)(2,1)} %copy.30), calls=%async_computation.3 | async-start | bytes 3145728 | tf_op jit(solution)/shard_map/all_to_all | solution.py:238
  151.8 5.9 %copy.31.basis_ref = bf16[16,512,192]{2,1,0:T(8,128)(2,1)} copy(bf16[16,512,192]{1,2,0:T(8,128)(2,1)} %param.9) | data formatting | bytes 6291456 | tf_op args[1]
  158.3 3.1 %copy.32.north_ref = bf16[16,192,256]{2,1,0:T(8,128)(2,1)} copy(bf16[16,192,256]{2,0,1:T(8,128)(2,1)} %bitcast.18) | data formatting | bytes 3145728 | tf_op jit(solution)/shard_map/reshape | solution.py:239
  161.4 27.9 %all-to-all-done.3 = bf16[6,32,16,256]{3,2,0,1:T(8,128)(2,1)S(1)} async-done(((bf16[6,32,16,256]{3,2,0,1:T(8,128)(2,1)}), bf16[6,32,16,256]{3,2,0,1:T(8,128)(2,1)S(1)}, u32[]{:S(2)}, u32[]{:S(2)}) %all-to-all-start.3) | async-done | bytes 1572896 | tf_op jit(solution)/shard_map/all_to_all | solution.py:238
  189.3 1.7 copy.33.south_ref
  191.0 9.5 %shard_map.84 = f32[16,512,256]{2,1,0:T(8,128)} custom-call(s32[16]{0:T(128)} %copy-done.6, bf16[16,512,192]{2,1,0:T(8,128)(2,1)} %copy.31.basis_ref, bf16[16,192,256]{2,1,0:T(8,128)(2,1)} %copy.32.north_ref, bf16[16,192,256]{2,1,0:T(8,128)(2,1)} %copy.33.south_ref, bf16[16,512,256]{2,1,0:T(8,128)(2,1)} %spec_ref.1, f32[1,256]{1,0:T(1,128)} %bitcast.51), custom_call_target="tpu_custom_call" | custom-call | flops 1610612736 | bytes 18874368 | tf_op jit(solution)/shard_map/pallas_call | solution.py:145
  (45 shorter events, 5.3 us)
Async XLA Ops:
  0.9 6.5 %copy-start.6 = (s32[16]{0:T(128)}, s32[16]{0:T(128)S(1)}, u32[]{:S(2)}) copy-start(s32[16]{0:T(128)S(1)} %get-tuple-element.16.wave_ref) | copy-start | bytes 196
  1.2 6.3 %copy-start.5 = (bf16[16,512,192]{1,2,0:T(8,128)(2,1)S(1)}, bf16[16,512,192]{1,2,0:T(8,128)(2,1)}, u32[]{:S(2)}) copy-start(bf16[16,512,192]{1,2,0:T(8,128)(2,1)} %param.9) | copy-start | bytes 9437188
  13.7 50.5 %all-to-all-start = ((bf16[32,7,16,256]{3,2,1,0:T(8,128)(2,1)}), bf16[32,7,16,256]{3,2,1,0:T(8,128)(2,1)S(1)}, u32[]{:S(2)}, u32[]{:S(2)}) async-start(bf16[32,7,16,256]{3,2,1,0:T(8,128)(2,1)} %pad_maximum_fusion.1), calls=%async_computation | async-start | bytes 3670016 | tf_op jit(solution)/shard_map/all_to_all | solution.py:225
  37.9 26.5 %copy-start.7 = (f32[128]{0:T(128)S(1)}, f32[128]{0:T(128)}, u32[]{:S(2)}) copy-start(f32[128]{0:T(128)} %param.14) | copy-start | bytes 1540
  39.8 28.9 %copy-start.4 = (f32[1024]{0:T(1024)S(1)}, f32[1024]{0:T(1024)}, u32[]{:S(2)}) copy-start(f32[1024]{0:T(1024)} %param.12) | copy-start | bytes 12292
  64.3 41.8 %all-to-all-start.2 = ((bf16[32,6,16,256]{3,2,1,0:T(8,128)(2,1)}), bf16[32,6,16,256]{3,2,1,0:T(8,128)(2,1)S(1)}, u32[]{:S(2)}, u32[]{:S(2)}) async-start(bf16[32,6,16,256]{3,2,1,0:T(8,128)(2,1)} %bitcast.48), calls=%async_computation.2 | async-start | bytes 3145728 | tf_op jit(solution)/shard_map/all_to_all | solution.py:245
  68.6 1.0 copy-start
  69.6 0.9 copy-start.2
  101.9 8.2 %copy-start.1 = (bf16[128,1024]{1,0:T(8,128)(2,1)S(1)}, bf16[128,1024]{1,0:T(8,128)(2,1)}, u32[]{:S(2)}) copy-start(bf16[128,1024]{1,0:T(8,128)(2,1)} %in_w_ref.3) | copy-start | bytes 786436
  101.9 8.2 %copy-start.3 = (bf16[1024,128]{1,0:T(8,128)(2,1)S(1)}, bf16[1024,128]{1,0:T(8,128)(2,1)}, u32[]{:S(2)}) copy-start(bf16[1024,128]{1,0:T(8,128)(2,1)} %out_w_ref.3) | copy-start | bytes 786436
  106.1 41.6 %all-to-all-start.1 = ((bf16[6,32,16,256]{3,2,0,1:T(8,128)(2,1)}), bf16[6,32,16,256]{3,2,0,1:T(8,128)(2,1)}, u32[]{:S(2)}, u32[]{:S(2)}) async-start(bf16[6,32,16,256]{3,2,0,1:T(8,128)(2,1)} %copy.29), calls=%async_computation.1 | async-start | bytes 3145728 | tf_op jit(solution)/shard_map/all_to_all | solution.py:238
  147.7 41.6 %all-to-all-start.3 = ((bf16[6,32,16,256]{3,2,0,1:T(8,128)(2,1)}), bf16[6,32,16,256]{3,2,0,1:T(8,128)(2,1)S(1)}, u32[]{:S(2)}, u32[]{:S(2)}) async-start(bf16[6,32,16,256]{3,2,0,1:T(8,128)(2,1)} %copy.30), calls=%async_computation.3 | async-start | bytes 3145728 | tf_op jit(solution)/shard_map/all_to_all | solution.py:238
  151.7 5.9 %copy-start.8 = (f32[128]{0:T(128)S(1)}, f32[128]{0:T(128)}, u32[]{:S(2)}) copy-start(f32[128]{0:T(128)} %param.15) | copy-start | bytes 1540
